TPU v7x, 512 devices: a whole 4x4x16 slice. The times are simulated.
512 devices in a mesh: seq: 32 (over z, x_hi), fsdp: 16 (over y, x_lo, core).
Axes of the slice: x: 4 (x_hi: 2, x_lo: 2; x = x_hi * 2 + x_lo), y: 4, z: 16, core: 2. Of those that a mesh axis runs over, the one named last changes fastest.
Arguments:
- inputs: bfloat16 [5376, 65536], P('fsdp', 'seq'), may hold values from -6 to 6
- value_weight: bfloat16 [5376, 1024], P('fsdp'), may hold values from -0.078125 to 0.078125
- threshold: float32 [1024], replicated, may hold values from 0.004 to 0.03
- queries: bfloat16 [65536, 2048], P(('seq', 'fsdp')), may hold values from -180 to 180
- keys: bfloat16 [65536, 1024], P(('seq', 'fsdp')), may hold values from -6 to 6
- out_grad: bfloat16 [65536, 2048], P(('seq', 'fsdp')), may hold values from -0.59765625 to 0.59765625
Outputs:
- grad_weight: bfloat16 [5376, 1024], P('fsdp')
- grad_logit: float32 [1024], replicated
All inputs are finite; a program needn't handle non-finite values.
Results may differ from a plain program's by a relative error of at most 0.0058.
Values may be sent and summed in bfloat16 or wider, within the bound.
No kernel may reach another device: no remote copies, remote signals or barrier semaphores. Data moves between devices by JAX's collectives and lax.ppermute only.
A program may use at most 64 MiB of HBM per device.

v0:
```python
import jax
import jax.numpy as jnp
from jax import lax
from jax.sharding import PartitionSpec as P

HEAD = 128
Q_HEADS = 16
KV_HEADS = 8
WINDOW = 1024
TOK_DEV = 128


pre_scale = 168.0 ** (-0.5)
masked_score = -1e30


def passed_along(value, axis, steps):
    count = lax.axis_size(axis)
    first, last = (max(0, -steps), min(count, count - steps))
    return lax.ppermute(value, axis, [(source, source + steps) for source in range(first, last)])


def local(inputs, value_weight, threshold, queries, keys, out_grad):
    tok_rows = queries.shape[0]
    hop_count = WINDOW // TOK_DEV
    span_keys = (hop_count + 1) * tok_rows
    head_ratio = Q_HEADS // KV_HEADS
    kv_pair = 2
    group_count = KV_HEADS // kv_pair
    position = lax.axis_index(("seq", "fsdp"))
    earlier = [
        passed_along(keys, ("seq", "fsdp"), distance) for distance in range(hop_count, 0, -1)
    ]
    key_rows = jnp.concatenate(earlier + [keys], axis=0)
    query_pos = position * tok_rows + jnp.arange(tok_rows, dtype=jnp.int32)
    key_pos = (position - hop_count) * tok_rows + jnp.arange(span_keys, dtype=jnp.int32)
    offset = query_pos[:, None] - key_pos[None, :]
    visible = (offset >= 0) & (offset < WINDOW) & (key_pos >= 0)[None, :]
    q_span = kv_pair * head_ratio * HEAD
    k_span = kv_pair * HEAD

    def group_step(group_index, running):
        q_cols = lax.dynamic_slice_in_dim(queries, group_index * q_span, q_span, 1).reshape(
            tok_rows, kv_pair, head_ratio, HEAD
        )
        d_cols = lax.dynamic_slice_in_dim(out_grad, group_index * q_span, q_span, 1).reshape(
            tok_rows, kv_pair, head_ratio, HEAD
        )
        k_cols = lax.dynamic_slice_in_dim(key_rows, group_index * k_span, k_span, 1).reshape(
            span_keys, kv_pair, HEAD
        )
        scores = (
            jnp.einsum("qgrd,kgd->grqk", q_cols, k_cols, preferred_element_type=jnp.float32)
            * pre_scale
        )
        scores = jnp.where(visible, scores, masked_score)
        row_max = jnp.max(scores, axis=-1, keepdims=True)
        weights = jnp.exp(scores - row_max)
        probabilities = (weights / jnp.sum(weights, axis=-1, keepdims=True)).astype(jnp.bfloat16)
        value_part = jnp.einsum(
            "grqk,qgrd->kgd", probabilities, d_cols, preferred_element_type=jnp.float32
        )
        return lax.dynamic_update_slice_in_dim(
            running, value_part.reshape(span_keys, k_span), group_index * k_span, 1
        )

    partial_grad = lax.fori_loop(
        0, group_count, group_step, jnp.zeros((span_keys, value_weight.shape[1]), jnp.float32)
    )

    def block_at(distance):
        return partial_grad[
            (hop_count - distance) * tok_rows : (hop_count - distance + 1) * tok_rows
        ]

    own_grad = block_at(0)
    for distance in range(1, hop_count + 1):
        own_grad = own_grad + passed_along(block_at(distance), ("seq", "fsdp"), -distance)
    value_grad = own_grad.astype(jnp.bfloat16)
    local_grad = jnp.dot(
        inputs,
        lax.all_gather(value_grad, "fsdp", axis=0, tiled=True),
        preferred_element_type=jnp.float32,
    )
    weight_full = value_weight.astype(jnp.float32)
    kept_mask = jnp.abs(weight_full) > threshold[None, :]
    signed = jnp.where(kept_mask, jnp.sign(weight_full), 0.0)
    dense_grad = lax.psum(local_grad, "seq")
    logit_sum = lax.psum(jnp.sum(dense_grad * signed, axis=0), "fsdp")
    grad_logit = -logit_sum * threshold * (1.0 - threshold)
    grad_weight = jnp.where(kept_mask, dense_grad, 0.0).astype(jnp.bfloat16)
    return (grad_weight, grad_logit)


def solution(mesh):
    return jax.shard_map(
        local,
        mesh=mesh,
        in_specs=(
            P("fsdp", "seq"),
            P("fsdp", None),
            P(),
            P(("seq", "fsdp"), None),
            P(("seq", "fsdp"), None),
            P(("seq", "fsdp"), None),
        ),
        out_specs=(P("fsdp", None), P()),
        check_vma=False,
    )
```

profile of v0, /device:TPU:6, one launch (start us, length us, event | category | flops | bytes accessed | tf_op | source)
XLA Modules:
  0.0 632.6 jit_solution(2895090624501307343)
XLA Ops:
  7.2 1.2 copy.13
  8.4 1.9 collective-permute-start.7
  10.4 3.8 collective-permute-start.6
  14.1 4.7 collective-permute-start.2
  18.9 4.8 collective-permute-start.1
  23.6 3.9 collective-permute-start
  28.6 13.7 %collective-permute-done = bf16[128,1024]{0,1:T(8,128)(2,1)S(1)} collective-permute-done((bf16[128,1024]{0,1:T(8,128)(2,1)S(1)}, bf16[128,1024]{0,1:T(8,128)(2,1)S(1)}, u32[]{:S(2)}, u32[]{:S(2)}) %collective-permute-start) | collective-permute-done | bytes 262176 | tf_op jit(solution)/shard_map/ppermute | solution.py:20
  42.3 1.9 collective-permute-start.3
  45.0 2.2 collective-permute-start.4
  48.0 2.4 collective-permute-start.5
  51.1 10.6 %collective-permute-done.3 = bf16[128,1024]{0,1:T(8,128)(2,1)S(1)} collective-permute-done((bf16[128,1024]{0,1:T(8,128)(2,1)S(1)}, bf16[128,1024]{0,1:T(8,128)(2,1)S(1)}, u32[]{:S(2)}, u32[]{:S(2)}) %collective-permute-start.3) | collective-permute-done | bytes 262176 | tf_op jit(solution)/shard_map/ppermute | solution.py:20
  66.3 2.4 broadcast_in_dim.34
  68.7 35.4 %while.14 = (s32[]{:T(128)}, f32[1152,1024]{0,1:T(8,128)}, bf16[128,2048]{1,0:T(8,128)(2,1)}, bf16[1152,1024]{0,1:T(8,128)(2,1)}, bf16[128,2048]{1,0:T(8,128)(2,...) while((s32[]{:T(128)}, f32[1152,1024]{0,1:T(8,128)}, ...), condition=%wide.region_3.4_spmd.clone, body=%wide.region_0.3_spmd.clone.sunk | while | flops 459033344 | bytes 7829933 | solution.py:67
  68.7 1.8 fusion.44
  71.7 1.1 constant_dynamic-slice_fusion.6
  72.9 1.6 fusion.45
  74.5 2.0 fusion.46
  77.6 1.8 fusion.44
  80.6 1.1 constant_dynamic-slice_fusion.6
  81.7 1.6 fusion.45
  83.3 2.0 fusion.46
  86.4 1.8 fusion.44
  89.4 1.1 constant_dynamic-slice_fusion.6
  90.5 1.6 fusion.45
  92.1 2.0 fusion.46
  94.1 1.1 constant_dynamic-update-slice_fusion.11
  95.3 1.8 fusion.44
  99.4 1.6 fusion.45
  101.0 2.0 fusion.46
  104.1 2.5 fusion.23
  106.6 4.3 collective-permute-start.8
  111.0 1.9 collective-permute-start.14
  112.9 2.0 collective-permute-start.13
  114.9 2.0 collective-permute-start.12
  116.9 2.0 collective-permute-start.11
  118.9 17.9 %collective-permute-start.10 = (f32[128,1024]{0,1:T(8,128)S(1)}, f32[128,1024]{0,1:T(8,128)S(1)}, u32[]{:S(2)}, u32[]{:S(2)}) collective-permute-start(f32[128,1024]{0,1:T(8,128)S(1)} %get-tuple-element.172), channel_id=1, source_target_pairs={{3,0},{4,1},{5,2},{6,3},{7,4},{8,5},{9,6},{10,7},{11,8},{12,9},{13... | collective-permute-start | bytes 1572872 | tf_op jit(solution)/shard_map/ppermute | solution.py:20
  136.8 1.9 collective-permute-start.9
  138.8 16.2 %collective-permute-done.13 = f32[128,1024]{0,1:T(8,128)S(1)} collective-permute-done((f32[128,1024]{0,1:T(8,128)S(1)}, f32[128,1024]{0,1:T(8,128)S(1)}, u32[]{:S(2)}, u32[]{:S(2)}) %collective-permute-start.13) | collective-permute-done | bytes 524320 | tf_op jit(solution)/shard_map/ppermute | solution.py:20
  155.0 5.5 collective-permute-start.15
  160.5 17.8 %collective-permute-done.12 = f32[128,1024]{0,1:T(8,128)S(1)} collective-permute-done((f32[128,1024]{0,1:T(8,128)S(1)}, f32[128,1024]{0,1:T(8,128)S(1)}, u32[]{:S(2)}, u32[]{:S(2)}) %collective-permute-start.12) | collective-permute-done | bytes 524320 | tf_op jit(solution)/shard_map/ppermute | solution.py:20
  178.3 4.4 collective-permute-done.11
  182.7 7.5 %collective-permute-done.15 = f32[128,1024]{0,1:T(8,128)S(1)} collective-permute-done((f32[128,1024]{0,1:T(8,128)S(1)}, f32[128,1024]{0,1:T(8,128)S(1)}, u32[]{:S(2)}, u32[]{:S(2)}) %collective-permute-start.15) | collective-permute-done | bytes 524320 | tf_op jit(solution)/shard_map/ppermute | solution.py:20
  190.2 2.0 add_convert_fusion
  192.3 89.2 %all-gather.2.cloned.1.call-done = bf16[2048,1024]{0,1:T(8,128)(2,1)} async-done(((bf16[128,1024]{0,1:T(8,128)(2,1)}), bf16[2048,1024]{0,1:T(8,128)(2,1)}) %all-gather.2.cloned.1.call-update) | async-done | bytes 4194320 | tf_op jit(solution)/shard_map/all_gather | solution.py:82
  281.5 4.9 convolution_bitcast_fusion
  286.4 312.0 %all-reduce.2.cloned.1.call-done = f32[336,1024]{1,0:T(8,128)} async-done(((f32[336,1024]{1,0:T(8,128)}), f32[336,1024]{1,0:T(8,128)}) %all-reduce.2.cloned.1.call-update) | async-done | bytes 1376272 | tf_op jit(solution)/shard_map/psum | solution.py:88
  598.4 2.0 fusion.21
  600.5 23.6 %psum.15 = f32[1024]{0:T(1024)S(1)} all-reduce(f32[1024]{0:T(1024)S(1)} %fusion.21), channel_id=1, replica_groups=mesh['seq'=32,'fsdp'=16] {'fsdp'}, use_global_device_ids=true, to_apply=%region_6.7 | all-reduce | flops 1024 | bytes 8192 | tf_op jit(solution)/shard_map/psum | solution.py:89
  (68 shorter events, 19.1 us)
Async XLA Ops:
  7.2 274.3 %copy-start = (bf16[336,2048]{1,0:T(8,128)(2,1)S(1)}, bf16[336,2048]{1,0:T(8,128)(2,1)}, u32[]{:S(2)}) copy-start(bf16[336,2048]{1,0:T(8,128)(2,1)} %param.8) | copy-start | bytes 4128772
  7.2 274.3 %all-gather.2.cloned.1.call-start = ((), (), s32[]{:S(2)}) async-start(), calls=%async_computation | async-start | bytes 4456448 | tf_op jit(solution)/shard_map/all_gather | solution.py:82
  8.4 56.3 %collective-permute-start.7 = (bf16[128,1024]{0,1:T(8,128)(2,1)S(1)}, bf16[128,1024]{0,1:T(8,128)(2,1)S(1)}, u32[]{:S(2)}, u32[]{:S(2)}) collective-permute-start(bf16[128,1024]{0,1:T(8,128)(2,1)S(1)} %copy.13), channel_id=1, source_target_pairs={{0,1},{1,2},{2,3},{3,4},{4,5},{5,6},{6,7},{7,8},{8,9},{9,10},{10,1... | collective-permute-start | bytes 786440 | tf_op jit(solution)/shard_map/ppermute | solution.py:20
  10.4 53.6 %collective-permute-start.6 = (bf16[128,1024]{0,1:T(8,128)(2,1)S(1)}, bf16[128,1024]{0,1:T(8,128)(2,1)S(1)}, u32[]{:S(2)}, u32[]{:S(2)}) collective-permute-start(bf16[128,1024]{0,1:T(8,128)(2,1)S(1)} %copy.13), channel_id=1, source_target_pairs={{0,2},{1,3},{2,4},{3,5},{4,6},{5,7},{6,8},{7,9},{8,10},{9,11},{10,... | collective-permute-start | bytes 786440 | tf_op jit(solution)/shard_map/ppermute | solution.py:20
  14.1 33.9 %collective-permute-start.2 = (bf16[128,1024]{0,1:T(8,128)(2,1)S(1)}, bf16[128,1024]{0,1:T(8,128)(2,1)S(1)}, u32[]{:S(2)}, u32[]{:S(2)}) collective-permute-start(bf16[128,1024]{0,1:T(8,128)(2,1)S(1)} %copy.13), channel_id=1, source_target_pairs={{0,6},{1,7},{2,8},{3,9},{4,10},{5,11},{6,12},{7,13},{8,14},{9,15},... | collective-permute-start | bytes 786440 | tf_op jit(solution)/shard_map/ppermute | solution.py:20
  18.9 26.1 %collective-permute-start.1 = (bf16[128,1024]{0,1:T(8,128)(2,1)S(1)}, bf16[128,1024]{0,1:T(8,128)(2,1)S(1)}, u32[]{:S(2)}, u32[]{:S(2)}) collective-permute-start(bf16[128,1024]{0,1:T(8,128)(2,1)S(1)} %copy.13), channel_id=1, source_target_pairs={{0,7},{1,8},{2,9},{3,10},{4,11},{5,12},{6,13},{7,14},{8,15},{9,16}... | collective-permute-start | bytes 786440 | tf_op jit(solution)/shard_map/ppermute | solution.py:20
  23.6 18.7 %collective-permute-start = (bf16[128,1024]{0,1:T(8,128)(2,1)S(1)}, bf16[128,1024]{0,1:T(8,128)(2,1)S(1)}, u32[]{:S(2)}, u32[]{:S(2)}) collective-permute-start(bf16[128,1024]{0,1:T(8,128)(2,1)S(1)} %copy.13), channel_id=1, source_target_pairs={{0,8},{1,9},{2,10},{3,11},{4,12},{5,13},{6,14},{7,15},{8,16},{9,17... | collective-permute-start | bytes 786440 | tf_op jit(solution)/shard_map/ppermute | solution.py:20
  42.3 19.4 %collective-permute-start.3 = (bf16[128,1024]{0,1:T(8,128)(2,1)S(1)}, bf16[128,1024]{0,1:T(8,128)(2,1)S(1)}, u32[]{:S(2)}, u32[]{:S(2)}) collective-permute-start(bf16[128,1024]{0,1:T(8,128)(2,1)S(1)} %copy.13), channel_id=1, source_target_pairs={{0,5},{1,6},{2,7},{3,8},{4,9},{5,10},{6,11},{7,12},{8,13},{9,14},{... | collective-permute-start | bytes 786440 | tf_op jit(solution)/shard_map/ppermute | solution.py:20
  45.0 17.5 %collective-permute-start.4 = (bf16[128,1024]{0,1:T(8,128)(2,1)S(1)}, bf16[128,1024]{0,1:T(8,128)(2,1)S(1)}, u32[]{:S(2)}, u32[]{:S(2)}) collective-permute-start(bf16[128,1024]{0,1:T(8,128)(2,1)S(1)} %copy.13), channel_id=1, source_target_pairs={{0,4},{1,5},{2,6},{3,7},{4,8},{5,9},{6,10},{7,11},{8,12},{9,13},{1... | collective-permute-start | bytes 786440 | tf_op jit(solution)/shard_map/ppermute | solution.py:20
  48.0 15.3 %collective-permute-start.5 = (bf16[128,1024]{0,1:T(8,128)(2,1)S(1)}, bf16[128,1024]{0,1:T(8,128)(2,1)S(1)}, u32[]{:S(2)}, u32[]{:S(2)}) collective-permute-start(bf16[128,1024]{0,1:T(8,128)(2,1)S(1)} %copy.13), channel_id=1, source_target_pairs={{0,3},{1,4},{2,5},{3,6},{4,7},{5,8},{6,9},{7,10},{8,11},{9,12},{10... | collective-permute-start | bytes 786440 | tf_op jit(solution)/shard_map/ppermute | solution.py:20
  68.7 3.0 copy-start.3
  76.4 1.1 copy-start.4
  77.6 3.0 copy-start.3
  85.3 1.1 copy-start.4
  86.4 3.0 copy-start.3
  94.1 1.1 copy-start.4
  95.3 3.0 copy-start.3
  103.0 1.1 copy-start.4
  106.6 12.3 %collective-permute-start.8 = (f32[128,1024]{0,1:T(8,128)S(1)}, f32[128,1024]{0,1:T(8,128)S(1)}, u32[]{:S(2)}, u32[]{:S(2)}) collective-permute-start(f32[128,1024]{0,1:T(8,128)S(1)} %get-tuple-element.167), channel_id=1, source_target_pairs={{1,0},{2,1},{3,2},{4,3},{5,4},{6,5},{7,6},{8,7},{9,8},{10,9},{11,1... | collective-permute-start | bytes 1572872 | tf_op jit(solution)/shard_map/ppermute | solution.py:20
  111.0 25.9 %collective-permute-start.14 = (f32[128,1024]{0,1:T(8,128)S(1)}, f32[128,1024]{0,1:T(8,128)S(1)}, u32[]{:S(2)}, u32[]{:S(2)}) collective-permute-start(f32[128,1024]{0,1:T(8,128)S(1)} %get-tuple-element.168), channel_id=1, source_target_pairs={{7,0},{8,1},{9,2},{10,3},{11,4},{12,5},{13,6},{14,7},{15,8},{16,9}... | collective-permute-start | bytes 1572872 | tf_op jit(solution)/shard_map/ppermute | solution.py:20
  112.9 42.1 %collective-permute-start.13 = (f32[128,1024]{0,1:T(8,128)S(1)}, f32[128,1024]{0,1:T(8,128)S(1)}, u32[]{:S(2)}, u32[]{:S(2)}) collective-permute-start(f32[128,1024]{0,1:T(8,128)S(1)} %get-tuple-element.169), channel_id=1, source_target_pairs={{6,0},{7,1},{8,2},{9,3},{10,4},{11,5},{12,6},{13,7},{14,8},{15,9},... | collective-permute-start | bytes 1572872 | tf_op jit(solution)/shard_map/ppermute | solution.py:20
  114.9 63.4 %collective-permute-start.12 = (f32[128,1024]{0,1:T(8,128)S(1)}, f32[128,1024]{0,1:T(8,128)S(1)}, u32[]{:S(2)}, u32[]{:S(2)}) collective-permute-start(f32[128,1024]{0,1:T(8,128)S(1)} %get-tuple-element.170), channel_id=1, source_target_pairs={{5,0},{6,1},{7,2},{8,3},{9,4},{10,5},{11,6},{12,7},{13,8},{14,9},{... | collective-permute-start | bytes 1572872 | tf_op jit(solution)/shard_map/ppermute | solution.py:20
  116.9 65.8 %collective-permute-start.11 = (f32[128,1024]{0,1:T(8,128)S(1)}, f32[128,1024]{0,1:T(8,128)S(1)}, u32[]{:S(2)}, u32[]{:S(2)}) collective-permute-start(f32[128,1024]{0,1:T(8,128)S(1)} %get-tuple-element.171), channel_id=1, source_target_pairs={{4,0},{5,1},{6,2},{7,3},{8,4},{9,5},{10,6},{11,7},{12,8},{13,9},{1... | collective-permute-start | bytes 1572872 | tf_op jit(solution)/shard_map/ppermute | solution.py:20
  118.9 63.8 %collective-permute-start.10 = (f32[128,1024]{0,1:T(8,128)S(1)}, f32[128,1024]{0,1:T(8,128)S(1)}, u32[]{:S(2)}, u32[]{:S(2)}) collective-permute-start(f32[128,1024]{0,1:T(8,128)S(1)} %get-tuple-element.172), channel_id=1, source_target_pairs={{3,0},{4,1},{5,2},{6,3},{7,4},{8,5},{9,6},{10,7},{11,8},{12,9},{13... | collective-permute-start | bytes 1572872 | tf_op jit(solution)/shard_map/ppermute | solution.py:20
  136.8 45.9 %collective-permute-start.9 = (f32[128,1024]{0,1:T(8,128)S(1)}, f32[128,1024]{0,1:T(8,128)S(1)}, u32[]{:S(2)}, u32[]{:S(2)}) collective-permute-start(f32[128,1024]{0,1:T(8,128)S(1)} %get-tuple-element.173), channel_id=1, source_target_pairs={{2,0},{3,1},{4,2},{5,3},{6,4},{7,5},{8,6},{9,7},{10,8},{11,9},{12,... | collective-permute-start | bytes 1572872 | tf_op jit(solution)/shard_map/ppermute | solution.py:20
  155.0 35.2 %collective-permute-start.15 = (f32[128,1024]{0,1:T(8,128)S(1)}, f32[128,1024]{0,1:T(8,128)S(1)}, u32[]{:S(2)}, u32[]{:S(2)}) collective-permute-start(f32[128,1024]{0,1:T(8,128)S(1)} %get-tuple-element.174), channel_id=1, source_target_pairs={{8,0},{9,1},{10,2},{11,3},{12,4},{13,5},{14,6},{15,7},{16,8},{17,9... | collective-permute-start | bytes 1572872 | tf_op jit(solution)/shard_map/ppermute | solution.py:20
  192.2 406.2 %copy-start.2 = (bf16[336,1024]{1,0:T(8,128)(2,1)S(1)}, bf16[336,1024]{1,0:T(8,128)(2,1)}, u32[]{:S(2)}) copy-start(bf16[336,1024]{1,0:T(8,128)(2,1)} %param.9) | copy-start | bytes 2064388
  192.2 406.2 %copy-start.5 = (f32[1024]{0:T(1024)S(1)}, f32[1024]{0:T(1024)}, u32[]{:S(2)}) copy-start(f32[1024]{0:T(1024)} %param.10) | copy-start | bytes 12292
  192.2 406.2 %all-reduce.2.cloned.1.call-start = ((), (), s32[]{:S(2)}) async-start(), calls=%async_computation.1 | async-start | bytes 2752512 | tf_op jit(solution)/shard_map/psum | solution.py:88
  598.4 26.2 %copy-start.1 = (f32[336,1024]{1,0:T(8,128)S(1)}, f32[336,1024]{1,0:T(8,128)}, u32[]{:S(2)}) copy-start(f32[336,1024]{1,0:T(8,128)} %all-reduce.2.cloned.1.call-done) | copy-start | bytes 4128772
Sparse Core Ops, SparseCore 0:
  192.3 89.0 all-gather.1
  286.5 311.8 all-reduce.1
where the time goes:
time: 639 us; the launch traced here: 633 us
  waiting for transfers between devices  472 us (74%)
  starting transfers between devices  63.2 us (10%)
  local copies, waits for them, and re-layouts  26.8 us (4%)
  blocking collectives  23.6 us (4%)
  matrix products  19.2 us (3%)
  between operations  14.3 us (2%)
  other arithmetic  13.8 us (2%)
    psum x1, waiting for transfers between devices, local(): dense_grad = lax.psum(local_grad, 'seq')  312 us
    all_gather x1, waiting for transfers between devices, local(): lax.all_gather(value_grad, 'fsdp', axis=0, tiled=True)  89.2 us
    ppermute x16, waiting for transfers between devices, passed_along(): lax.ppermute(value, axis, [(source, source + steps) for source in range(f...  70.3 us
    ppermute x16, starting transfers between devices, passed_along(): lax.ppermute(value, axis, [(source, source + steps) for source in range(f...  63.1 us
    psum x1, blocking collectives, local(): logit_sum = lax.psum(jnp.sum(dense_grad * signed, axis=0), 'fsdp')  23.6 us
  transfers between devices with their start and end apart: 18, of which 8 were waited for; matrix products, arithmetic and copies ran while one was open for 1% of the time, Pallas kernels for 0%

commit v1 on v0

v1 whole, which is shorter than its diff:
```python
import math

import jax
import jax.numpy as jnp
from jax import lax
from jax.sharding import Mesh
from jax.sharding import PartitionSpec as P

HEAD = 128
Q_HEADS = 16
KV_HEADS = 8
WINDOW = 1024
TOK_DEV = 128


pre_scale = 168.0 ** (-0.5)
masked_score = -1e30

SEQ = ("z", "xh")
FSDP = ("y", "xl", "c")
ALL = SEQ + FSDP


def passed_along(value, axis, count, steps):
    first, last = (max(0, -steps), min(count, count - steps))
    return lax.ppermute(value, axis, [(source, source + steps) for source in range(first, last)])


def make_local(sizes):
    n_all = math.prod(sizes[a] for a in ALL)
    n_seq = math.prod(sizes[a] for a in SEQ)
    n_fsdp = math.prod(sizes[a] for a in FSDP)

    def local(inputs, value_weight, threshold, queries, keys, out_grad):
        tok_rows = queries.shape[0]
        hop_count = WINDOW // TOK_DEV
        span_keys = (hop_count + 1) * tok_rows
        head_ratio = Q_HEADS // KV_HEADS
        kv_pair = 2
        group_count = KV_HEADS // kv_pair
        position = lax.axis_index(ALL)
        earlier = [passed_along(keys, ALL, n_all, distance) for distance in range(hop_count, 0, -1)]
        key_rows = jnp.concatenate(earlier + [keys], axis=0)
        query_pos = position * tok_rows + jnp.arange(tok_rows, dtype=jnp.int32)
        key_pos = (position - hop_count) * tok_rows + jnp.arange(span_keys, dtype=jnp.int32)
        offset = query_pos[:, None] - key_pos[None, :]
        visible = (offset >= 0) & (offset < WINDOW) & (key_pos >= 0)[None, :]
        q_span = kv_pair * head_ratio * HEAD
        k_span = kv_pair * HEAD

        def group_step(group_index, running):
            q_cols = lax.dynamic_slice_in_dim(queries, group_index * q_span, q_span, 1).reshape(
                tok_rows, kv_pair, head_ratio, HEAD
            )
            d_cols = lax.dynamic_slice_in_dim(out_grad, group_index * q_span, q_span, 1).reshape(
                tok_rows, kv_pair, head_ratio, HEAD
            )
            k_cols = lax.dynamic_slice_in_dim(key_rows, group_index * k_span, k_span, 1).reshape(
                span_keys, kv_pair, HEAD
            )
            scores = (
                jnp.einsum("qgrd,kgd->grqk", q_cols, k_cols, preferred_element_type=jnp.float32)
                * pre_scale
            )
            scores = jnp.where(visible, scores, masked_score)
            row_max = jnp.max(scores, axis=-1, keepdims=True)
            weights = jnp.exp(scores - row_max)
            probabilities = (weights / jnp.sum(weights, axis=-1, keepdims=True)).astype(jnp.bfloat16)
            value_part = jnp.einsum(
                "grqk,qgrd->kgd", probabilities, d_cols, preferred_element_type=jnp.float32
            )
            return lax.dynamic_update_slice_in_dim(
                running, value_part.reshape(span_keys, k_span), group_index * k_span, 1
            )

        partial_grad = lax.fori_loop(
            0, group_count, group_step, jnp.zeros((span_keys, value_weight.shape[1]), jnp.float32)
        )

        def block_at(distance):
            return partial_grad[
                (hop_count - distance) * tok_rows : (hop_count - distance + 1) * tok_rows
            ]

        own_grad = block_at(0)
        for distance in range(1, hop_count + 1):
            sent = passed_along(block_at(distance), ALL, n_all, -distance)
            own_grad = own_grad + sent
        value_grad = own_grad.astype(jnp.bfloat16)

        spread = jnp.broadcast_to(value_grad[None], (n_fsdp,) + value_grad.shape)
        gathered = lax.all_to_all(spread, FSDP, 0, 0, tiled=True).reshape(
            n_fsdp * tok_rows, value_grad.shape[1]
        )
        local_grad = jnp.dot(inputs, gathered, preferred_element_type=jnp.float32)

        weight_full = value_weight.astype(jnp.float32)
        kept_mask = jnp.abs(weight_full) > threshold[None, :]
        signed = jnp.where(kept_mask, jnp.sign(weight_full), 0.0)

        logit_part = jnp.sum(local_grad * signed, axis=0)
        logit_sum = lax.psum(logit_part, ALL)
        grad_logit = -logit_sum * threshold * (1.0 - threshold)

        rows, cols = local_grad.shape
        piece = cols // n_seq
        pieces = local_grad.reshape(rows, n_seq, piece)
        received = lax.all_to_all(pieces, SEQ, 1, 1, tiled=True)
        dense_piece = jnp.sum(received, axis=1)
        seq_index = lax.axis_index(SEQ)
        kept_piece = lax.dynamic_slice_in_dim(kept_mask, seq_index * piece, piece, 1)
        weight_piece = jnp.where(kept_piece, dense_piece, 0.0).astype(jnp.bfloat16)
        weight_piece = lax.all_gather(weight_piece, "xh", axis=1, tiled=True)
        grad_weight = lax.all_gather(weight_piece, "z", axis=1, tiled=True)
        return (grad_weight, grad_logit)

    return local


def solution(mesh):
    names = mesh.axis_names
    assert tuple(names) == ("seq", "fsdp")
    n_seq, n_fsdp = mesh.devices.shape
    sizes = {"z": n_seq // 2, "xh": 2, "y": n_fsdp // 4, "xl": 2, "c": 2}
    phys = Mesh(
        mesh.devices.reshape([sizes[a] for a in ALL]), ALL
    )
    return jax.shard_map(
        make_local(sizes),
        mesh=phys,
        in_specs=(
            P(FSDP, SEQ),
            P(FSDP, None),
            P(),
            P(ALL, None),
            P(ALL, None),
            P(ALL, None),
        ),
        out_specs=(P(FSDP, None), P()),
        check_vma=False,
    )
```

time: 639 us -> 467 us (0.73)
  waiting for transfers between devices: 472 us -> 131 us
  blocking collectives: 23.6 us -> 177 us
  starting transfers between devices: 63.2 us -> 92.4 us
  between operations: 14.3 us -> 0.88 us
    psum x1 -> x0, waiting for transfers between devices: 312 us -> none  [local(): dense_grad = lax.psum(local_grad, 'seq')]
    psum x1, blocking collectives: 23.6 us -> 138 us  [local(): logit_sum = lax.psum(logit_part, ALL)]
    all_gather x1 -> x0, waiting for transfers between devices: 89.2 us -> none  [local(): lax.all_gather(value_grad, 'fsdp', axis=0, tiled=True)]
    all_to_all x0 -> x2, waiting for transfers between devices: none -> 48.8 us  [the longest x1 48.8 us: local(): lax.all_to_all(spread, FSDP, 0, 0, tiled=True)]
    all_to_all x0 -> x2, starting transfers between devices: none -> 40.5 us  [the longest x1 21.6 us: local(): lax.all_to_all(spread, FSDP, 0, 0, tiled=True)]
    all_gather x0 -> x2, blocking collectives: none -> 39.3 us  [the longest x1 33.3 us: local(): grad_weight = lax.all_gather(weight_piece, 'z', axis=1, tiled=True)]
    ppermute x16, waiting for transfers between devices: 70.3 us -> 82.4 us  [passed_along(): lax.ppermute(value, axis, [(source, source + steps) for source in range(f...]
    ppermute x16, starting transfers between devices: 63.1 us -> 51.9 us  [passed_along(): lax.ppermute(value, axis, [(source, source + steps) for source in range(f...]
  transfers between devices with their start and end apart: 18 -> 18, of which waited for: 8 -> 10; matrix products, arithmetic and copies ran while one was open for 1% -> 2% of each run, Pallas kernels for 0% -> 0%
where the time goes in v1:
time: 467 us; the launch traced here: 465 us
  blocking collectives  177 us (38%)
  waiting for transfers between devices  131 us (28%)
  starting transfers between devices  92.4 us (20%)
  local copies, waits for them, and re-layouts  30.9 us (7%)
  matrix products  20.6 us (4%)
  other arithmetic  11.2 us (2%)
    psum x1, blocking collectives, local(): logit_sum = lax.psum(logit_part, ALL)  138 us
    ppermute x16, waiting for transfers between devices, passed_along(): lax.ppermute(value, axis, [(source, source + steps) for source in range(f...  82.4 us
    ppermute x16, starting transfers between devices, passed_along(): lax.ppermute(value, axis, [(source, source + steps) for source in range(f...  51.9 us
    all_to_all x1, waiting for transfers between devices, local(): lax.all_to_all(spread, FSDP, 0, 0, tiled=True)  48.8 us
    all_gather x1, blocking collectives, local(): grad_weight = lax.all_gather(weight_piece, 'z', axis=1, tiled=True)  33.3 us
    all_to_all x1, starting transfers between devices, local(): lax.all_to_all(spread, FSDP, 0, 0, tiled=True)  21.6 us
    all_to_all x1, starting transfers between devices, local(): received = lax.all_to_all(pieces, SEQ, 1, 1, tiled=True)  18.9 us
  transfers between devices with their start and end apart: 18, of which 10 were waited for; matrix products, arithmetic and copies ran while one was open for 2% of the time, Pallas kernels for 0%

profile of v1, /device:TPU:6, one launch (start us, length us, event | category | flops | bytes accessed | tf_op | source)
XLA Modules:
  0.0 464.7 jit_solution(15453910034897072233)
XLA Ops:
  1.9 5.1 %collective-permute-start = (bf16[128,1024]{0,1:T(8,128)(2,1)S(1)}, bf16[128,1024]{0,1:T(8,128)(2,1)S(1)}, u32[]{:S(2)}, u32[]{:S(2)}) collective-permute-start(bf16[128,1024]{0,1:T(8,128)(2,1)S(1)} %copy.50), channel_id=1, source_target_pairs={{0,8},{1,9},{2,10},{3,11},{4,12},{5,13},{6,14},{7,15},{8,16},{9,17... | collective-permute-start | bytes 786440 | tf_op jit(solution)/shard_map/ppermute | solution.py:26
  7.0 3.0 collective-permute-start.1
  10.0 5.6 %collective-permute-start.2 = (bf16[128,1024]{0,1:T(8,128)(2,1)S(1)}, bf16[128,1024]{0,1:T(8,128)(2,1)S(1)}, u32[]{:S(2)}, u32[]{:S(2)}) collective-permute-start(bf16[128,1024]{0,1:T(8,128)(2,1)S(1)} %copy.50), channel_id=1, source_target_pairs={{0,6},{1,7},{2,8},{3,9},{4,10},{5,11},{6,12},{7,13},{8,14},{9,15},... | collective-permute-start | bytes 786440 | tf_op jit(solution)/shard_map/ppermute | solution.py:26
  15.6 2.3 collective-permute-start.3
  17.9 3.7 collective-permute-start.4
  22.3 2.9 collective-permute-done
  25.2 1.9 collective-permute-start.5
  27.9 2.1 collective-permute-start.6
  30.7 11.9 %collective-permute-done.2 = bf16[128,1024]{0,1:T(8,128)(2,1)S(1)} collective-permute-done((bf16[128,1024]{0,1:T(8,128)(2,1)S(1)}, bf16[128,1024]{0,1:T(8,128)(2,1)S(1)}, u32[]{:S(2)}, u32[]{:S(2)}) %collective-permute-start.2) | collective-permute-done | bytes 262176 | tf_op jit(solution)/shard_map/ppermute | solution.py:26
  42.6 1.9 collective-permute-start.7
  48.3 2.0 collective-permute-done.7
  51.8 2.4 broadcast_in_dim.43
  54.2 35.7 %while.14 = (s32[]{:T(128)}, f32[1152,1024]{0,1:T(8,128)}, bf16[128,2048]{1,0:T(8,128)(2,1)}, bf16[1152,1024]{0,1:T(8,128)(2,1)}, bf16[128,2048]{1,0:T(8,128)(2,...) while((s32[]{:T(128)}, f32[1152,1024]{0,1:T(8,128)}, ...), condition=%wide.region_3.4_spmd.clone, body=%wide.region_0.3_spmd.clone.sunk | while | flops 459033344 | bytes 7806429 | solution.py:76
  56.4 1.8 fusion.44
  58.2 1.6 fusion.45
  60.0 2.0 fusion.46
  65.4 1.8 fusion.44
  67.2 1.6 fusion.45
  68.9 2.0 fusion.46
  74.3 1.8 fusion.44
  76.1 1.6 fusion.45
  77.8 2.0 fusion.46
  83.2 1.8 fusion.44
  85.0 1.6 fusion.45
  86.8 2.0 fusion.46
  89.9 2.5 fusion.23
  92.4 4.8 %collective-permute-start.10 = (f32[128,1024]{0,1:T(8,128)S(1)}, f32[128,1024]{0,1:T(8,128)S(1)}, u32[]{:S(2)}, u32[]{:S(2)}) collective-permute-start(f32[128,1024]{0,1:T(8,128)S(1)} %get-tuple-element.192), channel_id=1, source_target_pairs={{3,0},{4,1},{5,2},{6,3},{7,4},{8,5},{9,6},{10,7},{11,8},{12,9},{13... | collective-permute-start | bytes 1572872 | tf_op jit(solution)/shard_map/ppermute | solution.py:26
  97.3 2.8 collective-permute-start.11
  100.0 1.9 collective-permute-start.12
  102.0 4.7 %collective-permute-start.13 = (f32[128,1024]{0,1:T(8,128)S(1)}, f32[128,1024]{0,1:T(8,128)S(1)}, u32[]{:S(2)}, u32[]{:S(2)}) collective-permute-start(f32[128,1024]{0,1:T(8,128)S(1)} %get-tuple-element.189), channel_id=1, source_target_pairs={{6,0},{7,1},{8,2},{9,3},{10,4},{11,5},{12,6},{13,7},{14,8},{15,9},... | collective-permute-start | bytes 1572872 | tf_op jit(solution)/shard_map/ppermute | solution.py:26
  106.7 1.9 collective-permute-start.14
  108.9 1.9 collective-permute-start.15
  110.8 20.9 %collective-permute-done.11 = f32[128,1024]{0,1:T(8,128)S(1)} collective-permute-done((f32[128,1024]{0,1:T(8,128)S(1)}, f32[128,1024]{0,1:T(8,128)S(1)}, u32[]{:S(2)}, u32[]{:S(2)}) %collective-permute-start.11) | collective-permute-done | bytes 524320 | tf_op jit(solution)/shard_map/ppermute | solution.py:26
  131.7 6.3 %collective-permute-start.8 = (f32[128,1024]{0,1:T(8,128)S(1)}, f32[128,1024]{0,1:T(8,128)S(1)}, u32[]{:S(2)}, u32[]{:S(2)}) collective-permute-start(f32[128,1024]{0,1:T(8,128)S(1)} %get-tuple-element.187), channel_id=1, source_target_pairs={{1,0},{2,1},{3,2},{4,3},{5,4},{6,5},{7,6},{8,7},{9,8},{10,9},{11,1... | collective-permute-start | bytes 1572872 | tf_op jit(solution)/shard_map/ppermute | solution.py:26
  138.0 17.1 %collective-permute-done.12 = f32[128,1024]{0,1:T(8,128)S(1)} collective-permute-done((f32[128,1024]{0,1:T(8,128)S(1)}, f32[128,1024]{0,1:T(8,128)S(1)}, u32[]{:S(2)}, u32[]{:S(2)}) %collective-permute-start.12) | collective-permute-done | bytes 524320 | tf_op jit(solution)/shard_map/ppermute | solution.py:26
  155.1 1.9 collective-permute-start.9
  157.0 9.3 %collective-permute-done.13 = f32[128,1024]{0,1:T(8,128)S(1)} collective-permute-done((f32[128,1024]{0,1:T(8,128)S(1)}, f32[128,1024]{0,1:T(8,128)S(1)}, u32[]{:S(2)}, u32[]{:S(2)}) %collective-permute-start.13) | collective-permute-done | bytes 524320 | tf_op jit(solution)/shard_map/ppermute | solution.py:26
  166.3 5.0 %collective-permute-done.8 = f32[128,1024]{0,1:T(8,128)S(1)} collective-permute-done((f32[128,1024]{0,1:T(8,128)S(1)}, f32[128,1024]{0,1:T(8,128)S(1)}, u32[]{:S(2)}, u32[]{:S(2)}) %collective-permute-start.8) | collective-permute-done | bytes 524320 | tf_op jit(solution)/shard_map/ppermute | solution.py:26
  171.3 13.1 %collective-permute-done.9 = f32[128,1024]{0,1:T(8,128)S(1)} collective-permute-done((f32[128,1024]{0,1:T(8,128)S(1)}, f32[128,1024]{0,1:T(8,128)S(1)}, u32[]{:S(2)}, u32[]{:S(2)}) %collective-permute-start.9) | collective-permute-done | bytes 524320 | tf_op jit(solution)/shard_map/ppermute | solution.py:26
  185.8 2.5 broadcast_in_dim.44
  188.3 21.6 %all-to-all-start = ((bf16[16,128,1024]{2,1,0:T(8,128)(2,1)}), bf16[16,128,1024]{2,1,0:T(8,128)(2,1)}, u32[]{:S(2)}, u32[]{:S(2)}) async-start(bf16[16,128,1024]{2,1,0:T(8,128)(2,1)} %broadcast_in_dim.44), calls=%async_computation | async-start | bytes 8388608 | tf_op jit(solution)/shard_map/all_to_all | solution.py:92
  210.3 48.8 %all-to-all-done = bf16[16,128,1024]{2,1,0:T(8,128)(2,1)} async-done(((bf16[16,128,1024]{2,1,0:T(8,128)(2,1)}), bf16[16,128,1024]{2,1,0:T(8,128)(2,1)}, u32[]{:S(2)}, u32[]{:S(2)}) %all-to-all-start) | async-done | bytes 4194336 | tf_op jit(solution)/shard_map/all_to_all | solution.py:92
  259.1 6.2 %fusion.21 = (f32[1024]{0:T(1024)S(1)}, f32[1024,336]{1,0:T(8,128)}) fusion(bf16[336,1024]{0,1:T(8,128)(2,1)S(1)} %copy.49, f32[1024]{0:T(1024)S(1)} %copy-done.5, bf16[2048,1024]{1,0:T(8,128)(2,1)} %bitcast, bf16[336,2048]{1,0:T(8,128)(2,1)S(1)} %copy-done), kind=kOutput, calls=%fused_computation.28 | convolution fusion | flops 1411693568 | bytes 7643136 | tf_op jit(solution)/shard_map/dot_general | solution.py:95
  265.2 18.9 %all-to-all-start.1 = ((f32[336,32,32]{0,2,1:T(8,128)}), f32[336,32,32]{0,2,1:T(8,128)S(1)}, u32[]{:S(2)}, u32[]{:S(2)}) async-start(f32[336,32,32]{0,2,1:T(8,128)} %bitcast.67), calls=%async_computation.1 | async-start | bytes 3145728 | tf_op jit(solution)/shard_map/all_to_all | solution.py:108
  284.1 1.5 fusion.18
  285.6 138.0 %psum.7 = f32[1024]{0:T(1024)S(1)} all-reduce(f32[1024]{0:T(1024)S(1)} %get-tuple-element.195), channel_id=1, replica_groups=mesh['z'=16,'xh'=2,'y'=4,'xl'=2,'c'=2] {'z','xh','y','xl','c'}, use_global_device_ids=true, to_apply=%region_6.7 | all-reduce | flops 1024 | bytes 8192 | tf_op jit(solution)/shard_map/psum | solution.py:102
  424.3 6.0 %all_gather.6 = bf16[336,64]{0,1:T(8,128)(2,1)S(1)} all-gather(bf16[336,32]{0,1:T(8,128)(2,1)S(1)} %select_convert_fusion), channel_id=1, replica_groups=mesh['z'=16,'xh'=2,'y'=4,'xl'=2,'c'=2] {'xh'}, dimensions={1}, use_global_device_ids=true | all-gather | bytes 64512 | tf_op jit(solution)/shard_map/all_gather | solution.py:113
  430.3 33.3 %all_gather.7 = bf16[336,1024]{0,1:T(8,128)(2,1)S(1)} all-gather(bf16[336,64]{0,1:T(8,128)(2,1)S(1)} %all_gather.6), channel_id=1, replica_groups=mesh['z'=16,'xh'=2,'y'=4,'xl'=2,'c'=2] {'z'}, dimensions={1}, use_global_device_ids=true | all-gather | bytes 731136 | tf_op jit(solution)/shard_map/all_gather | solution.py:114
  (89 shorter events, 26.4 us)
Async XLA Ops:
  0.6 258.4 %copy-start = (bf16[336,2048]{1,0:T(8,128)(2,1)S(1)}, bf16[336,2048]{1,0:T(8,128)(2,1)}, u32[]{:S(2)}) copy-start(bf16[336,2048]{1,0:T(8,128)(2,1)} %param.8) | copy-start | bytes 4128772
  1.9 23.3 %collective-permute-start = (bf16[128,1024]{0,1:T(8,128)(2,1)S(1)}, bf16[128,1024]{0,1:T(8,128)(2,1)S(1)}, u32[]{:S(2)}, u32[]{:S(2)}) collective-permute-start(bf16[128,1024]{0,1:T(8,128)(2,1)S(1)} %copy.50), channel_id=1, source_target_pairs={{0,8},{1,9},{2,10},{3,11},{4,12},{5,13},{6,14},{7,15},{8,16},{9,17... | collective-permute-start | bytes 786440 | tf_op jit(solution)/shard_map/ppermute | solution.py:26
  7.0 20.9 %collective-permute-start.1 = (bf16[128,1024]{0,1:T(8,128)(2,1)S(1)}, bf16[128,1024]{0,1:T(8,128)(2,1)S(1)}, u32[]{:S(2)}, u32[]{:S(2)}) collective-permute-start(bf16[128,1024]{0,1:T(8,128)(2,1)S(1)} %copy.50), channel_id=1, source_target_pairs={{0,7},{1,8},{2,9},{3,10},{4,11},{5,12},{6,13},{7,14},{8,15},{9,16}... | collective-permute-start | bytes 786440 | tf_op jit(solution)/shard_map/ppermute | solution.py:26
  10.0 32.6 %collective-permute-start.2 = (bf16[128,1024]{0,1:T(8,128)(2,1)S(1)}, bf16[128,1024]{0,1:T(8,128)(2,1)S(1)}, u32[]{:S(2)}, u32[]{:S(2)}) collective-permute-start(bf16[128,1024]{0,1:T(8,128)(2,1)S(1)} %copy.50), channel_id=1, source_target_pairs={{0,6},{1,7},{2,8},{3,9},{4,10},{5,11},{6,12},{7,13},{8,14},{9,15},... | collective-permute-start | bytes 786440 | tf_op jit(solution)/shard_map/ppermute | solution.py:26
  15.6 29.7 %collective-permute-start.3 = (bf16[128,1024]{0,1:T(8,128)(2,1)S(1)}, bf16[128,1024]{0,1:T(8,128)(2,1)S(1)}, u32[]{:S(2)}, u32[]{:S(2)}) collective-permute-start(bf16[128,1024]{0,1:T(8,128)(2,1)S(1)} %copy.50), channel_id=1, source_target_pairs={{0,5},{1,6},{2,7},{3,8},{4,9},{5,10},{6,11},{7,12},{8,13},{9,14},{... | collective-permute-start | bytes 786440 | tf_op jit(solution)/shard_map/ppermute | solution.py:26
  17.9 28.0 %collective-permute-start.4 = (bf16[128,1024]{0,1:T(8,128)(2,1)S(1)}, bf16[128,1024]{0,1:T(8,128)(2,1)S(1)}, u32[]{:S(2)}, u32[]{:S(2)}) collective-permute-start(bf16[128,1024]{0,1:T(8,128)(2,1)S(1)} %copy.50), channel_id=1, source_target_pairs={{0,4},{1,5},{2,6},{3,7},{4,8},{5,9},{6,10},{7,11},{8,12},{9,13},{1... | collective-permute-start | bytes 786440 | tf_op jit(solution)/shard_map/ppermute | solution.py:26
  25.2 21.6 %collective-permute-start.5 = (bf16[128,1024]{0,1:T(8,128)(2,1)S(1)}, bf16[128,1024]{0,1:T(8,128)(2,1)S(1)}, u32[]{:S(2)}, u32[]{:S(2)}) collective-permute-start(bf16[128,1024]{0,1:T(8,128)(2,1)S(1)} %copy.50), channel_id=1, source_target_pairs={{0,3},{1,4},{2,5},{3,6},{4,7},{5,8},{6,9},{7,10},{8,11},{9,12},{10... | collective-permute-start | bytes 786440 | tf_op jit(solution)/shard_map/ppermute | solution.py:26
  27.9 19.6 %collective-permute-start.6 = (bf16[128,1024]{0,1:T(8,128)(2,1)S(1)}, bf16[128,1024]{0,1:T(8,128)(2,1)S(1)}, u32[]{:S(2)}, u32[]{:S(2)}) collective-permute-start(bf16[128,1024]{0,1:T(8,128)(2,1)S(1)} %copy.50), channel_id=1, source_target_pairs={{0,2},{1,3},{2,4},{3,5},{4,6},{5,7},{6,8},{7,9},{8,10},{9,11},{10,... | collective-permute-start | bytes 786440 | tf_op jit(solution)/shard_map/ppermute | solution.py:26
  42.6 7.7 %collective-permute-start.7 = (bf16[128,1024]{0,1:T(8,128)(2,1)S(1)}, bf16[128,1024]{0,1:T(8,128)(2,1)S(1)}, u32[]{:S(2)}, u32[]{:S(2)}) collective-permute-start(bf16[128,1024]{0,1:T(8,128)(2,1)S(1)} %copy.50), channel_id=1, source_target_pairs={{0,1},{1,2},{2,3},{3,4},{4,5},{5,6},{6,7},{7,8},{8,9},{9,10},{10,1... | collective-permute-start | bytes 786440 | tf_op jit(solution)/shard_map/ppermute | solution.py:26
  54.2 5.6 %copy-start.3 = (pred[1152]{0:T(1024)(128)(4,1)}, pred[1152]{0:T(1024)(128)(4,1)S(1)}, u32[]{:S(2)}) copy-start(pred[1152]{0:T(1024)(128)(4,1)S(1)} %get-tuple-element.285) | copy-start | bytes 3460 | tf_op jit(solution)/shard_map/while
  54.2 5.6 %copy-start.6 = (s32[128]{0:T(128)}, s32[128]{0:T(128)S(1)}, u32[]{:S(2)}) copy-start(s32[128]{0:T(128)S(1)} %get-tuple-element.284) | copy-start | bytes 1540 | tf_op jit(solution)/shard_map/while
  62.0 1.1 copy-start.4
  62.0 1.1 copy-start.7
  63.1 5.7 %copy-start.3 = (pred[1152]{0:T(1024)(128)(4,1)}, pred[1152]{0:T(1024)(128)(4,1)S(1)}, u32[]{:S(2)}) copy-start(pred[1152]{0:T(1024)(128)(4,1)S(1)} %get-tuple-element.285) | copy-start | bytes 3460 | tf_op jit(solution)/shard_map/while
  63.1 5.7 %copy-start.6 = (s32[128]{0:T(128)}, s32[128]{0:T(128)S(1)}, u32[]{:S(2)}) copy-start(s32[128]{0:T(128)S(1)} %get-tuple-element.284) | copy-start | bytes 1540 | tf_op jit(solution)/shard_map/while
  70.9 1.1 copy-start.4
  70.9 1.1 copy-start.7
  72.0 5.7 %copy-start.3 = (pred[1152]{0:T(1024)(128)(4,1)}, pred[1152]{0:T(1024)(128)(4,1)S(1)}, u32[]{:S(2)}) copy-start(pred[1152]{0:T(1024)(128)(4,1)S(1)} %get-tuple-element.285) | copy-start | bytes 3460 | tf_op jit(solution)/shard_map/while
  72.0 5.7 %copy-start.6 = (s32[128]{0:T(128)}, s32[128]{0:T(128)S(1)}, u32[]{:S(2)}) copy-start(s32[128]{0:T(128)S(1)} %get-tuple-element.284) | copy-start | bytes 1540 | tf_op jit(solution)/shard_map/while
  79.8 1.1 copy-start.4
  79.8 1.1 copy-start.7
  81.0 5.7 %copy-start.3 = (pred[1152]{0:T(1024)(128)(4,1)}, pred[1152]{0:T(1024)(128)(4,1)S(1)}, u32[]{:S(2)}) copy-start(pred[1152]{0:T(1024)(128)(4,1)S(1)} %get-tuple-element.285) | copy-start | bytes 3460 | tf_op jit(solution)/shard_map/while
  81.0 5.7 %copy-start.6 = (s32[128]{0:T(128)}, s32[128]{0:T(128)S(1)}, u32[]{:S(2)}) copy-start(s32[128]{0:T(128)S(1)} %get-tuple-element.284) | copy-start | bytes 1540 | tf_op jit(solution)/shard_map/while
  88.8 1.1 copy-start.4
  88.8 1.1 copy-start.7
  92.4 16.5 %collective-permute-start.10 = (f32[128,1024]{0,1:T(8,128)S(1)}, f32[128,1024]{0,1:T(8,128)S(1)}, u32[]{:S(2)}, u32[]{:S(2)}) collective-permute-start(f32[128,1024]{0,1:T(8,128)S(1)} %get-tuple-element.192), channel_id=1, source_target_pairs={{3,0},{4,1},{5,2},{6,3},{7,4},{8,5},{9,6},{10,7},{11,8},{12,9},{13... | collective-permute-start | bytes 1572872 | tf_op jit(solution)/shard_map/ppermute | solution.py:26
  97.3 34.4 %collective-permute-start.11 = (f32[128,1024]{0,1:T(8,128)S(1)}, f32[128,1024]{0,1:T(8,128)S(1)}, u32[]{:S(2)}, u32[]{:S(2)}) collective-permute-start(f32[128,1024]{0,1:T(8,128)S(1)} %get-tuple-element.191), channel_id=1, source_target_pairs={{4,0},{5,1},{6,2},{7,3},{8,4},{9,5},{10,6},{11,7},{12,8},{13,9},{1... | collective-permute-start | bytes 1572872 | tf_op jit(solution)/shard_map/ppermute | solution.py:26
  100.0 55.0 %collective-permute-start.12 = (f32[128,1024]{0,1:T(8,128)S(1)}, f32[128,1024]{0,1:T(8,128)S(1)}, u32[]{:S(2)}, u32[]{:S(2)}) collective-permute-start(f32[128,1024]{0,1:T(8,128)S(1)} %get-tuple-element.190), channel_id=1, source_target_pairs={{5,0},{6,1},{7,2},{8,3},{9,4},{10,5},{11,6},{12,7},{13,8},{14,9},{... | collective-permute-start | bytes 1572872 | tf_op jit(solution)/shard_map/ppermute | solution.py:26
  102.0 64.3 %collective-permute-start.13 = (f32[128,1024]{0,1:T(8,128)S(1)}, f32[128,1024]{0,1:T(8,128)S(1)}, u32[]{:S(2)}, u32[]{:S(2)}) collective-permute-start(f32[128,1024]{0,1:T(8,128)S(1)} %get-tuple-element.189), channel_id=1, source_target_pairs={{6,0},{7,1},{8,2},{9,3},{10,4},{11,5},{12,6},{13,7},{14,8},{15,9},... | collective-permute-start | bytes 1572872 | tf_op jit(solution)/shard_map/ppermute | solution.py:26
  106.7 59.6 %collective-permute-start.14 = (f32[128,1024]{0,1:T(8,128)S(1)}, f32[128,1024]{0,1:T(8,128)S(1)}, u32[]{:S(2)}, u32[]{:S(2)}) collective-permute-start(f32[128,1024]{0,1:T(8,128)S(1)} %get-tuple-element.188), channel_id=1, source_target_pairs={{7,0},{8,1},{9,2},{10,3},{11,4},{12,5},{13,6},{14,7},{15,8},{16,9}... | collective-permute-start | bytes 1572872 | tf_op jit(solution)/shard_map/ppermute | solution.py:26
  108.9 57.4 %collective-permute-start.15 = (f32[128,1024]{0,1:T(8,128)S(1)}, f32[128,1024]{0,1:T(8,128)S(1)}, u32[]{:S(2)}, u32[]{:S(2)}) collective-permute-start(f32[128,1024]{0,1:T(8,128)S(1)} %get-tuple-element.194), channel_id=1, source_target_pairs={{8,0},{9,1},{10,2},{11,3},{12,4},{13,5},{14,6},{15,7},{16,8},{17,9... | collective-permute-start | bytes 1572872 | tf_op jit(solution)/shard_map/ppermute | solution.py:26
  131.7 39.6 %collective-permute-start.8 = (f32[128,1024]{0,1:T(8,128)S(1)}, f32[128,1024]{0,1:T(8,128)S(1)}, u32[]{:S(2)}, u32[]{:S(2)}) collective-permute-start(f32[128,1024]{0,1:T(8,128)S(1)} %get-tuple-element.187), channel_id=1, source_target_pairs={{1,0},{2,1},{3,2},{4,3},{5,4},{6,5},{7,6},{8,7},{9,8},{10,9},{11,1... | collective-permute-start | bytes 1572872 | tf_op jit(solution)/shard_map/ppermute | solution.py:26
  155.1 29.3 %collective-permute-start.9 = (f32[128,1024]{0,1:T(8,128)S(1)}, f32[128,1024]{0,1:T(8,128)S(1)}, u32[]{:S(2)}, u32[]{:S(2)}) collective-permute-start(f32[128,1024]{0,1:T(8,128)S(1)} %get-tuple-element.193), channel_id=1, source_target_pairs={{2,0},{3,1},{4,2},{5,3},{6,4},{7,5},{8,6},{9,7},{10,8},{11,9},{12,... | collective-permute-start | bytes 1572872 | tf_op jit(solution)/shard_map/ppermute | solution.py:26
  188.3 21.6 %copy-start.2 = (bf16[336,1024]{1,0:T(8,128)(2,1)S(1)}, bf16[336,1024]{1,0:T(8,128)(2,1)}, u32[]{:S(2)}) copy-start(bf16[336,1024]{1,0:T(8,128)(2,1)} %param.9) | copy-start | bytes 2064388
  188.3 70.8 %copy-start.5 = (f32[1024]{0:T(1024)S(1)}, f32[1024]{0:T(1024)}, u32[]{:S(2)}) copy-start(f32[1024]{0:T(1024)} %param.10) | copy-start | bytes 12292
  188.3 70.8 %all-to-all-start = ((bf16[16,128,1024]{2,1,0:T(8,128)(2,1)}), bf16[16,128,1024]{2,1,0:T(8,128)(2,1)}, u32[]{:S(2)}, u32[]{:S(2)}) async-start(bf16[16,128,1024]{2,1,0:T(8,128)(2,1)} %broadcast_in_dim.44), calls=%async_computation | async-start | bytes 8388608 | tf_op jit(solution)/shard_map/all_to_all | solution.py:92
  210.2 55.0 %copy-start.1 = (bf16[336,1024]{0,1:T(8,128)(2,1)}, bf16[336,1024]{0,1:T(8,128)(2,1)S(1)}, u32[]{:S(2)}) copy-start(bf16[336,1024]{0,1:T(8,128)(2,1)S(1)} %copy.49) | copy-start | bytes 2064388
  265.2 159.0 %all-to-all-start.1 = ((f32[336,32,32]{0,2,1:T(8,128)}), f32[336,32,32]{0,2,1:T(8,128)S(1)}, u32[]{:S(2)}, u32[]{:S(2)}) async-start(f32[336,32,32]{0,2,1:T(8,128)} %bitcast.67), calls=%async_computation.1 | async-start | bytes 3145728 | tf_op jit(solution)/shard_map/all_to_all | solution.py:108

commit v2 on v1

--- a/solution.py
+++ b/solution.py
@@ -99,19 +99,28 @@
         signed = jnp.where(kept_mask, jnp.sign(weight_full), 0.0)
 
         logit_part = jnp.sum(local_grad * signed, axis=0)
-        logit_sum = lax.psum(logit_part, ALL)
-        grad_logit = -logit_sum * threshold * (1.0 - threshold)
+        for axis in reversed(FSDP):
+            logit_part = lax.psum(logit_part, axis)
 
         rows, cols = local_grad.shape
         piece = cols // n_seq
-        pieces = local_grad.reshape(rows, n_seq, piece)
+        payload = jnp.concatenate([local_grad, logit_part[None]], axis=0)
+        pieces = payload.reshape(rows + 1, n_seq, piece)
         received = lax.all_to_all(pieces, SEQ, 1, 1, tiled=True)
-        dense_piece = jnp.sum(received, axis=1)
+        summed = jnp.sum(received, axis=1)
+        dense_piece = summed[:rows]
+        logit_piece = summed[rows:]
         seq_index = lax.axis_index(SEQ)
         kept_piece = lax.dynamic_slice_in_dim(kept_mask, seq_index * piece, piece, 1)
         weight_piece = jnp.where(kept_piece, dense_piece, 0.0).astype(jnp.bfloat16)
-        weight_piece = lax.all_gather(weight_piece, "xh", axis=1, tiled=True)
-        grad_weight = lax.all_gather(weight_piece, "z", axis=1, tiled=True)
+        logit_hi = logit_piece.astype(jnp.bfloat16)
+        logit_lo = (logit_piece - logit_hi.astype(jnp.float32)).astype(jnp.bfloat16)
+        out_piece = jnp.concatenate([weight_piece, logit_hi, logit_lo], axis=0)
+        out_piece = lax.all_gather(out_piece, "xh", axis=1, tiled=True)
+        out_full = lax.all_gather(out_piece, "z", axis=1, tiled=True)
+        grad_weight = out_full[:rows]
+        logit_sum = out_full[rows].astype(jnp.float32) + out_full[rows + 1].astype(jnp.float32)
+        grad_logit = -logit_sum * threshold * (1.0 - threshold)
         return (grad_weight, grad_logit)
 
     return local

time: 467 us -> 434 us (0.929)
  blocking collectives: 177 us -> 65.5 us
  waiting for transfers between devices: 131 us -> 200 us
    psum x1 -> x3, blocking collectives: 138 us -> 27.5 us  [local(): logit_part = lax.psum(logit_part, axis)]
    all_to_all x1, waiting for transfers between devices: 0.01 us -> 71.1 us  [local(): received = lax.all_to_all(pieces, SEQ, 1, 1, tiled=True)]
  transfers between devices with their start and end apart: 18 -> 18, of which waited for: 10 -> 11; matrix products, arithmetic and copies ran while one was open for 2% -> 2% of each run, Pallas kernels for 0% -> 0%
where the time goes in v2:
time: 434 us; the launch traced here: 432 us
  waiting for transfers between devices  200 us (46%)
  starting transfers between devices  95 us (22%)
  blocking collectives  65.5 us (15%)
  local copies, waits for them, and re-layouts  34.2 us (8%)
  matrix products  21.6 us (5%)
  other arithmetic  14.6 us (3%)
    ppermute x16, waiting for transfers between devices, passed_along(): lax.ppermute(value, axis, [(source, source + steps) for source in range(f...  80 us
    all_to_all x1, waiting for transfers between devices, local(): received = lax.all_to_all(pieces, SEQ, 1, 1, tiled=True)  71.1 us
    ppermute x16, starting transfers between devices, passed_along(): lax.ppermute(value, axis, [(source, source + steps) for source in range(f...  53.1 us
    all_to_all x1, waiting for transfers between devices, local(): lax.all_to_all(spread, FSDP, 0, 0, tiled=True)  48.8 us
    all_gather x1, blocking collectives, local(): out_full = lax.all_gather(out_piece, 'z', axis=1, tiled=True)  32.1 us
    psum x3, blocking collectives, local(): logit_part = lax.psum(logit_part, axis)  27.5 us
    all_to_all x1, starting transfers between devices, local(): lax.all_to_all(spread, FSDP, 0, 0, tiled=True)  21.3 us
    all_to_all x1, starting transfers between devices, local(): received = lax.all_to_all(pieces, SEQ, 1, 1, tiled=True)  20.5 us
  transfers between devices with their start and end apart: 18, of which 11 were waited for; matrix products, arithmetic and copies ran while one was open for 2% of the time, Pallas kernels for 0%

profile of v2, /device:TPU:6, one launch (start us, length us, event | category | flops | bytes accessed | tf_op | source)
XLA Modules:
  0.0 431.9 jit_solution(14299108750359982254)
XLA Ops:
  1.9 5.1 %collective-permute-start = (bf16[128,1024]{0,1:T(8,128)(2,1)S(1)}, bf16[128,1024]{0,1:T(8,128)(2,1)S(1)}, u32[]{:S(2)}, u32[]{:S(2)}) collective-permute-start(bf16[128,1024]{0,1:T(8,128)(2,1)S(1)} %copy.88), channel_id=1, source_target_pairs={{0,8},{1,9},{2,10},{3,11},{4,12},{5,13},{6,14},{7,15},{8,16},{9,17... | collective-permute-start | bytes 786440 | tf_op jit(solution)/shard_map/ppermute | solution.py:26
  7.0 3.0 collective-permute-start.1
  10.0 5.6 %collective-permute-start.2 = (bf16[128,1024]{0,1:T(8,128)(2,1)S(1)}, bf16[128,1024]{0,1:T(8,128)(2,1)S(1)}, u32[]{:S(2)}, u32[]{:S(2)}) collective-permute-start(bf16[128,1024]{0,1:T(8,128)(2,1)S(1)} %copy.88), channel_id=1, source_target_pairs={{0,6},{1,7},{2,8},{3,9},{4,10},{5,11},{6,12},{7,13},{8,14},{9,15},... | collective-permute-start | bytes 786440 | tf_op jit(solution)/shard_map/ppermute | solution.py:26
  15.6 2.3 collective-permute-start.3
  17.9 3.7 collective-permute-start.4
  23.4 1.8 collective-permute-done
  25.2 1.9 collective-permute-start.5
  27.8 3.2 collective-permute-start.6
  31.8 10.7 %collective-permute-done.2 = bf16[128,1024]{0,1:T(8,128)(2,1)S(1)} collective-permute-done((bf16[128,1024]{0,1:T(8,128)(2,1)S(1)}, bf16[128,1024]{0,1:T(8,128)(2,1)S(1)}, u32[]{:S(2)}, u32[]{:S(2)}) %collective-permute-start.2) | collective-permute-done | bytes 262176 | tf_op jit(solution)/shard_map/ppermute | solution.py:26
  42.6 1.9 collective-permute-start.7
  48.3 1.9 collective-permute-done.7
  51.8 2.4 broadcast_in_dim.44
  54.2 38.0 %while.14 = (s32[]{:T(128)}, f32[1152,1024]{0,1:T(8,128)}, bf16[128,2048]{1,0:T(8,128)(2,1)}, bf16[1152,1024]{0,1:T(8,128)(2,1)}, bf16[128,2048]{1,0:T(8,128)(2,...) while((s32[]{:T(128)}, f32[1152,1024]{0,1:T(8,128)}, ...), condition=%wide.region_3.4_spmd.clone, body=%wide.region_0.3_spmd.clone.sunk | while | flops 459033344 | bytes 7793005 | solution.py:76
  56.4 1.5 fusion.46
  58.0 1.6 fusion.47
  60.4 2.2 fusion.48
  67.5 1.6 fusion.47
  69.9 2.2 fusion.48
  77.0 1.6 fusion.47
  79.4 2.2 fusion.48
  86.5 1.6 fusion.47
  88.9 2.2 fusion.48
  92.2 2.5 fusion.24
  94.7 4.9 %collective-permute-start.10 = (f32[128,1024]{0,1:T(8,128)S(1)}, f32[128,1024]{0,1:T(8,128)S(1)}, u32[]{:S(2)}, u32[]{:S(2)}) collective-permute-start(f32[128,1024]{0,1:T(8,128)S(1)} %get-tuple-element.210), channel_id=1, source_target_pairs={{3,0},{4,1},{5,2},{6,3},{7,4},{8,5},{9,6},{10,7},{11,8},{12,9},{13... | collective-permute-start | bytes 1572872 | tf_op jit(solution)/shard_map/ppermute | solution.py:26
  99.6 2.8 collective-permute-start.11
  102.3 1.9 collective-permute-start.12
  104.3 4.7 %collective-permute-start.13 = (f32[128,1024]{0,1:T(8,128)S(1)}, f32[128,1024]{0,1:T(8,128)S(1)}, u32[]{:S(2)}, u32[]{:S(2)}) collective-permute-start(f32[128,1024]{0,1:T(8,128)S(1)} %get-tuple-element.207), channel_id=1, source_target_pairs={{6,0},{7,1},{8,2},{9,3},{10,4},{11,5},{12,6},{13,7},{14,8},{15,9},... | collective-permute-start | bytes 1572872 | tf_op jit(solution)/shard_map/ppermute | solution.py:26
  109.0 1.9 collective-permute-start.14
  111.2 1.9 collective-permute-start.15
  113.1 20.9 %collective-permute-done.11 = f32[128,1024]{0,1:T(8,128)S(1)} collective-permute-done((f32[128,1024]{0,1:T(8,128)S(1)}, f32[128,1024]{0,1:T(8,128)S(1)}, u32[]{:S(2)}, u32[]{:S(2)}) %collective-permute-start.11) | collective-permute-done | bytes 524320 | tf_op jit(solution)/shard_map/ppermute | solution.py:26
  134.0 6.3 %collective-permute-start.8 = (f32[128,1024]{0,1:T(8,128)S(1)}, f32[128,1024]{0,1:T(8,128)S(1)}, u32[]{:S(2)}, u32[]{:S(2)}) collective-permute-start(f32[128,1024]{0,1:T(8,128)S(1)} %get-tuple-element.205), channel_id=1, source_target_pairs={{1,0},{2,1},{3,2},{4,3},{5,4},{6,5},{7,6},{8,7},{9,8},{10,9},{11,1... | collective-permute-start | bytes 1572872 | tf_op jit(solution)/shard_map/ppermute | solution.py:26
  140.3 17.1 %collective-permute-done.12 = f32[128,1024]{0,1:T(8,128)S(1)} collective-permute-done((f32[128,1024]{0,1:T(8,128)S(1)}, f32[128,1024]{0,1:T(8,128)S(1)}, u32[]{:S(2)}, u32[]{:S(2)}) %collective-permute-start.12) | collective-permute-done | bytes 524320 | tf_op jit(solution)/shard_map/ppermute | solution.py:26
  157.4 1.9 collective-permute-start.9
  159.3 9.3 %collective-permute-done.13 = f32[128,1024]{0,1:T(8,128)S(1)} collective-permute-done((f32[128,1024]{0,1:T(8,128)S(1)}, f32[128,1024]{0,1:T(8,128)S(1)}, u32[]{:S(2)}, u32[]{:S(2)}) %collective-permute-start.13) | collective-permute-done | bytes 524320 | tf_op jit(solution)/shard_map/ppermute | solution.py:26
  168.6 5.0 %collective-permute-done.8 = f32[128,1024]{0,1:T(8,128)S(1)} collective-permute-done((f32[128,1024]{0,1:T(8,128)S(1)}, f32[128,1024]{0,1:T(8,128)S(1)}, u32[]{:S(2)}, u32[]{:S(2)}) %collective-permute-start.8) | collective-permute-done | bytes 524320 | tf_op jit(solution)/shard_map/ppermute | solution.py:26
  173.6 13.1 %collective-permute-done.9 = f32[128,1024]{0,1:T(8,128)S(1)} collective-permute-done((f32[128,1024]{0,1:T(8,128)S(1)}, f32[128,1024]{0,1:T(8,128)S(1)}, u32[]{:S(2)}, u32[]{:S(2)}) %collective-permute-start.9) | collective-permute-done | bytes 524320 | tf_op jit(solution)/shard_map/ppermute | solution.py:26
  188.2 2.5 broadcast_in_dim.45
  190.7 21.3 %all-to-all-start = ((bf16[16,128,1024]{2,1,0:T(8,128)(2,1)}), bf16[16,128,1024]{2,1,0:T(8,128)(2,1)}, u32[]{:S(2)}, u32[]{:S(2)}) async-start(bf16[16,128,1024]{2,1,0:T(8,128)(2,1)} %broadcast_in_dim.45), calls=%async_computation | async-start | bytes 8388608 | tf_op jit(solution)/shard_map/all_to_all | solution.py:92
  212.4 48.8 %all-to-all-done = bf16[16,128,1024]{2,1,0:T(8,128)(2,1)} async-done(((bf16[16,128,1024]{2,1,0:T(8,128)(2,1)}), bf16[16,128,1024]{2,1,0:T(8,128)(2,1)}, u32[]{:S(2)}, u32[]{:S(2)}) %all-to-all-start) | async-done | bytes 4194336 | tf_op jit(solution)/shard_map/all_to_all | solution.py:92
  261.2 6.2 %fusion.21 = (f32[1024]{0:T(1024)S(1)}, f32[1024,336]{1,0:T(8,128)}) fusion(bf16[336,1024]{0,1:T(8,128)(2,1)S(1)} %copy.87, f32[1024]{0:T(1024)S(1)} %copy-done.3, bf16[2048,1024]{1,0:T(8,128)(2,1)} %bitcast, bf16[336,2048]{1,0:T(8,128)(2,1)S(1)} %copy-done), kind=kOutput, calls=%fused_computation.28 | convolution fusion | flops 1411693568 | bytes 7643136 | tf_op jit(solution)/shard_map/dot_general | solution.py:95
  267.4 2.4 psum.21
  269.8 4.9 %psum.22 = f32[1024]{0:T(1024)S(1)} all-reduce(f32[1024]{0:T(1024)S(1)} %psum.21), channel_id=1, replica_groups=mesh['z'=16,'xh'=2,'y'=4,'xl'=2,'c'=2] {'xl'}, use_global_device_ids=true, to_apply=%region_6.7 | all-reduce | flops 1024 | bytes 8192 | tf_op jit(solution)/shard_map/psum | solution.py:103
  275.1 20.1 %psum.23 = f32[1,32,32]{0,2,1:T(8,128)S(1)} all-reduce(f32[1,32,32]{0,2,1:T(8,128)S(1)} %concatenate.19), channel_id=1, replica_groups=mesh['z'=16,'xh'=2,'y'=4,'xl'=2,'c'=2] {'y'}, use_global_device_ids=true, to_apply=%region_7.8 | all-reduce | flops 1024 | bytes 8192 | tf_op jit(solution)/shard_map/psum | solution.py:103
  295.2 2.8 pad_maximum_fusion
  298.0 20.5 %all-to-all-start.1 = ((f32[337,32,32]{0,2,1:T(8,128)}), f32[337,32,32]{0,2,1:T(8,128)S(1)}, u32[]{:S(2)}, u32[]{:S(2)}) async-start(f32[337,32,32]{0,2,1:T(8,128)} %pad_maximum_fusion), calls=%async_computation.1 | async-start | bytes 3145728 | tf_op jit(solution)/shard_map/all_to_all | solution.py:109
  320.0 71.1 %all-to-all-done.1 = f32[337,32,32]{0,2,1:T(8,128)S(1)} async-done(((f32[337,32,32]{0,2,1:T(8,128)}), f32[337,32,32]{0,2,1:T(8,128)S(1)}, u32[]{:S(2)}, u32[]{:S(2)}) %all-to-all-start.1) | async-done | bytes 1380384 | tf_op jit(solution)/shard_map/all_to_all | solution.py:109
  391.7 6.0 %all_gather.6 = bf16[338,64]{0,1:T(8,128)(2,1)S(1)} all-gather(bf16[338,32]{0,1:T(8,128)(2,1)S(1)} %pad_maximum_fusion.1), channel_id=1, replica_groups=mesh['z'=16,'xh'=2,'y'=4,'xl'=2,'c'=2] {'xh'}, dimensions={1}, use_global_device_ids=true | all-gather | bytes 64896 | tf_op jit(solution)/shard_map/all_gather | solution.py:119
  397.7 32.1 %all_gather.7 = bf16[338,1024]{0,1:T(8,128)(2,1)S(1)} all-gather(bf16[338,64]{0,1:T(8,128)(2,1)S(1)} %all_gather.6), channel_id=1, replica_groups=mesh['z'=16,'xh'=2,'y'=4,'xl'=2,'c'=2] {'z'}, dimensions={1}, use_global_device_ids=true | all-gather | bytes 735488 | tf_op jit(solution)/shard_map/all_gather | solution.py:120
  (68 shorter events, 37.3 us)
Async XLA Ops:
  0.6 260.6 %copy-start = (bf16[336,2048]{1,0:T(8,128)(2,1)S(1)}, bf16[336,2048]{1,0:T(8,128)(2,1)}, u32[]{:S(2)}) copy-start(bf16[336,2048]{1,0:T(8,128)(2,1)} %param.8) | copy-start | bytes 4128772
  1.9 23.3 %collective-permute-start = (bf16[128,1024]{0,1:T(8,128)(2,1)S(1)}, bf16[128,1024]{0,1:T(8,128)(2,1)S(1)}, u32[]{:S(2)}, u32[]{:S(2)}) collective-permute-start(bf16[128,1024]{0,1:T(8,128)(2,1)S(1)} %copy.88), channel_id=1, source_target_pairs={{0,8},{1,9},{2,10},{3,11},{4,12},{5,13},{6,14},{7,15},{8,16},{9,17... | collective-permute-start | bytes 786440 | tf_op jit(solution)/shard_map/ppermute | solution.py:26
  7.0 20.9 %collective-permute-start.1 = (bf16[128,1024]{0,1:T(8,128)(2,1)S(1)}, bf16[128,1024]{0,1:T(8,128)(2,1)S(1)}, u32[]{:S(2)}, u32[]{:S(2)}) collective-permute-start(bf16[128,1024]{0,1:T(8,128)(2,1)S(1)} %copy.88), channel_id=1, source_target_pairs={{0,7},{1,8},{2,9},{3,10},{4,11},{5,12},{6,13},{7,14},{8,15},{9,16}... | collective-permute-start | bytes 786440 | tf_op jit(solution)/shard_map/ppermute | solution.py:26
  10.0 32.6 %collective-permute-start.2 = (bf16[128,1024]{0,1:T(8,128)(2,1)S(1)}, bf16[128,1024]{0,1:T(8,128)(2,1)S(1)}, u32[]{:S(2)}, u32[]{:S(2)}) collective-permute-start(bf16[128,1024]{0,1:T(8,128)(2,1)S(1)} %copy.88), channel_id=1, source_target_pairs={{0,6},{1,7},{2,8},{3,9},{4,10},{5,11},{6,12},{7,13},{8,14},{9,15},... | collective-permute-start | bytes 786440 | tf_op jit(solution)/shard_map/ppermute | solution.py:26
  15.6 29.6 %collective-permute-start.3 = (bf16[128,1024]{0,1:T(8,128)(2,1)S(1)}, bf16[128,1024]{0,1:T(8,128)(2,1)S(1)}, u32[]{:S(2)}, u32[]{:S(2)}) collective-permute-start(bf16[128,1024]{0,1:T(8,128)(2,1)S(1)} %copy.88), channel_id=1, source_target_pairs={{0,5},{1,6},{2,7},{3,8},{4,9},{5,10},{6,11},{7,12},{8,13},{9,14},{... | collective-permute-start | bytes 786440 | tf_op jit(solution)/shard_map/ppermute | solution.py:26
  17.9 28.1 %collective-permute-start.4 = (bf16[128,1024]{0,1:T(8,128)(2,1)S(1)}, bf16[128,1024]{0,1:T(8,128)(2,1)S(1)}, u32[]{:S(2)}, u32[]{:S(2)}) collective-permute-start(bf16[128,1024]{0,1:T(8,128)(2,1)S(1)} %copy.88), channel_id=1, source_target_pairs={{0,4},{1,5},{2,6},{3,7},{4,8},{5,9},{6,10},{7,11},{8,12},{9,13},{1... | collective-permute-start | bytes 786440 | tf_op jit(solution)/shard_map/ppermute | solution.py:26
  25.2 21.6 %collective-permute-start.5 = (bf16[128,1024]{0,1:T(8,128)(2,1)S(1)}, bf16[128,1024]{0,1:T(8,128)(2,1)S(1)}, u32[]{:S(2)}, u32[]{:S(2)}) collective-permute-start(bf16[128,1024]{0,1:T(8,128)(2,1)S(1)} %copy.88), channel_id=1, source_target_pairs={{0,3},{1,4},{2,5},{3,6},{4,7},{5,8},{6,9},{7,10},{8,11},{9,12},{10... | collective-permute-start | bytes 786440 | tf_op jit(solution)/shard_map/ppermute | solution.py:26
  27.8 19.7 %collective-permute-start.6 = (bf16[128,1024]{0,1:T(8,128)(2,1)S(1)}, bf16[128,1024]{0,1:T(8,128)(2,1)S(1)}, u32[]{:S(2)}, u32[]{:S(2)}) collective-permute-start(bf16[128,1024]{0,1:T(8,128)(2,1)S(1)} %copy.88), channel_id=1, source_target_pairs={{0,2},{1,3},{2,4},{3,5},{4,6},{5,7},{6,8},{7,9},{8,10},{9,11},{10,... | collective-permute-start | bytes 786440 | tf_op jit(solution)/shard_map/ppermute | solution.py:26
  42.6 7.7 %collective-permute-start.7 = (bf16[128,1024]{0,1:T(8,128)(2,1)S(1)}, bf16[128,1024]{0,1:T(8,128)(2,1)S(1)}, u32[]{:S(2)}, u32[]{:S(2)}) collective-permute-start(bf16[128,1024]{0,1:T(8,128)(2,1)S(1)} %copy.88), channel_id=1, source_target_pairs={{0,1},{1,2},{2,3},{3,4},{4,5},{5,6},{6,7},{7,8},{8,9},{9,10},{10,1... | collective-permute-start | bytes 786440 | tf_op jit(solution)/shard_map/ppermute | solution.py:26
  94.7 16.5 %collective-permute-start.10 = (f32[128,1024]{0,1:T(8,128)S(1)}, f32[128,1024]{0,1:T(8,128)S(1)}, u32[]{:S(2)}, u32[]{:S(2)}) collective-permute-start(f32[128,1024]{0,1:T(8,128)S(1)} %get-tuple-element.210), channel_id=1, source_target_pairs={{3,0},{4,1},{5,2},{6,3},{7,4},{8,5},{9,6},{10,7},{11,8},{12,9},{13... | collective-permute-start | bytes 1572872 | tf_op jit(solution)/shard_map/ppermute | solution.py:26
  99.6 34.4 %collective-permute-start.11 = (f32[128,1024]{0,1:T(8,128)S(1)}, f32[128,1024]{0,1:T(8,128)S(1)}, u32[]{:S(2)}, u32[]{:S(2)}) collective-permute-start(f32[128,1024]{0,1:T(8,128)S(1)} %get-tuple-element.209), channel_id=1, source_target_pairs={{4,0},{5,1},{6,2},{7,3},{8,4},{9,5},{10,6},{11,7},{12,8},{13,9},{1... | collective-permute-start | bytes 1572872 | tf_op jit(solution)/shard_map/ppermute | solution.py:26
  102.3 55.0 %collective-permute-start.12 = (f32[128,1024]{0,1:T(8,128)S(1)}, f32[128,1024]{0,1:T(8,128)S(1)}, u32[]{:S(2)}, u32[]{:S(2)}) collective-permute-start(f32[128,1024]{0,1:T(8,128)S(1)} %get-tuple-element.208), channel_id=1, source_target_pairs={{5,0},{6,1},{7,2},{8,3},{9,4},{10,5},{11,6},{12,7},{13,8},{14,9},{... | collective-permute-start | bytes 1572872 | tf_op jit(solution)/shard_map/ppermute | solution.py:26
  104.3 64.3 %collective-permute-start.13 = (f32[128,1024]{0,1:T(8,128)S(1)}, f32[128,1024]{0,1:T(8,128)S(1)}, u32[]{:S(2)}, u32[]{:S(2)}) collective-permute-start(f32[128,1024]{0,1:T(8,128)S(1)} %get-tuple-element.207), channel_id=1, source_target_pairs={{6,0},{7,1},{8,2},{9,3},{10,4},{11,5},{12,6},{13,7},{14,8},{15,9},... | collective-permute-start | bytes 1572872 | tf_op jit(solution)/shard_map/ppermute | solution.py:26
  109.0 59.6 %collective-permute-start.14 = (f32[128,1024]{0,1:T(8,128)S(1)}, f32[128,1024]{0,1:T(8,128)S(1)}, u32[]{:S(2)}, u32[]{:S(2)}) collective-permute-start(f32[128,1024]{0,1:T(8,128)S(1)} %get-tuple-element.206), channel_id=1, source_target_pairs={{7,0},{8,1},{9,2},{10,3},{11,4},{12,5},{13,6},{14,7},{15,8},{16,9}... | collective-permute-start | bytes 1572872 | tf_op jit(solution)/shard_map/ppermute | solution.py:26
  111.2 57.4 %collective-permute-start.15 = (f32[128,1024]{0,1:T(8,128)S(1)}, f32[128,1024]{0,1:T(8,128)S(1)}, u32[]{:S(2)}, u32[]{:S(2)}) collective-permute-start(f32[128,1024]{0,1:T(8,128)S(1)} %get-tuple-element.212), channel_id=1, source_target_pairs={{8,0},{9,1},{10,2},{11,3},{12,4},{13,5},{14,6},{15,7},{16,8},{17,9... | collective-permute-start | bytes 1572872 | tf_op jit(solution)/shard_map/ppermute | solution.py:26
  134.0 39.6 %collective-permute-start.8 = (f32[128,1024]{0,1:T(8,128)S(1)}, f32[128,1024]{0,1:T(8,128)S(1)}, u32[]{:S(2)}, u32[]{:S(2)}) collective-permute-start(f32[128,1024]{0,1:T(8,128)S(1)} %get-tuple-element.205), channel_id=1, source_target_pairs={{1,0},{2,1},{3,2},{4,3},{5,4},{6,5},{7,6},{8,7},{9,8},{10,9},{11,1... | collective-permute-start | bytes 1572872 | tf_op jit(solution)/shard_map/ppermute | solution.py:26
  157.4 29.4 %collective-permute-start.9 = (f32[128,1024]{0,1:T(8,128)S(1)}, f32[128,1024]{0,1:T(8,128)S(1)}, u32[]{:S(2)}, u32[]{:S(2)}) collective-permute-start(f32[128,1024]{0,1:T(8,128)S(1)} %get-tuple-element.211), channel_id=1, source_target_pairs={{2,0},{3,1},{4,2},{5,3},{6,4},{7,5},{8,6},{9,7},{10,8},{11,9},{12,... | collective-permute-start | bytes 1572872 | tf_op jit(solution)/shard_map/ppermute | solution.py:26
  190.7 21.3 %copy-start.2 = (bf16[336,1024]{1,0:T(8,128)(2,1)S(1)}, bf16[336,1024]{1,0:T(8,128)(2,1)}, u32[]{:S(2)}) copy-start(bf16[336,1024]{1,0:T(8,128)(2,1)} %param.9) | copy-start | bytes 2064388
  190.7 70.5 %copy-start.3 = (f32[1024]{0:T(1024)S(1)}, f32[1024]{0:T(1024)}, u32[]{:S(2)}) copy-start(f32[1024]{0:T(1024)} %param.10) | copy-start | bytes 12292
  190.7 70.5 %all-to-all-start = ((bf16[16,128,1024]{2,1,0:T(8,128)(2,1)}), bf16[16,128,1024]{2,1,0:T(8,128)(2,1)}, u32[]{:S(2)}, u32[]{:S(2)}) async-start(bf16[16,128,1024]{2,1,0:T(8,128)(2,1)} %broadcast_in_dim.45), calls=%async_computation | async-start | bytes 8388608 | tf_op jit(solution)/shard_map/all_to_all | solution.py:92
  212.4 55.0 %copy-start.1 = (bf16[336,1024]{0,1:T(8,128)(2,1)}, bf16[336,1024]{0,1:T(8,128)(2,1)S(1)}, u32[]{:S(2)}) copy-start(bf16[336,1024]{0,1:T(8,128)(2,1)S(1)} %copy.87) | copy-start | bytes 2064388
  298.0 93.1 %all-to-all-start.1 = ((f32[337,32,32]{0,2,1:T(8,128)}), f32[337,32,32]{0,2,1:T(8,128)S(1)}, u32[]{:S(2)}, u32[]{:S(2)}) async-start(f32[337,32,32]{0,2,1:T(8,128)} %pad_maximum_fusion), calls=%async_computation.1 | async-start | bytes 3145728 | tf_op jit(solution)/shard_map/all_to_all | solution.py:109

commit v3 on v2

--- a/solution.py
+++ b/solution.py
@@ -84,8 +84,8 @@
 
         own_grad = block_at(0)
         for distance in range(1, hop_count + 1):
-            sent = passed_along(block_at(distance), ALL, n_all, -distance)
-            own_grad = own_grad + sent
+            sent = passed_along(block_at(distance).astype(jnp.bfloat16), ALL, n_all, -distance)
+            own_grad = own_grad + sent.astype(jnp.float32)
         value_grad = own_grad.astype(jnp.bfloat16)
 
         spread = jnp.broadcast_to(value_grad[None], (n_fsdp,) + value_grad.shape)

time: 434 us -> 378 us (0.87)
  waiting for transfers between devices: 200 us -> 163 us
  starting transfers between devices: 95 us -> 76.4 us
    ppermute x16, waiting for transfers between devices: 80 us -> 42.6 us  [passed_along(): lax.ppermute(value, axis, [(source, source + steps) for source in range(f...]
    all_to_all x1, starting transfers between devices: 21.3 us -> 8.78 us  [local(): lax.all_to_all(spread, FSDP, 0, 0, tiled=True)]
    ppermute x16, starting transfers between devices: 53.1 us -> 48.7 us  [passed_along(): lax.ppermute(value, axis, [(source, source + steps) for source in range(f...]
  transfers between devices with their start and end apart: 18 -> 18, of which waited for: 11 -> 9; matrix products, arithmetic and copies ran while one was open for 2% -> 2% of each run, Pallas kernels for 0% -> 0%
where the time goes in v3:
time: 378 us; the launch traced here: 376 us
  waiting for transfers between devices  163 us (43%)
  starting transfers between devices  76.4 us (20%)
  blocking collectives  65.5 us (17%)
  local copies, waits for them, and re-layouts  32.1 us (8%)
  matrix products  21.6 us (6%)
  other arithmetic  17.3 us (5%)
    all_to_all x1, waiting for transfers between devices, local(): received = lax.all_to_all(pieces, SEQ, 1, 1, tiled=True)  71.1 us
    all_to_all x1, waiting for transfers between devices, local(): lax.all_to_all(spread, FSDP, 0, 0, tiled=True)  48.8 us
    ppermute x16, starting transfers between devices, passed_along(): lax.ppermute(value, axis, [(source, source + steps) for source in range(f...  48.7 us
    ppermute x16, waiting for transfers between devices, passed_along(): lax.ppermute(value, axis, [(source, source + steps) for source in range(f...  42.6 us
    all_gather x1, blocking collectives, local(): out_full = lax.all_gather(out_piece, 'z', axis=1, tiled=True)  32.1 us
    psum x3, blocking collectives, local(): logit_part = lax.psum(logit_part, axis)  27.5 us
    all_to_all x1, starting transfers between devices, local(): received = lax.all_to_all(pieces, SEQ, 1, 1, tiled=True)  18.9 us
    dot_general x4, matrix products, group_step(): jnp.einsum('grqk,qgrd->kgd', probabilities, d_cols, preferred_element_typ...  8.88 us
  transfers between devices with their start and end apart: 18, of which 9 were waited for; matrix products, arithmetic and copies ran while one was open for 2% of the time, Pallas kernels for 0%

profile of v3, /device:TPU:6, one launch (start us, length us, event | category | flops | bytes accessed | tf_op | source)
XLA Modules:
  0.0 376.5 jit_solution(9353215044761996383)
XLA Ops:
  1.9 5.1 %collective-permute-start = (bf16[128,1024]{0,1:T(8,128)(2,1)S(1)}, bf16[128,1024]{0,1:T(8,128)(2,1)S(1)}, u32[]{:S(2)}, u32[]{:S(2)}) collective-permute-start(bf16[128,1024]{0,1:T(8,128)(2,1)S(1)} %copy.88), channel_id=1, source_target_pairs={{0,8},{1,9},{2,10},{3,11},{4,12},{5,13},{6,14},{7,15},{8,16},{9,17... | collective-permute-start | bytes 786440 | tf_op jit(solution)/shard_map/ppermute | solution.py:26
  7.0 3.0 collective-permute-start.1
  10.0 5.6 %collective-permute-start.2 = (bf16[128,1024]{0,1:T(8,128)(2,1)S(1)}, bf16[128,1024]{0,1:T(8,128)(2,1)S(1)}, u32[]{:S(2)}, u32[]{:S(2)}) collective-permute-start(bf16[128,1024]{0,1:T(8,128)(2,1)S(1)} %copy.88), channel_id=1, source_target_pairs={{0,6},{1,7},{2,8},{3,9},{4,10},{5,11},{6,12},{7,13},{8,14},{9,15},... | collective-permute-start | bytes 786440 | tf_op jit(solution)/shard_map/ppermute | solution.py:26
  15.6 2.3 collective-permute-start.3
  17.9 3.7 collective-permute-start.4
  23.4 1.8 collective-permute-done
  25.2 1.9 collective-permute-start.5
  27.8 3.2 collective-permute-start.6
  31.8 10.7 %collective-permute-done.2 = bf16[128,1024]{0,1:T(8,128)(2,1)S(1)} collective-permute-done((bf16[128,1024]{0,1:T(8,128)(2,1)S(1)}, bf16[128,1024]{0,1:T(8,128)(2,1)S(1)}, u32[]{:S(2)}, u32[]{:S(2)}) %collective-permute-start.2) | collective-permute-done | bytes 262176 | tf_op jit(solution)/shard_map/ppermute | solution.py:26
  42.6 1.9 collective-permute-start.7
  48.3 1.9 collective-permute-done.7
  51.8 2.4 broadcast_in_dim.44
  54.2 38.0 %while.14 = (s32[]{:T(128)}, f32[1152,1024]{0,1:T(8,128)}, bf16[128,2048]{1,0:T(8,128)(2,1)}, bf16[1152,1024]{0,1:T(8,128)(2,1)}, bf16[128,2048]{1,0:T(8,128)(2,...) while((s32[]{:T(128)}, f32[1152,1024]{0,1:T(8,128)}, ...), condition=%wide.region_3.4_spmd.clone, body=%wide.region_0.3_spmd.clone.sunk | while | flops 459033344 | bytes 7793005 | solution.py:76
  56.4 1.5 fusion.46
  58.0 1.6 fusion.47
  60.4 2.2 fusion.48
  65.9 1.5 fusion.46
  67.5 1.6 fusion.47
  69.9 2.2 fusion.48
  75.5 1.5 fusion.46
  77.0 1.6 fusion.47
  79.4 2.2 fusion.48
  86.5 1.6 fusion.47
  88.9 2.2 fusion.48
  92.2 2.6 convert.10
  95.2 4.9 %collective-permute-start.10 = (bf16[128,1024]{0,1:T(8,128)(2,1)S(1)}, bf16[128,1024]{0,1:T(8,128)(2,1)S(1)}, u32[]{:S(2)}, u32[]{:S(2)}) collective-permute-start(bf16[128,1024]{0,1:T(8,128)(2,1)S(1)} %get-tuple-element.211), channel_id=1, source_target_pairs={{3,0},{4,1},{5,2},{6,3},{7,4},{8,5},{9,6},{10,7},{11,8},{12,9},{13... | collective-permute-start | bytes 786440 | tf_op jit(solution)/shard_map/ppermute | solution.py:26
  100.1 2.8 collective-permute-start.11
  102.8 1.9 collective-permute-start.12
  104.8 4.7 %collective-permute-start.13 = (bf16[128,1024]{0,1:T(8,128)(2,1)S(1)}, bf16[128,1024]{0,1:T(8,128)(2,1)S(1)}, u32[]{:S(2)}, u32[]{:S(2)}) collective-permute-start(bf16[128,1024]{0,1:T(8,128)(2,1)S(1)} %get-tuple-element.208), channel_id=1, source_target_pairs={{6,0},{7,1},{8,2},{9,3},{10,4},{11,5},{12,6},{13,7},{14,8},{15,9},... | collective-permute-start | bytes 786440 | tf_op jit(solution)/shard_map/ppermute | solution.py:26
  109.5 1.9 collective-permute-start.14
  111.4 1.9 collective-permute-start.15
  114.0 1.9 collective-permute-start.8
  115.9 12.2 %collective-permute-done.12 = bf16[128,1024]{0,1:T(8,128)(2,1)S(1)} collective-permute-done((bf16[128,1024]{0,1:T(8,128)(2,1)S(1)}, bf16[128,1024]{0,1:T(8,128)(2,1)S(1)}, u32[]{:S(2)}, u32[]{:S(2)}) %collective-permute-start.12) | collective-permute-done | bytes 262176 | tf_op jit(solution)/shard_map/ppermute | solution.py:26
  128.1 1.9 collective-permute-start.9
  130.0 3.7 collective-permute-done.13
  133.7 11.7 %collective-permute-done.9 = bf16[128,1024]{0,1:T(8,128)(2,1)S(1)} collective-permute-done((bf16[128,1024]{0,1:T(8,128)(2,1)S(1)}, bf16[128,1024]{0,1:T(8,128)(2,1)S(1)}, u32[]{:S(2)}, u32[]{:S(2)}) %collective-permute-start.9) | collective-permute-done | bytes 262176 | tf_op jit(solution)/shard_map/ppermute | solution.py:26
  146.9 2.5 broadcast_in_dim.45
  149.4 8.8 %all-to-all-start = ((bf16[16,128,1024]{2,1,0:T(8,128)(2,1)}), bf16[16,128,1024]{2,1,0:T(8,128)(2,1)}, u32[]{:S(2)}, u32[]{:S(2)}) async-start(bf16[16,128,1024]{2,1,0:T(8,128)(2,1)} %broadcast_in_dim.45), calls=%async_computation | async-start | bytes 8388608 | tf_op jit(solution)/shard_map/all_to_all | solution.py:92
  158.6 48.8 %all-to-all-done = bf16[16,128,1024]{2,1,0:T(8,128)(2,1)} async-done(((bf16[16,128,1024]{2,1,0:T(8,128)(2,1)}), bf16[16,128,1024]{2,1,0:T(8,128)(2,1)}, u32[]{:S(2)}, u32[]{:S(2)}) %all-to-all-start) | async-done | bytes 4194336 | tf_op jit(solution)/shard_map/all_to_all | solution.py:92
  207.4 6.2 %fusion.21 = (f32[1024]{0:T(1024)S(1)}, f32[1024,336]{1,0:T(8,128)}) fusion(bf16[336,1024]{0,1:T(8,128)(2,1)S(1)} %copy.87, f32[1024]{0:T(1024)S(1)} %copy-done.3, bf16[2048,1024]{1,0:T(8,128)(2,1)} %bitcast, bf16[336,2048]{1,0:T(8,128)(2,1)S(1)} %copy-done), kind=kOutput, calls=%fused_computation.28 | convolution fusion | flops 1411693568 | bytes 7643136 | tf_op jit(solution)/shard_map/dot_general | solution.py:95
  213.6 2.4 psum.21
  216.0 4.9 %psum.22 = f32[1024]{0:T(1024)S(1)} all-reduce(f32[1024]{0:T(1024)S(1)} %psum.21), channel_id=1, replica_groups=mesh['z'=16,'xh'=2,'y'=4,'xl'=2,'c'=2] {'xl'}, use_global_device_ids=true, to_apply=%region_6.7 | all-reduce | flops 1024 | bytes 8192 | tf_op jit(solution)/shard_map/psum | solution.py:103
  221.3 20.1 %psum.23 = f32[1,32,32]{0,2,1:T(8,128)S(1)} all-reduce(f32[1,32,32]{0,2,1:T(8,128)S(1)} %concatenate.19), channel_id=1, replica_groups=mesh['z'=16,'xh'=2,'y'=4,'xl'=2,'c'=2] {'y'}, use_global_device_ids=true, to_apply=%region_7.8 | all-reduce | flops 1024 | bytes 8192 | tf_op jit(solution)/shard_map/psum | solution.py:103
  241.4 2.8 pad_maximum_fusion
  244.2 18.9 %all-to-all-start.1 = ((f32[337,32,32]{0,2,1:T(8,128)}), f32[337,32,32]{0,2,1:T(8,128)S(1)}, u32[]{:S(2)}, u32[]{:S(2)}) async-start(f32[337,32,32]{0,2,1:T(8,128)} %pad_maximum_fusion), calls=%async_computation.1 | async-start | bytes 3145728 | tf_op jit(solution)/shard_map/all_to_all | solution.py:109
  264.6 71.1 %all-to-all-done.1 = f32[337,32,32]{0,2,1:T(8,128)S(1)} async-done(((f32[337,32,32]{0,2,1:T(8,128)}), f32[337,32,32]{0,2,1:T(8,128)S(1)}, u32[]{:S(2)}, u32[]{:S(2)}) %all-to-all-start.1) | async-done | bytes 1380384 | tf_op jit(solution)/shard_map/all_to_all | solution.py:109
  336.3 6.0 %all_gather.6 = bf16[338,64]{0,1:T(8,128)(2,1)S(1)} all-gather(bf16[338,32]{0,1:T(8,128)(2,1)S(1)} %pad_maximum_fusion.1), channel_id=1, replica_groups=mesh['z'=16,'xh'=2,'y'=4,'xl'=2,'c'=2] {'xh'}, dimensions={1}, use_global_device_ids=true | all-gather | bytes 64896 | tf_op jit(solution)/shard_map/all_gather | solution.py:119
  342.3 32.1 %all_gather.7 = bf16[338,1024]{0,1:T(8,128)(2,1)S(1)} all-gather(bf16[338,64]{0,1:T(8,128)(2,1)S(1)} %all_gather.6), channel_id=1, replica_groups=mesh['z'=16,'xh'=2,'y'=4,'xl'=2,'c'=2] {'z'}, dimensions={1}, use_global_device_ids=true | all-gather | bytes 735488 | tf_op jit(solution)/shard_map/all_gather | solution.py:120
  (69 shorter events, 35.1 us)
Async XLA Ops:
  0.6 206.8 %copy-start = (bf16[336,2048]{1,0:T(8,128)(2,1)S(1)}, bf16[336,2048]{1,0:T(8,128)(2,1)}, u32[]{:S(2)}) copy-start(bf16[336,2048]{1,0:T(8,128)(2,1)} %param.8) | copy-start | bytes 4128772
  1.9 23.3 %collective-permute-start = (bf16[128,1024]{0,1:T(8,128)(2,1)S(1)}, bf16[128,1024]{0,1:T(8,128)(2,1)S(1)}, u32[]{:S(2)}, u32[]{:S(2)}) collective-permute-start(bf16[128,1024]{0,1:T(8,128)(2,1)S(1)} %copy.88), channel_id=1, source_target_pairs={{0,8},{1,9},{2,10},{3,11},{4,12},{5,13},{6,14},{7,15},{8,16},{9,17... | collective-permute-start | bytes 786440 | tf_op jit(solution)/shard_map/ppermute | solution.py:26
  7.0 20.9 %collective-permute-start.1 = (bf16[128,1024]{0,1:T(8,128)(2,1)S(1)}, bf16[128,1024]{0,1:T(8,128)(2,1)S(1)}, u32[]{:S(2)}, u32[]{:S(2)}) collective-permute-start(bf16[128,1024]{0,1:T(8,128)(2,1)S(1)} %copy.88), channel_id=1, source_target_pairs={{0,7},{1,8},{2,9},{3,10},{4,11},{5,12},{6,13},{7,14},{8,15},{9,16}... | collective-permute-start | bytes 786440 | tf_op jit(solution)/shard_map/ppermute | solution.py:26
  10.0 32.6 %collective-permute-start.2 = (bf16[128,1024]{0,1:T(8,128)(2,1)S(1)}, bf16[128,1024]{0,1:T(8,128)(2,1)S(1)}, u32[]{:S(2)}, u32[]{:S(2)}) collective-permute-start(bf16[128,1024]{0,1:T(8,128)(2,1)S(1)} %copy.88), channel_id=1, source_target_pairs={{0,6},{1,7},{2,8},{3,9},{4,10},{5,11},{6,12},{7,13},{8,14},{9,15},... | collective-permute-start | bytes 786440 | tf_op jit(solution)/shard_map/ppermute | solution.py:26
  15.6 29.6 %collective-permute-start.3 = (bf16[128,1024]{0,1:T(8,128)(2,1)S(1)}, bf16[128,1024]{0,1:T(8,128)(2,1)S(1)}, u32[]{:S(2)}, u32[]{:S(2)}) collective-permute-start(bf16[128,1024]{0,1:T(8,128)(2,1)S(1)} %copy.88), channel_id=1, source_target_pairs={{0,5},{1,6},{2,7},{3,8},{4,9},{5,10},{6,11},{7,12},{8,13},{9,14},{... | collective-permute-start | bytes 786440 | tf_op jit(solution)/shard_map/ppermute | solution.py:26
  17.9 28.1 %collective-permute-start.4 = (bf16[128,1024]{0,1:T(8,128)(2,1)S(1)}, bf16[128,1024]{0,1:T(8,128)(2,1)S(1)}, u32[]{:S(2)}, u32[]{:S(2)}) collective-permute-start(bf16[128,1024]{0,1:T(8,128)(2,1)S(1)} %copy.88), channel_id=1, source_target_pairs={{0,4},{1,5},{2,6},{3,7},{4,8},{5,9},{6,10},{7,11},{8,12},{9,13},{1... | collective-permute-start | bytes 786440 | tf_op jit(solution)/shard_map/ppermute | solution.py:26
  25.2 21.6 %collective-permute-start.5 = (bf16[128,1024]{0,1:T(8,128)(2,1)S(1)}, bf16[128,1024]{0,1:T(8,128)(2,1)S(1)}, u32[]{:S(2)}, u32[]{:S(2)}) collective-permute-start(bf16[128,1024]{0,1:T(8,128)(2,1)S(1)} %copy.88), channel_id=1, source_target_pairs={{0,3},{1,4},{2,5},{3,6},{4,7},{5,8},{6,9},{7,10},{8,11},{9,12},{10... | collective-permute-start | bytes 786440 | tf_op jit(solution)/shard_map/ppermute | solution.py:26
  27.8 19.7 %collective-permute-start.6 = (bf16[128,1024]{0,1:T(8,128)(2,1)S(1)}, bf16[128,1024]{0,1:T(8,128)(2,1)S(1)}, u32[]{:S(2)}, u32[]{:S(2)}) collective-permute-start(bf16[128,1024]{0,1:T(8,128)(2,1)S(1)} %copy.88), channel_id=1, source_target_pairs={{0,2},{1,3},{2,4},{3,5},{4,6},{5,7},{6,8},{7,9},{8,10},{9,11},{10,... | collective-permute-start | bytes 786440 | tf_op jit(solution)/shard_map/ppermute | solution.py:26
  42.6 7.7 %collective-permute-start.7 = (bf16[128,1024]{0,1:T(8,128)(2,1)S(1)}, bf16[128,1024]{0,1:T(8,128)(2,1)S(1)}, u32[]{:S(2)}, u32[]{:S(2)}) collective-permute-start(bf16[128,1024]{0,1:T(8,128)(2,1)S(1)} %copy.88), channel_id=1, source_target_pairs={{0,1},{1,2},{2,3},{3,4},{4,5},{5,6},{6,7},{7,8},{8,9},{9,10},{10,1... | collective-permute-start | bytes 786440 | tf_op jit(solution)/shard_map/ppermute | solution.py:26
  95.2 16.2 %collective-permute-start.10 = (bf16[128,1024]{0,1:T(8,128)(2,1)S(1)}, bf16[128,1024]{0,1:T(8,128)(2,1)S(1)}, u32[]{:S(2)}, u32[]{:S(2)}) collective-permute-start(bf16[128,1024]{0,1:T(8,128)(2,1)S(1)} %get-tuple-element.211), channel_id=1, source_target_pairs={{3,0},{4,1},{5,2},{6,3},{7,4},{8,5},{9,6},{10,7},{11,8},{12,9},{13... | collective-permute-start | bytes 786440 | tf_op jit(solution)/shard_map/ppermute | solution.py:26
  100.1 14.0 %collective-permute-start.11 = (bf16[128,1024]{0,1:T(8,128)(2,1)S(1)}, bf16[128,1024]{0,1:T(8,128)(2,1)S(1)}, u32[]{:S(2)}, u32[]{:S(2)}) collective-permute-start(bf16[128,1024]{0,1:T(8,128)(2,1)S(1)} %get-tuple-element.210), channel_id=1, source_target_pairs={{4,0},{5,1},{6,2},{7,3},{8,4},{9,5},{10,6},{11,7},{12,8},{13,9},{1... | collective-permute-start | bytes 786440 | tf_op jit(solution)/shard_map/ppermute | solution.py:26
  102.8 25.3 %collective-permute-start.12 = (bf16[128,1024]{0,1:T(8,128)(2,1)S(1)}, bf16[128,1024]{0,1:T(8,128)(2,1)S(1)}, u32[]{:S(2)}, u32[]{:S(2)}) collective-permute-start(bf16[128,1024]{0,1:T(8,128)(2,1)S(1)} %get-tuple-element.209), channel_id=1, source_target_pairs={{5,0},{6,1},{7,2},{8,3},{9,4},{10,5},{11,6},{12,7},{13,8},{14,9},{... | collective-permute-start | bytes 786440 | tf_op jit(solution)/shard_map/ppermute | solution.py:26
  104.8 29.0 %collective-permute-start.13 = (bf16[128,1024]{0,1:T(8,128)(2,1)S(1)}, bf16[128,1024]{0,1:T(8,128)(2,1)S(1)}, u32[]{:S(2)}, u32[]{:S(2)}) collective-permute-start(bf16[128,1024]{0,1:T(8,128)(2,1)S(1)} %get-tuple-element.208), channel_id=1, source_target_pairs={{6,0},{7,1},{8,2},{9,3},{10,4},{11,5},{12,6},{13,7},{14,8},{15,9},... | collective-permute-start | bytes 786440 | tf_op jit(solution)/shard_map/ppermute | solution.py:26
  109.5 24.2 %collective-permute-start.14 = (bf16[128,1024]{0,1:T(8,128)(2,1)S(1)}, bf16[128,1024]{0,1:T(8,128)(2,1)S(1)}, u32[]{:S(2)}, u32[]{:S(2)}) collective-permute-start(bf16[128,1024]{0,1:T(8,128)(2,1)S(1)} %get-tuple-element.207), channel_id=1, source_target_pairs={{7,0},{8,1},{9,2},{10,3},{11,4},{12,5},{13,6},{14,7},{15,8},{16,9}... | collective-permute-start | bytes 786440 | tf_op jit(solution)/shard_map/ppermute | solution.py:26
  111.4 22.3 %collective-permute-start.15 = (bf16[128,1024]{0,1:T(8,128)(2,1)S(1)}, bf16[128,1024]{0,1:T(8,128)(2,1)S(1)}, u32[]{:S(2)}, u32[]{:S(2)}) collective-permute-start(bf16[128,1024]{0,1:T(8,128)(2,1)S(1)} %get-tuple-element.206), channel_id=1, source_target_pairs={{8,0},{9,1},{10,2},{11,3},{12,4},{13,5},{14,6},{15,7},{16,8},{17,9... | collective-permute-start | bytes 786440 | tf_op jit(solution)/shard_map/ppermute | solution.py:26
  114.0 19.7 %collective-permute-start.8 = (bf16[128,1024]{0,1:T(8,128)(2,1)S(1)}, bf16[128,1024]{0,1:T(8,128)(2,1)S(1)}, u32[]{:S(2)}, u32[]{:S(2)}) collective-permute-start(bf16[128,1024]{0,1:T(8,128)(2,1)S(1)} %get-tuple-element.205), channel_id=1, source_target_pairs={{1,0},{2,1},{3,2},{4,3},{5,4},{6,5},{7,6},{8,7},{9,8},{10,9},{11,1... | collective-permute-start | bytes 786440 | tf_op jit(solution)/shard_map/ppermute | solution.py:26
  128.1 17.3 %collective-permute-start.9 = (bf16[128,1024]{0,1:T(8,128)(2,1)S(1)}, bf16[128,1024]{0,1:T(8,128)(2,1)S(1)}, u32[]{:S(2)}, u32[]{:S(2)}) collective-permute-start(bf16[128,1024]{0,1:T(8,128)(2,1)S(1)} %get-tuple-element.212), channel_id=1, source_target_pairs={{2,0},{3,1},{4,2},{5,3},{6,4},{7,5},{8,6},{9,7},{10,8},{11,9},{12,... | collective-permute-start | bytes 786440 | tf_op jit(solution)/shard_map/ppermute | solution.py:26
  149.4 8.8 %copy-start.2 = (bf16[336,1024]{1,0:T(8,128)(2,1)S(1)}, bf16[336,1024]{1,0:T(8,128)(2,1)}, u32[]{:S(2)}) copy-start(bf16[336,1024]{1,0:T(8,128)(2,1)} %param.9) | copy-start | bytes 2064388
  149.4 58.0 %copy-start.3 = (f32[1024]{0:T(1024)S(1)}, f32[1024]{0:T(1024)}, u32[]{:S(2)}) copy-start(f32[1024]{0:T(1024)} %param.10) | copy-start | bytes 12292
  149.4 58.0 %all-to-all-start = ((bf16[16,128,1024]{2,1,0:T(8,128)(2,1)}), bf16[16,128,1024]{2,1,0:T(8,128)(2,1)}, u32[]{:S(2)}, u32[]{:S(2)}) async-start(bf16[16,128,1024]{2,1,0:T(8,128)(2,1)} %broadcast_in_dim.45), calls=%async_computation | async-start | bytes 8388608 | tf_op jit(solution)/shard_map/all_to_all | solution.py:92
  158.6 55.0 %copy-start.1 = (bf16[336,1024]{0,1:T(8,128)(2,1)}, bf16[336,1024]{0,1:T(8,128)(2,1)S(1)}, u32[]{:S(2)}) copy-start(bf16[336,1024]{0,1:T(8,128)(2,1)S(1)} %copy.87) | copy-start | bytes 2064388
  244.2 91.5 %all-to-all-start.1 = ((f32[337,32,32]{0,2,1:T(8,128)}), f32[337,32,32]{0,2,1:T(8,128)S(1)}, u32[]{:S(2)}, u32[]{:S(2)}) async-start(f32[337,32,32]{0,2,1:T(8,128)} %pad_maximum_fusion), calls=%async_computation.1 | async-start | bytes 3145728 | tf_op jit(solution)/shard_map/all_to_all | solution.py:109

commit v4 on v3

--- a/solution.py
+++ b/solution.py
@@ -73,44 +73,59 @@
                 running, value_part.reshape(span_keys, k_span), group_index * k_span, 1
             )
 
-        partial_grad = lax.fori_loop(
-            0, group_count, group_step, jnp.zeros((span_keys, value_weight.shape[1]), jnp.float32)
-        )
-
-        def block_at(distance):
-            return partial_grad[
-                (hop_count - distance) * tok_rows : (hop_count - distance + 1) * tok_rows
-            ]
-
-        own_grad = block_at(0)
-        for distance in range(1, hop_count + 1):
-            sent = passed_along(block_at(distance).astype(jnp.bfloat16), ALL, n_all, -distance)
-            own_grad = own_grad + sent.astype(jnp.float32)
-        value_grad = own_grad.astype(jnp.bfloat16)
-
-        spread = jnp.broadcast_to(value_grad[None], (n_fsdp,) + value_grad.shape)
-        gathered = lax.all_to_all(spread, FSDP, 0, 0, tiled=True).reshape(
-            n_fsdp * tok_rows, value_grad.shape[1]
-        )
-        local_grad = jnp.dot(inputs, gathered, preferred_element_type=jnp.float32)
-
         weight_full = value_weight.astype(jnp.float32)
         kept_mask = jnp.abs(weight_full) > threshold[None, :]
         signed = jnp.where(kept_mask, jnp.sign(weight_full), 0.0)
+        seq_index = lax.axis_index(SEQ)
+        n_chunks = 2
+        chunk_groups = group_count // n_chunks
+        chunk_cols = chunk_groups * k_span
+        rows = inputs.shape[0]
+
+        local_parts = []
+        for chunk in range(n_chunks):
+            def chunk_step(step, running, chunk=chunk):
+                return group_step(chunk * chunk_groups + step, running)
+
+            partial_grad = lax.fori_loop(
+                0,
+                chunk_groups,
+                chunk_step,
+                jnp.zeros((span_keys, value_weight.shape[1]), jnp.float32),
+            )
+            partial_grad = partial_grad[:, chunk * chunk_cols : (chunk + 1) * chunk_cols]
+
+            def block_at(distance):
+                return partial_grad[
+                    (hop_count - distance) * tok_rows : (hop_count - distance + 1) * tok_rows
+                ]
+
+            own_grad = block_at(0)
+            for distance in range(1, hop_count + 1):
+                sent = passed_along(block_at(distance).astype(jnp.bfloat16), ALL, n_all, -distance)
+                own_grad = own_grad + sent.astype(jnp.float32)
+            value_grad = own_grad.astype(jnp.bfloat16)
+
+            spread = jnp.broadcast_to(value_grad[None], (n_fsdp,) + value_grad.shape)
+            gathered = lax.all_to_all(spread, FSDP, 0, 0, tiled=True).reshape(
+                n_fsdp * tok_rows, chunk_cols
+            )
+            local_grad = jnp.dot(inputs, gathered, preferred_element_type=jnp.float32)
+            local_parts.append(local_grad)
+
+        local_grad = jnp.concatenate(local_parts, axis=1)
+        piece = local_grad.shape[1] // n_seq
 
         logit_part = jnp.sum(local_grad * signed, axis=0)
         for axis in reversed(FSDP):
             logit_part = lax.psum(logit_part, axis)
 
-        rows, cols = local_grad.shape
-        piece = cols // n_seq
         payload = jnp.concatenate([local_grad, logit_part[None]], axis=0)
         pieces = payload.reshape(rows + 1, n_seq, piece)
         received = lax.all_to_all(pieces, SEQ, 1, 1, tiled=True)
         summed = jnp.sum(received, axis=1)
         dense_piece = summed[:rows]
         logit_piece = summed[rows:]
-        seq_index = lax.axis_index(SEQ)
         kept_piece = lax.dynamic_slice_in_dim(kept_mask, seq_index * piece, piece, 1)
         weight_piece = jnp.where(kept_piece, dense_piece, 0.0).astype(jnp.bfloat16)
         logit_hi = logit_piece.astype(jnp.bfloat16)

time: 378 us -> 389 us (1.029)
  starting transfers between devices: 76.4 us -> 111 us
  waiting for transfers between devices: 163 us -> 130 us
  other arithmetic: 17.3 us -> 22.9 us
    all_to_all x1 -> x2, waiting for transfers between devices: 48.8 us -> 23.4 us  [local(): lax.all_to_all(spread, FSDP, 0, 0, tiled=True)]
    ppermute x16 -> x24, starting transfers between devices: 48.7 us -> 68.1 us  [passed_along(): lax.ppermute(value, axis, [(source, source + steps) for source in range(f...]
    ppermute x16 -> x24, waiting for transfers between devices: 42.6 us -> 34.2 us  [passed_along(): lax.ppermute(value, axis, [(source, source + steps) for source in range(f...]
    all_to_all x1 -> x2, starting transfers between devices: 8.78 us -> 17.1 us  [local(): lax.all_to_all(spread, FSDP, 0, 0, tiled=True)]
    all_to_all x1, starting transfers between devices: 18.9 us -> 25.7 us  [local(): received = lax.all_to_all(pieces, SEQ, 1, 1, tiled=True)]
    another operation x0 -> x2, local copies, waits for them, and re-layouts: none -> 4.87 us
    unnamed x20 -> x18, local copies, waits for them, and re-layouts: 8.87 us -> 8.83 us
  transfers between devices with their start and end apart: 18 -> 27, of which waited for: 9 -> 10; matrix products, arithmetic and copies ran while one was open for 2% -> 9% of each run, Pallas kernels for 0% -> 0%
where the time goes in v4:
time: 389 us; the launch traced here: 386 us
  waiting for transfers between devices  130 us (33%)
  starting transfers between devices  111 us (29%)
  blocking collectives  65.5 us (17%)
  local copies, waits for them, and re-layouts  35.1 us (9%)
  other arithmetic  22.9 us (6%)
  matrix products  21.1 us (5%)
    all_to_all x1, waiting for transfers between devices, local(): received = lax.all_to_all(pieces, SEQ, 1, 1, tiled=True)  72.3 us
    ppermute x24, starting transfers between devices, passed_along(): lax.ppermute(value, axis, [(source, source + steps) for source in range(f...  68.1 us
    ppermute x24, waiting for transfers between devices, passed_along(): lax.ppermute(value, axis, [(source, source + steps) for source in range(f...  34.2 us
    all_gather x1, blocking collectives, local(): out_full = lax.all_gather(out_piece, 'z', axis=1, tiled=True)  32.1 us
    psum x3, blocking collectives, local(): logit_part = lax.psum(logit_part, axis)  27.5 us
    all_to_all x1, starting transfers between devices, local(): received = lax.all_to_all(pieces, SEQ, 1, 1, tiled=True)  25.7 us
    all_to_all x2, waiting for transfers between devices, local(): lax.all_to_all(spread, FSDP, 0, 0, tiled=True)  23.4 us
    all_to_all x2, starting transfers between devices, local(): lax.all_to_all(spread, FSDP, 0, 0, tiled=True)  17.1 us
  transfers between devices with their start and end apart: 27, of which 10 were waited for; matrix products, arithmetic and copies ran while one was open for 9% of the time, Pallas kernels for 0%

profile of v4, /device:TPU:6, one launch (start us, length us, event | category | flops | bytes accessed | tf_op | source)
XLA Modules:
  0.0 386.5 jit_solution(693270269550272287)
XLA Ops:
  1.9 5.1 %collective-permute-start = (bf16[128,1024]{0,1:T(8,128)(2,1)S(1)}, bf16[128,1024]{0,1:T(8,128)(2,1)S(1)}, u32[]{:S(2)}, u32[]{:S(2)}) collective-permute-start(bf16[128,1024]{0,1:T(8,128)(2,1)S(1)} %copy.118), channel_id=1, source_target_pairs={{0,8},{1,9},{2,10},{3,11},{4,12},{5,13},{6,14},{7,15},{8,16},{9,17... | collective-permute-start | bytes 786440 | tf_op jit(solution)/shard_map/ppermute | solution.py:26
  7.0 3.0 collective-permute-start.1
  10.0 5.6 %collective-permute-start.2 = (bf16[128,1024]{0,1:T(8,128)(2,1)S(1)}, bf16[128,1024]{0,1:T(8,128)(2,1)S(1)}, u32[]{:S(2)}, u32[]{:S(2)}) collective-permute-start(bf16[128,1024]{0,1:T(8,128)(2,1)S(1)} %copy.118), channel_id=1, source_target_pairs={{0,6},{1,7},{2,8},{3,9},{4,10},{5,11},{6,12},{7,13},{8,14},{9,15},... | collective-permute-start | bytes 786440 | tf_op jit(solution)/shard_map/ppermute | solution.py:26
  15.6 2.3 collective-permute-start.3
  17.9 3.7 collective-permute-start.4
  27.9 3.2 collective-permute-start.6
  31.9 10.7 %collective-permute-done.2 = bf16[128,1024]{0,1:T(8,128)(2,1)S(1)} collective-permute-done((bf16[128,1024]{0,1:T(8,128)(2,1)S(1)}, bf16[128,1024]{0,1:T(8,128)(2,1)S(1)}, u32[]{:S(2)}, u32[]{:S(2)}) %collective-permute-start.2) | collective-permute-done | bytes 262176 | tf_op jit(solution)/shard_map/ppermute | solution.py:26
  48.3 2.0 collective-permute-done.7
  51.8 2.4 broadcast.43.clone.1
  54.2 18.9 %while.28 = (s32[]{:T(128)}, f32[1152,1024]{0,1:T(8,128)}, bf16[128,2048]{1,0:T(8,128)(2,1)}, bf16[1152,1024]{0,1:T(8,128)(2,1)}, bf16[128,2048]{1,0:T(8,128)(2,...) while((s32[]{:T(128)}, f32[1152,1024]{0,1:T(8,128)}, ...), condition=%wide.region_3.4_spmd.clone, body=%wide.region_0.3_spmd.clone.sunk | while | flops 459033344 | bytes 7793005 | solution.py:90
  60.4 2.2 fusion.83
  69.8 2.2 fusion.83
  73.2 2.6 convert.20
  75.9 4.8 %collective-permute-start.10 = (bf16[128,512]{0,1:T(8,128)(2,1)S(1)}, bf16[128,512]{0,1:T(8,128)(2,1)S(1)}, u32[]{:S(2)}, u32[]{:S(2)}) collective-permute-start(bf16[128,512]{0,1:T(8,128)(2,1)S(1)} %get-tuple-element.408), channel_id=1, source_target_pairs={{3,0},{4,1},{5,2},{6,3},{7,4},{8,5},{9,6},{10,7},{11,8},{12,9},{13... | collective-permute-start | bytes 393224 | tf_op jit(solution)/shard_map/ppermute | solution.py:26
  80.8 2.8 collective-permute-start.11
  83.6 1.9 collective-permute-start.12
  85.5 4.7 %collective-permute-start.13 = (bf16[128,512]{0,1:T(8,128)(2,1)S(1)}, bf16[128,512]{0,1:T(8,128)(2,1)S(1)}, u32[]{:S(2)}, u32[]{:S(2)}) collective-permute-start(bf16[128,512]{0,1:T(8,128)(2,1)S(1)} %get-tuple-element.405), channel_id=1, source_target_pairs={{6,0},{7,1},{8,2},{9,3},{10,4},{11,5},{12,6},{13,7},{14,8},{15,9},... | collective-permute-start | bytes 393224 | tf_op jit(solution)/shard_map/ppermute | solution.py:26
  90.2 1.9 collective-permute-start.14
  92.2 1.9 collective-permute-start.15
  94.1 1.9 collective-permute-start.8
  99.0 2.7 collective-permute-done.15
  101.7 7.1 %collective-permute-done.9 = bf16[128,512]{0,1:T(8,128)(2,1)S(1)} collective-permute-done((bf16[128,512]{0,1:T(8,128)(2,1)S(1)}, bf16[128,512]{0,1:T(8,128)(2,1)S(1)}, u32[]{:S(2)}, u32[]{:S(2)}) %collective-permute-start.9) | collective-permute-done | bytes 131104 | tf_op jit(solution)/shard_map/ppermute | solution.py:26
  111.5 6.9 %all-to-all-start = ((bf16[16,128,512]{2,1,0:T(8,128)(2,1)}), bf16[16,128,512]{2,1,0:T(8,128)(2,1)}, u32[]{:S(2)}, u32[]{:S(2)}) async-start(bf16[16,128,512]{2,1,0:T(8,128)(2,1)} %broadcast_in_dim.67), calls=%async_computation | async-start | bytes 4194304 | tf_op jit(solution)/shard_map/all_to_all | solution.py:110
  118.5 2.4 broadcast.43.clone
  120.9 19.0 %while.29 = (s32[]{:T(128)}, f32[1152,1024]{0,1:T(8,128)}, bf16[128,2048]{1,0:T(8,128)(2,1)}, bf16[1152,1024]{0,1:T(8,128)(2,1)}, bf16[128,2048]{1,0:T(8,128)(2,...) while((s32[]{:T(128)}, f32[1152,1024]{0,1:T(8,128)}, ...), condition=%wide.region_7.8_spmd.clone, body=%wide.region_4.7_spmd.clone.sunk | while | flops 459033344 | bytes 7793025 | solution.py:90
  127.1 2.2 fusion.91
  136.6 2.2 fusion.91
  139.9 2.6 convert.21
  142.7 2.0 collective-permute-start.16
  144.7 2.2 collective-permute-start.17
  146.9 2.6 collective-permute-start.18
  149.5 3.6 collective-permute-start.19
  153.1 2.5 collective-permute-start.20
  155.6 2.6 collective-permute-start.21
  162.1 5.9 %collective-permute-done.21 = bf16[128,512]{0,1:T(8,128)(2,1)S(1)} collective-permute-done((bf16[128,512]{0,1:T(8,128)(2,1)S(1)}, bf16[128,512]{0,1:T(8,128)(2,1)S(1)}, u32[]{:S(2)}, u32[]{:S(2)}) %collective-permute-start.21) | collective-permute-done | bytes 131104 | tf_op jit(solution)/shard_map/ppermute | solution.py:26
  168.1 3.0 collective-permute-done.23
  173.8 10.2 %all-to-all-start.1 = ((bf16[16,128,512]{2,1,0:T(8,128)(2,1)}), bf16[16,128,512]{2,1,0:T(8,128)(2,1)}, u32[]{:S(2)}, u32[]{:S(2)}) async-start(bf16[16,128,512]{2,1,0:T(8,128)(2,1)} %broadcast_in_dim.68), calls=%async_computation.1 | async-start | bytes 4194304 | tf_op jit(solution)/shard_map/all_to_all | solution.py:110
  184.3 2.9 convolution_bitcast_fusion.1
  187.2 23.4 %all-to-all-done.1 = bf16[16,128,512]{2,1,0:T(8,128)(2,1)} async-done(((bf16[16,128,512]{2,1,0:T(8,128)(2,1)}), bf16[16,128,512]{2,1,0:T(8,128)(2,1)}, u32[]{:S(2)}, u32[]{:S(2)}) %all-to-all-start.1) | async-done | bytes 2097184 | tf_op jit(solution)/shard_map/all_to_all | solution.py:110
  210.6 2.9 convolution_bitcast_fusion
  215.4 2.4 psum.21
  217.9 4.9 %psum.22 = f32[1024]{0:T(1024)S(1)} all-reduce(f32[1024]{0:T(1024)S(1)} %psum.21), channel_id=1, replica_groups=mesh['z'=16,'xh'=2,'y'=4,'xl'=2,'c'=2] {'xl'}, use_global_device_ids=true, to_apply=%region_10.11 | all-reduce | flops 1024 | bytes 8192 | tf_op jit(solution)/shard_map/psum | solution.py:121
  223.1 20.1 %psum.23 = f32[1,32,32]{0,2,1:T(8,128)S(1)} all-reduce(f32[1,32,32]{0,2,1:T(8,128)S(1)} %concatenate.23), channel_id=1, replica_groups=mesh['z'=16,'xh'=2,'y'=4,'xl'=2,'c'=2] {'y'}, use_global_device_ids=true, to_apply=%region_11.12 | all-reduce | flops 1024 | bytes 8192 | tf_op jit(solution)/shard_map/psum | solution.py:121
  243.2 2.8 pad_maximum_fusion.1
  246.1 25.7 %all-to-all-start.2 = ((f32[337,32,32]{0,2,1:T(8,128)}), f32[337,32,32]{0,2,1:T(8,128)}, u32[]{:S(2)}, u32[]{:S(2)}) async-start(f32[337,32,32]{0,2,1:T(8,128)} %pad_maximum_fusion.1), calls=%async_computation.2 | async-start | bytes 3145728 | tf_op jit(solution)/shard_map/all_to_all | solution.py:125
  272.1 72.3 %all-to-all-done.2 = f32[337,32,32]{0,2,1:T(8,128)} async-done(((f32[337,32,32]{0,2,1:T(8,128)}), f32[337,32,32]{0,2,1:T(8,128)}, u32[]{:S(2)}, u32[]{:S(2)}) %all-to-all-start.2) | async-done | bytes 1380384 | tf_op jit(solution)/shard_map/all_to_all | solution.py:125
  346.4 6.0 %all_gather.6 = bf16[338,64]{0,1:T(8,128)(2,1)S(1)} all-gather(bf16[338,32]{0,1:T(8,128)(2,1)S(1)} %pad_maximum_fusion.2), channel_id=1, replica_groups=mesh['z'=16,'xh'=2,'y'=4,'xl'=2,'c'=2] {'xh'}, dimensions={1}, use_global_device_ids=true | all-gather | bytes 64896 | tf_op jit(solution)/shard_map/all_gather | solution.py:134
  352.4 32.1 %all_gather.7 = bf16[338,1024]{0,1:T(8,128)(2,1)S(1)} all-gather(bf16[338,64]{0,1:T(8,128)(2,1)S(1)} %all_gather.6), channel_id=1, replica_groups=mesh['z'=16,'xh'=2,'y'=4,'xl'=2,'c'=2] {'z'}, dimensions={1}, use_global_device_ids=true | all-gather | bytes 735488 | tf_op jit(solution)/shard_map/all_gather | solution.py:135
  (94 shorter events, 63.9 us)
Async XLA Ops:
  0.6 183.7 %copy-start = (bf16[336,2048]{1,0:T(8,128)(2,1)S(1)}, bf16[336,2048]{1,0:T(8,128)(2,1)}, u32[]{:S(2)}) copy-start(bf16[336,2048]{1,0:T(8,128)(2,1)} %param.10) | copy-start | bytes 4128772
  1.9 23.3 %collective-permute-start = (bf16[128,1024]{0,1:T(8,128)(2,1)S(1)}, bf16[128,1024]{0,1:T(8,128)(2,1)S(1)}, u32[]{:S(2)}, u32[]{:S(2)}) collective-permute-start(bf16[128,1024]{0,1:T(8,128)(2,1)S(1)} %copy.118), channel_id=1, source_target_pairs={{0,8},{1,9},{2,10},{3,11},{4,12},{5,13},{6,14},{7,15},{8,16},{9,17... | collective-permute-start | bytes 786440 | tf_op jit(solution)/shard_map/ppermute | solution.py:26
  7.0 20.9 %collective-permute-start.1 = (bf16[128,1024]{0,1:T(8,128)(2,1)S(1)}, bf16[128,1024]{0,1:T(8,128)(2,1)S(1)}, u32[]{:S(2)}, u32[]{:S(2)}) collective-permute-start(bf16[128,1024]{0,1:T(8,128)(2,1)S(1)} %copy.118), channel_id=1, source_target_pairs={{0,7},{1,8},{2,9},{3,10},{4,11},{5,12},{6,13},{7,14},{8,15},{9,16}... | collective-permute-start | bytes 786440 | tf_op jit(solution)/shard_map/ppermute | solution.py:26
  10.0 32.6 %collective-permute-start.2 = (bf16[128,1024]{0,1:T(8,128)(2,1)S(1)}, bf16[128,1024]{0,1:T(8,128)(2,1)S(1)}, u32[]{:S(2)}, u32[]{:S(2)}) collective-permute-start(bf16[128,1024]{0,1:T(8,128)(2,1)S(1)} %copy.118), channel_id=1, source_target_pairs={{0,6},{1,7},{2,8},{3,9},{4,10},{5,11},{6,12},{7,13},{8,14},{9,15},... | collective-permute-start | bytes 786440 | tf_op jit(solution)/shard_map/ppermute | solution.py:26
  15.6 29.7 %collective-permute-start.3 = (bf16[128,1024]{0,1:T(8,128)(2,1)S(1)}, bf16[128,1024]{0,1:T(8,128)(2,1)S(1)}, u32[]{:S(2)}, u32[]{:S(2)}) collective-permute-start(bf16[128,1024]{0,1:T(8,128)(2,1)S(1)} %copy.118), channel_id=1, source_target_pairs={{0,5},{1,6},{2,7},{3,8},{4,9},{5,10},{6,11},{7,12},{8,13},{9,14},{... | collective-permute-start | bytes 786440 | tf_op jit(solution)/shard_map/ppermute | solution.py:26
  17.9 28.1 %collective-permute-start.4 = (bf16[128,1024]{0,1:T(8,128)(2,1)S(1)}, bf16[128,1024]{0,1:T(8,128)(2,1)S(1)}, u32[]{:S(2)}, u32[]{:S(2)}) collective-permute-start(bf16[128,1024]{0,1:T(8,128)(2,1)S(1)} %copy.118), channel_id=1, source_target_pairs={{0,4},{1,5},{2,6},{3,7},{4,8},{5,9},{6,10},{7,11},{8,12},{9,13},{1... | collective-permute-start | bytes 786440 | tf_op jit(solution)/shard_map/ppermute | solution.py:26
  25.2 21.6 %collective-permute-start.5 = (bf16[128,1024]{0,1:T(8,128)(2,1)S(1)}, bf16[128,1024]{0,1:T(8,128)(2,1)S(1)}, u32[]{:S(2)}, u32[]{:S(2)}) collective-permute-start(bf16[128,1024]{0,1:T(8,128)(2,1)S(1)} %copy.118), channel_id=1, source_target_pairs={{0,3},{1,4},{2,5},{3,6},{4,7},{5,8},{6,9},{7,10},{8,11},{9,12},{10... | collective-permute-start | bytes 786440 | tf_op jit(solution)/shard_map/ppermute | solution.py:26
  27.9 19.7 %collective-permute-start.6 = (bf16[128,1024]{0,1:T(8,128)(2,1)S(1)}, bf16[128,1024]{0,1:T(8,128)(2,1)S(1)}, u32[]{:S(2)}, u32[]{:S(2)}) collective-permute-start(bf16[128,1024]{0,1:T(8,128)(2,1)S(1)} %copy.118), channel_id=1, source_target_pairs={{0,2},{1,3},{2,4},{3,5},{4,6},{5,7},{6,8},{7,9},{8,10},{9,11},{10,... | collective-permute-start | bytes 786440 | tf_op jit(solution)/shard_map/ppermute | solution.py:26
  42.6 7.7 %collective-permute-start.7 = (bf16[128,1024]{0,1:T(8,128)(2,1)S(1)}, bf16[128,1024]{0,1:T(8,128)(2,1)S(1)}, u32[]{:S(2)}, u32[]{:S(2)}) collective-permute-start(bf16[128,1024]{0,1:T(8,128)(2,1)S(1)} %copy.118), channel_id=1, source_target_pairs={{0,1},{1,2},{2,3},{3,4},{4,5},{5,6},{6,7},{7,8},{8,9},{9,10},{10,1... | collective-permute-start | bytes 786440 | tf_op jit(solution)/shard_map/ppermute | solution.py:26
  75.9 16.2 %collective-permute-start.10 = (bf16[128,512]{0,1:T(8,128)(2,1)S(1)}, bf16[128,512]{0,1:T(8,128)(2,1)S(1)}, u32[]{:S(2)}, u32[]{:S(2)}) collective-permute-start(bf16[128,512]{0,1:T(8,128)(2,1)S(1)} %get-tuple-element.408), channel_id=1, source_target_pairs={{3,0},{4,1},{5,2},{6,3},{7,4},{8,5},{9,6},{10,7},{11,8},{12,9},{13... | collective-permute-start | bytes 393224 | tf_op jit(solution)/shard_map/ppermute | solution.py:26
  80.8 13.3 %collective-permute-start.11 = (bf16[128,512]{0,1:T(8,128)(2,1)S(1)}, bf16[128,512]{0,1:T(8,128)(2,1)S(1)}, u32[]{:S(2)}, u32[]{:S(2)}) collective-permute-start(bf16[128,512]{0,1:T(8,128)(2,1)S(1)} %get-tuple-element.407), channel_id=1, source_target_pairs={{4,0},{5,1},{6,2},{7,3},{8,4},{9,5},{10,6},{11,7},{12,8},{13,9},{1... | collective-permute-start | bytes 393224 | tf_op jit(solution)/shard_map/ppermute | solution.py:26
  83.6 12.4 %collective-permute-start.12 = (bf16[128,512]{0,1:T(8,128)(2,1)S(1)}, bf16[128,512]{0,1:T(8,128)(2,1)S(1)}, u32[]{:S(2)}, u32[]{:S(2)}) collective-permute-start(bf16[128,512]{0,1:T(8,128)(2,1)S(1)} %get-tuple-element.406), channel_id=1, source_target_pairs={{5,0},{6,1},{7,2},{8,3},{9,4},{10,5},{11,6},{12,7},{13,8},{14,9},{... | collective-permute-start | bytes 393224 | tf_op jit(solution)/shard_map/ppermute | solution.py:26
  85.5 12.5 %collective-permute-start.13 = (bf16[128,512]{0,1:T(8,128)(2,1)S(1)}, bf16[128,512]{0,1:T(8,128)(2,1)S(1)}, u32[]{:S(2)}, u32[]{:S(2)}) collective-permute-start(bf16[128,512]{0,1:T(8,128)(2,1)S(1)} %get-tuple-element.405), channel_id=1, source_target_pairs={{6,0},{7,1},{8,2},{9,3},{10,4},{11,5},{12,6},{13,7},{14,8},{15,9},... | collective-permute-start | bytes 393224 | tf_op jit(solution)/shard_map/ppermute | solution.py:26
  90.2 8.8 %collective-permute-start.14 = (bf16[128,512]{0,1:T(8,128)(2,1)S(1)}, bf16[128,512]{0,1:T(8,128)(2,1)S(1)}, u32[]{:S(2)}, u32[]{:S(2)}) collective-permute-start(bf16[128,512]{0,1:T(8,128)(2,1)S(1)} %get-tuple-element.404), channel_id=1, source_target_pairs={{7,0},{8,1},{9,2},{10,3},{11,4},{12,5},{13,6},{14,7},{15,8},{16,9}... | collective-permute-start | bytes 393224 | tf_op jit(solution)/shard_map/ppermute | solution.py:26
  92.2 9.6 %collective-permute-start.15 = (bf16[128,512]{0,1:T(8,128)(2,1)S(1)}, bf16[128,512]{0,1:T(8,128)(2,1)S(1)}, u32[]{:S(2)}, u32[]{:S(2)}) collective-permute-start(bf16[128,512]{0,1:T(8,128)(2,1)S(1)} %get-tuple-element.403), channel_id=1, source_target_pairs={{8,0},{9,1},{10,2},{11,3},{12,4},{13,5},{14,6},{15,7},{16,8},{17,9... | collective-permute-start | bytes 393224 | tf_op jit(solution)/shard_map/ppermute | solution.py:26
  94.1 7.6 %collective-permute-start.8 = (bf16[128,512]{0,1:T(8,128)(2,1)S(1)}, bf16[128,512]{0,1:T(8,128)(2,1)S(1)}, u32[]{:S(2)}, u32[]{:S(2)}) collective-permute-start(bf16[128,512]{0,1:T(8,128)(2,1)S(1)} %get-tuple-element.402), channel_id=1, source_target_pairs={{1,0},{2,1},{3,2},{4,3},{5,4},{6,5},{7,6},{8,7},{9,8},{10,9},{11,1... | collective-permute-start | bytes 393224 | tf_op jit(solution)/shard_map/ppermute | solution.py:26
  96.0 12.7 %collective-permute-start.9 = (bf16[128,512]{0,1:T(8,128)(2,1)S(1)}, bf16[128,512]{0,1:T(8,128)(2,1)S(1)}, u32[]{:S(2)}, u32[]{:S(2)}) collective-permute-start(bf16[128,512]{0,1:T(8,128)(2,1)S(1)} %get-tuple-element.409), channel_id=1, source_target_pairs={{2,0},{3,1},{4,2},{5,3},{6,4},{7,5},{8,6},{9,7},{10,8},{11,9},{12,... | collective-permute-start | bytes 393224 | tf_op jit(solution)/shard_map/ppermute | solution.py:26
  111.5 60.7 %all-to-all-start = ((bf16[16,128,512]{2,1,0:T(8,128)(2,1)}), bf16[16,128,512]{2,1,0:T(8,128)(2,1)}, u32[]{:S(2)}, u32[]{:S(2)}) async-start(bf16[16,128,512]{2,1,0:T(8,128)(2,1)} %broadcast_in_dim.67), calls=%async_computation | async-start | bytes 4194304 | tf_op jit(solution)/shard_map/all_to_all | solution.py:110
  142.7 12.9 %collective-permute-start.16 = (bf16[128,512]{0,1:T(8,128)(2,1)S(1)}, bf16[128,512]{0,1:T(8,128)(2,1)S(1)}, u32[]{:S(2)}, u32[]{:S(2)}) collective-permute-start(bf16[128,512]{0,1:T(8,128)(2,1)S(1)} %get-tuple-element.410), channel_id=1, source_target_pairs={{1,0},{2,1},{3,2},{4,3},{5,4},{6,5},{7,6},{8,7},{9,8},{10,9},{11,1... | collective-permute-start | bytes 393224 | tf_op jit(solution)/shard_map/ppermute | solution.py:26
  144.7 13.5 %collective-permute-start.17 = (bf16[128,512]{0,1:T(8,128)(2,1)S(1)}, bf16[128,512]{0,1:T(8,128)(2,1)S(1)}, u32[]{:S(2)}, u32[]{:S(2)}) collective-permute-start(bf16[128,512]{0,1:T(8,128)(2,1)S(1)} %get-tuple-element.417), channel_id=1, source_target_pairs={{2,0},{3,1},{4,2},{5,3},{6,4},{7,5},{8,6},{9,7},{10,8},{11,9},{12,... | collective-permute-start | bytes 393224 | tf_op jit(solution)/shard_map/ppermute | solution.py:26
  146.9 13.3 %collective-permute-start.18 = (bf16[128,512]{0,1:T(8,128)(2,1)S(1)}, bf16[128,512]{0,1:T(8,128)(2,1)S(1)}, u32[]{:S(2)}, u32[]{:S(2)}) collective-permute-start(bf16[128,512]{0,1:T(8,128)(2,1)S(1)} %get-tuple-element.416), channel_id=1, source_target_pairs={{3,0},{4,1},{5,2},{6,3},{7,4},{8,5},{9,6},{10,7},{11,8},{12,9},{13... | collective-permute-start | bytes 393224 | tf_op jit(solution)/shard_map/ppermute | solution.py:26
  149.5 12.6 %collective-permute-start.19 = (bf16[128,512]{0,1:T(8,128)(2,1)S(1)}, bf16[128,512]{0,1:T(8,128)(2,1)S(1)}, u32[]{:S(2)}, u32[]{:S(2)}) collective-permute-start(bf16[128,512]{0,1:T(8,128)(2,1)S(1)} %get-tuple-element.415), channel_id=1, source_target_pairs={{4,0},{5,1},{6,2},{7,3},{8,4},{9,5},{10,6},{11,7},{12,8},{13,9},{1... | collective-permute-start | bytes 393224 | tf_op jit(solution)/shard_map/ppermute | solution.py:26
  153.1 9.0 %collective-permute-start.20 = (bf16[128,512]{0,1:T(8,128)(2,1)S(1)}, bf16[128,512]{0,1:T(8,128)(2,1)S(1)}, u32[]{:S(2)}, u32[]{:S(2)}) collective-permute-start(bf16[128,512]{0,1:T(8,128)(2,1)S(1)} %get-tuple-element.414), channel_id=1, source_target_pairs={{5,0},{6,1},{7,2},{8,3},{9,4},{10,5},{11,6},{12,7},{13,8},{14,9},{... | collective-permute-start | bytes 393224 | tf_op jit(solution)/shard_map/ppermute | solution.py:26
  155.6 12.5 %collective-permute-start.21 = (bf16[128,512]{0,1:T(8,128)(2,1)S(1)}, bf16[128,512]{0,1:T(8,128)(2,1)S(1)}, u32[]{:S(2)}, u32[]{:S(2)}) collective-permute-start(bf16[128,512]{0,1:T(8,128)(2,1)S(1)} %get-tuple-element.413), channel_id=1, source_target_pairs={{6,0},{7,1},{8,2},{9,3},{10,4},{11,5},{12,6},{13,7},{14,8},{15,9},... | collective-permute-start | bytes 393224 | tf_op jit(solution)/shard_map/ppermute | solution.py:26
  158.2 9.8 %collective-permute-start.22 = (bf16[128,512]{0,1:T(8,128)(2,1)S(1)}, bf16[128,512]{0,1:T(8,128)(2,1)S(1)}, u32[]{:S(2)}, u32[]{:S(2)}) collective-permute-start(bf16[128,512]{0,1:T(8,128)(2,1)S(1)} %get-tuple-element.412), channel_id=1, source_target_pairs={{7,0},{8,1},{9,2},{10,3},{11,4},{12,5},{13,6},{14,7},{15,8},{16,9}... | collective-permute-start | bytes 393224 | tf_op jit(solution)/shard_map/ppermute | solution.py:26
  160.2 10.8 %collective-permute-start.23 = (bf16[128,512]{0,1:T(8,128)(2,1)S(1)}, bf16[128,512]{0,1:T(8,128)(2,1)S(1)}, u32[]{:S(2)}, u32[]{:S(2)}) collective-permute-start(bf16[128,512]{0,1:T(8,128)(2,1)S(1)} %get-tuple-element.411), channel_id=1, source_target_pairs={{8,0},{9,1},{10,2},{11,3},{12,4},{13,5},{14,6},{15,7},{16,8},{17,9... | collective-permute-start | bytes 393224 | tf_op jit(solution)/shard_map/ppermute | solution.py:26
  173.8 10.2 %copy-start.1 = (bf16[336,1024]{1,0:T(8,128)(2,1)S(1)}, bf16[336,1024]{1,0:T(8,128)(2,1)}, u32[]{:S(2)}) copy-start(bf16[336,1024]{1,0:T(8,128)(2,1)} %param.11) | copy-start | bytes 2064388
  173.8 36.9 %all-to-all-start.1 = ((bf16[16,128,512]{2,1,0:T(8,128)(2,1)}), bf16[16,128,512]{2,1,0:T(8,128)(2,1)}, u32[]{:S(2)}, u32[]{:S(2)}) async-start(bf16[16,128,512]{2,1,0:T(8,128)(2,1)} %broadcast_in_dim.68), calls=%async_computation.1 | async-start | bytes 4194304 | tf_op jit(solution)/shard_map/all_to_all | solution.py:110
  210.6 2.9 copy-start.2
  246.1 98.3 %all-to-all-start.2 = ((f32[337,32,32]{0,2,1:T(8,128)}), f32[337,32,32]{0,2,1:T(8,128)}, u32[]{:S(2)}, u32[]{:S(2)}) async-start(f32[337,32,32]{0,2,1:T(8,128)} %pad_maximum_fusion.1), calls=%async_computation.2 | async-start | bytes 3145728 | tf_op jit(solution)/shard_map/all_to_all | solution.py:125

commit v5 on v1

--- a/solution.py
+++ b/solution.py
@@ -84,8 +84,8 @@
 
         own_grad = block_at(0)
         for distance in range(1, hop_count + 1):
-            sent = passed_along(block_at(distance), ALL, n_all, -distance)
-            own_grad = own_grad + sent
+            sent = passed_along(block_at(distance).astype(jnp.bfloat16), ALL, n_all, -distance)
+            own_grad = own_grad + sent.astype(jnp.float32)
         value_grad = own_grad.astype(jnp.bfloat16)
 
         spread = jnp.broadcast_to(value_grad[None], (n_fsdp,) + value_grad.shape)
@@ -99,13 +99,15 @@
         signed = jnp.where(kept_mask, jnp.sign(weight_full), 0.0)
 
         logit_part = jnp.sum(local_grad * signed, axis=0)
-        logit_sum = lax.psum(logit_part, ALL)
-        grad_logit = -logit_sum * threshold * (1.0 - threshold)
 
         rows, cols = local_grad.shape
         piece = cols // n_seq
         pieces = local_grad.reshape(rows, n_seq, piece)
         received = lax.all_to_all(pieces, SEQ, 1, 1, tiled=True)
+        for axis in reversed(ALL):
+            logit_part = lax.psum(logit_part, axis)
+        grad_logit = -logit_part * threshold * (1.0 - threshold)
+
         dense_piece = jnp.sum(received, axis=1)
         seq_index = lax.axis_index(SEQ)
         kept_piece = lax.dynamic_slice_in_dim(kept_mask, seq_index * piece, piece, 1)

time: 467 us -> 364 us (0.78)
  blocking collectives: 177 us -> 129 us
  waiting for transfers between devices: 131 us -> 93.7 us
  starting transfers between devices: 92.4 us -> 74.9 us
    psum x1 -> x5, blocking collectives: 138 us -> 91.8 us  [local(): logit_part = lax.psum(logit_part, axis)]
    ppermute x16, waiting for transfers between devices: 82.4 us -> 44.9 us  [passed_along(): lax.ppermute(value, axis, [(source, source + steps) for source in range(f...]
    all_to_all x1, starting transfers between devices: 21.6 us -> 8.75 us  [local(): lax.all_to_all(spread, FSDP, 0, 0, tiled=True)]
  transfers between devices with their start and end apart: 18 -> 18, of which waited for: 10 -> 8; matrix products, arithmetic and copies ran while one was open for 2% -> 2% of each run, Pallas kernels for 0% -> 0%
where the time goes in v5:
time: 364 us; the launch traced here: 363 us
  blocking collectives  129 us (35%)
  waiting for transfers between devices  93.7 us (26%)
  starting transfers between devices  74.9 us (21%)
  local copies, waits for them, and re-layouts  28.9 us (8%)
  matrix products  20.6 us (6%)
  other arithmetic  13.8 us (4%)
    psum x5, blocking collectives, local(): logit_part = lax.psum(logit_part, axis)  91.8 us
    all_to_all x1, waiting for transfers between devices, local(): lax.all_to_all(spread, FSDP, 0, 0, tiled=True)  48.8 us
    ppermute x16, starting transfers between devices, passed_along(): lax.ppermute(value, axis, [(source, source + steps) for source in range(f...  47.6 us
    ppermute x16, waiting for transfers between devices, passed_along(): lax.ppermute(value, axis, [(source, source + steps) for source in range(f...  44.9 us
    all_gather x1, blocking collectives, local(): grad_weight = lax.all_gather(weight_piece, 'z', axis=1, tiled=True)  31.6 us
    all_to_all x1, starting transfers between devices, local(): received = lax.all_to_all(pieces, SEQ, 1, 1, tiled=True)  18.6 us
    unnamed x19, local copies, waits for them, and re-layouts  8.79 us
    all_to_all x1, starting transfers between devices, local(): lax.all_to_all(spread, FSDP, 0, 0, tiled=True)  8.75 us
  transfers between devices with their start and end apart: 18, of which 8 were waited for; matrix products, arithmetic and copies ran while one was open for 2% of the time, Pallas kernels for 0%

profile of v5, /device:TPU:6, one launch (start us, length us, event | category | flops | bytes accessed | tf_op | source)
XLA Modules:
  0.0 362.6 jit_solution(4671796324730566197)
XLA Ops:
  1.9 5.1 %collective-permute-start = (bf16[128,1024]{0,1:T(8,128)(2,1)S(1)}, bf16[128,1024]{0,1:T(8,128)(2,1)S(1)}, u32[]{:S(2)}, u32[]{:S(2)}) collective-permute-start(bf16[128,1024]{0,1:T(8,128)(2,1)S(1)} %copy.50), channel_id=1, source_target_pairs={{0,8},{1,9},{2,10},{3,11},{4,12},{5,13},{6,14},{7,15},{8,16},{9,17... | collective-permute-start | bytes 786440 | tf_op jit(solution)/shard_map/ppermute | solution.py:26
  7.0 3.0 collective-permute-start.1
  10.0 5.6 %collective-permute-start.2 = (bf16[128,1024]{0,1:T(8,128)(2,1)S(1)}, bf16[128,1024]{0,1:T(8,128)(2,1)S(1)}, u32[]{:S(2)}, u32[]{:S(2)}) collective-permute-start(bf16[128,1024]{0,1:T(8,128)(2,1)S(1)} %copy.50), channel_id=1, source_target_pairs={{0,6},{1,7},{2,8},{3,9},{4,10},{5,11},{6,12},{7,13},{8,14},{9,15},... | collective-permute-start | bytes 786440 | tf_op jit(solution)/shard_map/ppermute | solution.py:26
  15.6 2.3 collective-permute-start.3
  17.9 3.7 %collective-permute-start.4 = (bf16[128,1024]{0,1:T(8,128)(2,1)S(1)}, bf16[128,1024]{0,1:T(8,128)(2,1)S(1)}, u32[]{:S(2)}, u32[]{:S(2)}) collective-permute-start(bf16[128,1024]{0,1:T(8,128)(2,1)S(1)} %copy.50), channel_id=1, source_target_pairs={{0,4},{1,5},{2,6},{3,7},{4,8},{5,9},{6,10},{7,11},{8,12},{9,13},{1... | collective-permute-start | bytes 786440 | tf_op jit(solution)/shard_map/ppermute | solution.py:26
  22.3 2.9 collective-permute-done
  25.2 1.9 collective-permute-start.5
  27.8 2.1 collective-permute-start.6
  30.7 11.9 %collective-permute-done.2 = bf16[128,1024]{0,1:T(8,128)(2,1)S(1)} collective-permute-done((bf16[128,1024]{0,1:T(8,128)(2,1)S(1)}, bf16[128,1024]{0,1:T(8,128)(2,1)S(1)}, u32[]{:S(2)}, u32[]{:S(2)}) %collective-permute-start.2) | collective-permute-done | bytes 262176 | tf_op jit(solution)/shard_map/ppermute | solution.py:26
  42.6 1.9 collective-permute-start.7
  48.3 1.9 collective-permute-done.7
  51.8 2.4 broadcast_in_dim.43
  54.2 35.7 %while.14 = (s32[]{:T(128)}, f32[1152,1024]{0,1:T(8,128)}, bf16[128,2048]{1,0:T(8,128)(2,1)}, bf16[1152,1024]{0,1:T(8,128)(2,1)}, bf16[128,2048]{1,0:T(8,128)(2,...) while((s32[]{:T(128)}, f32[1152,1024]{0,1:T(8,128)}, ...), condition=%wide.region_3.4_spmd.clone, body=%wide.region_0.3_spmd.clone.sunk | while | flops 459033344 | bytes 7806429 | solution.py:76
  56.4 1.8 fusion.44
  58.2 1.6 fusion.45
  60.0 2.0 fusion.46
  65.4 1.8 fusion.44
  67.1 1.6 fusion.45
  68.9 2.0 fusion.46
  74.3 1.8 fusion.44
  76.1 1.6 fusion.45
  77.8 2.0 fusion.46
  83.2 1.8 fusion.44
  86.8 2.0 fusion.46
  89.9 2.6 convert.10
  92.9 4.8 %collective-permute-start.10 = (bf16[128,1024]{0,1:T(8,128)(2,1)S(1)}, bf16[128,1024]{0,1:T(8,128)(2,1)S(1)}, u32[]{:S(2)}, u32[]{:S(2)}) collective-permute-start(bf16[128,1024]{0,1:T(8,128)(2,1)S(1)} %get-tuple-element.193), channel_id=1, source_target_pairs={{3,0},{4,1},{5,2},{6,3},{7,4},{8,5},{9,6},{10,7},{11,8},{12,9},{13... | collective-permute-start | bytes 786440 | tf_op jit(solution)/shard_map/ppermute | solution.py:26
  97.7 2.8 collective-permute-start.11
  100.5 1.9 collective-permute-start.12
  102.4 4.8 %collective-permute-start.13 = (bf16[128,1024]{0,1:T(8,128)(2,1)S(1)}, bf16[128,1024]{0,1:T(8,128)(2,1)S(1)}, u32[]{:S(2)}, u32[]{:S(2)}) collective-permute-start(bf16[128,1024]{0,1:T(8,128)(2,1)S(1)} %get-tuple-element.190), channel_id=1, source_target_pairs={{6,0},{7,1},{8,2},{9,3},{10,4},{11,5},{12,6},{13,7},{14,8},{15,9},... | collective-permute-start | bytes 786440 | tf_op jit(solution)/shard_map/ppermute | solution.py:26
  107.2 1.9 collective-permute-start.14
  109.1 1.9 collective-permute-start.15
  111.7 1.9 collective-permute-start.8
  113.6 12.2 %collective-permute-done.12 = bf16[128,1024]{0,1:T(8,128)(2,1)S(1)} collective-permute-done((bf16[128,1024]{0,1:T(8,128)(2,1)S(1)}, bf16[128,1024]{0,1:T(8,128)(2,1)S(1)}, u32[]{:S(2)}, u32[]{:S(2)}) %collective-permute-start.12) | collective-permute-done | bytes 262176 | tf_op jit(solution)/shard_map/ppermute | solution.py:26
  125.8 1.9 collective-permute-start.9
  127.7 3.7 %collective-permute-done.13 = bf16[128,1024]{0,1:T(8,128)(2,1)S(1)} collective-permute-done((bf16[128,1024]{0,1:T(8,128)(2,1)S(1)}, bf16[128,1024]{0,1:T(8,128)(2,1)S(1)}, u32[]{:S(2)}, u32[]{:S(2)}) %collective-permute-start.13) | collective-permute-done | bytes 262176 | tf_op jit(solution)/shard_map/ppermute | solution.py:26
  131.4 11.7 %collective-permute-done.9 = bf16[128,1024]{0,1:T(8,128)(2,1)S(1)} collective-permute-done((bf16[128,1024]{0,1:T(8,128)(2,1)S(1)}, bf16[128,1024]{0,1:T(8,128)(2,1)S(1)}, u32[]{:S(2)}, u32[]{:S(2)}) %collective-permute-start.9) | collective-permute-done | bytes 262176 | tf_op jit(solution)/shard_map/ppermute | solution.py:26
  144.6 2.5 broadcast_in_dim.44
  147.1 8.8 %all-to-all-start = ((bf16[16,128,1024]{2,1,0:T(8,128)(2,1)}), bf16[16,128,1024]{2,1,0:T(8,128)(2,1)}, u32[]{:S(2)}, u32[]{:S(2)}) async-start(bf16[16,128,1024]{2,1,0:T(8,128)(2,1)} %broadcast_in_dim.44), calls=%async_computation | async-start | bytes 8388608 | tf_op jit(solution)/shard_map/all_to_all | solution.py:92
  156.2 48.8 %all-to-all-done = bf16[16,128,1024]{2,1,0:T(8,128)(2,1)} async-done(((bf16[16,128,1024]{2,1,0:T(8,128)(2,1)}), bf16[16,128,1024]{2,1,0:T(8,128)(2,1)}, u32[]{:S(2)}, u32[]{:S(2)}) %all-to-all-start) | async-done | bytes 4194336 | tf_op jit(solution)/shard_map/all_to_all | solution.py:92
  205.1 6.2 %fusion.21 = (f32[1024]{0:T(1024)S(1)}, f32[1024,336]{1,0:T(8,128)}) fusion(bf16[336,1024]{0,1:T(8,128)(2,1)S(1)} %copy.49, f32[1024]{0:T(1024)S(1)} %copy-done.5, bf16[2048,1024]{1,0:T(8,128)(2,1)} %bitcast, bf16[336,2048]{1,0:T(8,128)(2,1)S(1)} %copy-done), kind=kOutput, calls=%fused_computation.28 | convolution fusion | flops 1411693568 | bytes 7643136 | tf_op jit(solution)/shard_map/dot_general | solution.py:95
  211.2 18.6 %all-to-all-start.1 = ((f32[336,32,32]{0,2,1:T(8,128)}), f32[336,32,32]{0,2,1:T(8,128)S(1)}, u32[]{:S(2)}, u32[]{:S(2)}) async-start(f32[336,32,32]{0,2,1:T(8,128)} %bitcast.67), calls=%async_computation.1 | async-start | bytes 3145728 | tf_op jit(solution)/shard_map/all_to_all | solution.py:106
  231.3 2.5 psum.35
  233.8 5.1 %psum.36 = f32[1024]{0:T(1024)S(1)} all-reduce(f32[1024]{0:T(1024)S(1)} %psum.35), channel_id=1, replica_groups=mesh['z'=16,'xh'=2,'y'=4,'xl'=2,'c'=2] {'xl'}, use_global_device_ids=true, to_apply=%region_7.8 | all-reduce | flops 1024 | bytes 8192 | tf_op jit(solution)/shard_map/psum | solution.py:108
  238.8 8.3 %psum.37 = f32[1024]{0:T(1024)S(1)} all-reduce(f32[1024]{0:T(1024)S(1)} %psum.36), channel_id=1, replica_groups=mesh['z'=16,'xh'=2,'y'=4,'xl'=2,'c'=2] {'y'}, use_global_device_ids=true, to_apply=%region_8.9 | all-reduce | flops 1024 | bytes 8192 | tf_op jit(solution)/shard_map/psum | solution.py:108
  247.2 6.4 %psum.38 = f32[1024]{0:T(1024)S(1)} all-reduce(f32[1024]{0:T(1024)S(1)} %psum.37), channel_id=1, replica_groups=mesh['z'=16,'xh'=2,'y'=4,'xl'=2,'c'=2] {'xh'}, use_global_device_ids=true, to_apply=%region_9.10 | all-reduce | flops 1024 | bytes 8192 | tf_op jit(solution)/shard_map/psum | solution.py:108
  253.6 69.5 %psum.39 = f32[1024]{0:T(1024)S(1)} all-reduce(f32[1024]{0:T(1024)S(1)} %psum.38), channel_id=1, replica_groups=mesh['z'=16,'xh'=2,'y'=4,'xl'=2,'c'=2] {'z'}, use_global_device_ids=true, to_apply=%region_10.11 | all-reduce | flops 1024 | bytes 8192 | tf_op jit(solution)/shard_map/psum | solution.py:108
  323.8 6.0 %all_gather.6 = bf16[336,64]{0,1:T(8,128)(2,1)S(1)} all-gather(bf16[336,32]{0,1:T(8,128)(2,1)S(1)} %select_convert_fusion), channel_id=1, replica_groups=mesh['z'=16,'xh'=2,'y'=4,'xl'=2,'c'=2] {'xh'}, dimensions={1}, use_global_device_ids=true | all-gather | bytes 64512 | tf_op jit(solution)/shard_map/all_gather | solution.py:115
  329.8 31.6 %all_gather.7 = bf16[336,1024]{0,1:T(8,128)(2,1)S(1)} all-gather(bf16[336,64]{0,1:T(8,128)(2,1)S(1)} %all_gather.6), channel_id=1, replica_groups=mesh['z'=16,'xh'=2,'y'=4,'xl'=2,'c'=2] {'z'}, dimensions={1}, use_global_device_ids=true | all-gather | bytes 731136 | tf_op jit(solution)/shard_map/all_gather | solution.py:116
  (94 shorter events, 30.4 us)
Async XLA Ops:
  0.6 204.4 %copy-start = (bf16[336,2048]{1,0:T(8,128)(2,1)S(1)}, bf16[336,2048]{1,0:T(8,128)(2,1)}, u32[]{:S(2)}) copy-start(bf16[336,2048]{1,0:T(8,128)(2,1)} %param.8) | copy-start | bytes 4128772
  1.9 23.3 %collective-permute-start = (bf16[128,1024]{0,1:T(8,128)(2,1)S(1)}, bf16[128,1024]{0,1:T(8,128)(2,1)S(1)}, u32[]{:S(2)}, u32[]{:S(2)}) collective-permute-start(bf16[128,1024]{0,1:T(8,128)(2,1)S(1)} %copy.50), channel_id=1, source_target_pairs={{0,8},{1,9},{2,10},{3,11},{4,12},{5,13},{6,14},{7,15},{8,16},{9,17... | collective-permute-start | bytes 786440 | tf_op jit(solution)/shard_map/ppermute | solution.py:26
  7.0 20.9 %collective-permute-start.1 = (bf16[128,1024]{0,1:T(8,128)(2,1)S(1)}, bf16[128,1024]{0,1:T(8,128)(2,1)S(1)}, u32[]{:S(2)}, u32[]{:S(2)}) collective-permute-start(bf16[128,1024]{0,1:T(8,128)(2,1)S(1)} %copy.50), channel_id=1, source_target_pairs={{0,7},{1,8},{2,9},{3,10},{4,11},{5,12},{6,13},{7,14},{8,15},{9,16}... | collective-permute-start | bytes 786440 | tf_op jit(solution)/shard_map/ppermute | solution.py:26
  10.0 32.6 %collective-permute-start.2 = (bf16[128,1024]{0,1:T(8,128)(2,1)S(1)}, bf16[128,1024]{0,1:T(8,128)(2,1)S(1)}, u32[]{:S(2)}, u32[]{:S(2)}) collective-permute-start(bf16[128,1024]{0,1:T(8,128)(2,1)S(1)} %copy.50), channel_id=1, source_target_pairs={{0,6},{1,7},{2,8},{3,9},{4,10},{5,11},{6,12},{7,13},{8,14},{9,15},... | collective-permute-start | bytes 786440 | tf_op jit(solution)/shard_map/ppermute | solution.py:26
  15.6 29.6 %collective-permute-start.3 = (bf16[128,1024]{0,1:T(8,128)(2,1)S(1)}, bf16[128,1024]{0,1:T(8,128)(2,1)S(1)}, u32[]{:S(2)}, u32[]{:S(2)}) collective-permute-start(bf16[128,1024]{0,1:T(8,128)(2,1)S(1)} %copy.50), channel_id=1, source_target_pairs={{0,5},{1,6},{2,7},{3,8},{4,9},{5,10},{6,11},{7,12},{8,13},{9,14},{... | collective-permute-start | bytes 786440 | tf_op jit(solution)/shard_map/ppermute | solution.py:26
  17.9 28.1 %collective-permute-start.4 = (bf16[128,1024]{0,1:T(8,128)(2,1)S(1)}, bf16[128,1024]{0,1:T(8,128)(2,1)S(1)}, u32[]{:S(2)}, u32[]{:S(2)}) collective-permute-start(bf16[128,1024]{0,1:T(8,128)(2,1)S(1)} %copy.50), channel_id=1, source_target_pairs={{0,4},{1,5},{2,6},{3,7},{4,8},{5,9},{6,10},{7,11},{8,12},{9,13},{1... | collective-permute-start | bytes 786440 | tf_op jit(solution)/shard_map/ppermute | solution.py:26
  25.2 21.6 %collective-permute-start.5 = (bf16[128,1024]{0,1:T(8,128)(2,1)S(1)}, bf16[128,1024]{0,1:T(8,128)(2,1)S(1)}, u32[]{:S(2)}, u32[]{:S(2)}) collective-permute-start(bf16[128,1024]{0,1:T(8,128)(2,1)S(1)} %copy.50), channel_id=1, source_target_pairs={{0,3},{1,4},{2,5},{3,6},{4,7},{5,8},{6,9},{7,10},{8,11},{9,12},{10... | collective-permute-start | bytes 786440 | tf_op jit(solution)/shard_map/ppermute | solution.py:26
  27.8 19.7 %collective-permute-start.6 = (bf16[128,1024]{0,1:T(8,128)(2,1)S(1)}, bf16[128,1024]{0,1:T(8,128)(2,1)S(1)}, u32[]{:S(2)}, u32[]{:S(2)}) collective-permute-start(bf16[128,1024]{0,1:T(8,128)(2,1)S(1)} %copy.50), channel_id=1, source_target_pairs={{0,2},{1,3},{2,4},{3,5},{4,6},{5,7},{6,8},{7,9},{8,10},{9,11},{10,... | collective-permute-start | bytes 786440 | tf_op jit(solution)/shard_map/ppermute | solution.py:26
  42.6 7.7 %collective-permute-start.7 = (bf16[128,1024]{0,1:T(8,128)(2,1)S(1)}, bf16[128,1024]{0,1:T(8,128)(2,1)S(1)}, u32[]{:S(2)}, u32[]{:S(2)}) collective-permute-start(bf16[128,1024]{0,1:T(8,128)(2,1)S(1)} %copy.50), channel_id=1, source_target_pairs={{0,1},{1,2},{2,3},{3,4},{4,5},{5,6},{6,7},{7,8},{8,9},{9,10},{10,1... | collective-permute-start | bytes 786440 | tf_op jit(solution)/shard_map/ppermute | solution.py:26
  54.2 5.6 %copy-start.3 = (pred[1152]{0:T(1024)(128)(4,1)}, pred[1152]{0:T(1024)(128)(4,1)S(1)}, u32[]{:S(2)}) copy-start(pred[1152]{0:T(1024)(128)(4,1)S(1)} %get-tuple-element.285) | copy-start | bytes 3460 | tf_op jit(solution)/shard_map/while
  54.2 5.6 %copy-start.6 = (s32[128]{0:T(128)}, s32[128]{0:T(128)S(1)}, u32[]{:S(2)}) copy-start(s32[128]{0:T(128)S(1)} %get-tuple-element.284) | copy-start | bytes 1540 | tf_op jit(solution)/shard_map/while
  62.0 1.1 copy-start.4
  62.0 1.1 copy-start.7
  63.1 5.7 %copy-start.3 = (pred[1152]{0:T(1024)(128)(4,1)}, pred[1152]{0:T(1024)(128)(4,1)S(1)}, u32[]{:S(2)}) copy-start(pred[1152]{0:T(1024)(128)(4,1)S(1)} %get-tuple-element.285) | copy-start | bytes 3460 | tf_op jit(solution)/shard_map/while
  63.1 5.7 %copy-start.6 = (s32[128]{0:T(128)}, s32[128]{0:T(128)S(1)}, u32[]{:S(2)}) copy-start(s32[128]{0:T(128)S(1)} %get-tuple-element.284) | copy-start | bytes 1540 | tf_op jit(solution)/shard_map/while
  70.9 1.2 copy-start.4
  70.9 1.2 copy-start.7
  72.1 5.7 %copy-start.3 = (pred[1152]{0:T(1024)(128)(4,1)}, pred[1152]{0:T(1024)(128)(4,1)S(1)}, u32[]{:S(2)}) copy-start(pred[1152]{0:T(1024)(128)(4,1)S(1)} %get-tuple-element.285) | copy-start | bytes 3460 | tf_op jit(solution)/shard_map/while
  72.1 5.7 %copy-start.6 = (s32[128]{0:T(128)}, s32[128]{0:T(128)S(1)}, u32[]{:S(2)}) copy-start(s32[128]{0:T(128)S(1)} %get-tuple-element.284) | copy-start | bytes 1540 | tf_op jit(solution)/shard_map/while
  79.8 1.1 copy-start.4
  79.9 1.1 copy-start.7
  81.0 5.7 %copy-start.3 = (pred[1152]{0:T(1024)(128)(4,1)}, pred[1152]{0:T(1024)(128)(4,1)S(1)}, u32[]{:S(2)}) copy-start(pred[1152]{0:T(1024)(128)(4,1)S(1)} %get-tuple-element.285) | copy-start | bytes 3460 | tf_op jit(solution)/shard_map/while
  81.0 5.7 %copy-start.6 = (s32[128]{0:T(128)}, s32[128]{0:T(128)S(1)}, u32[]{:S(2)}) copy-start(s32[128]{0:T(128)S(1)} %get-tuple-element.284) | copy-start | bytes 1540 | tf_op jit(solution)/shard_map/while
  88.8 1.1 copy-start.4
  88.8 1.1 copy-start.7
  92.9 16.2 %collective-permute-start.10 = (bf16[128,1024]{0,1:T(8,128)(2,1)S(1)}, bf16[128,1024]{0,1:T(8,128)(2,1)S(1)}, u32[]{:S(2)}, u32[]{:S(2)}) collective-permute-start(bf16[128,1024]{0,1:T(8,128)(2,1)S(1)} %get-tuple-element.193), channel_id=1, source_target_pairs={{3,0},{4,1},{5,2},{6,3},{7,4},{8,5},{9,6},{10,7},{11,8},{12,9},{13... | collective-permute-start | bytes 786440 | tf_op jit(solution)/shard_map/ppermute | solution.py:26
  97.7 14.0 %collective-permute-start.11 = (bf16[128,1024]{0,1:T(8,128)(2,1)S(1)}, bf16[128,1024]{0,1:T(8,128)(2,1)S(1)}, u32[]{:S(2)}, u32[]{:S(2)}) collective-permute-start(bf16[128,1024]{0,1:T(8,128)(2,1)S(1)} %get-tuple-element.192), channel_id=1, source_target_pairs={{4,0},{5,1},{6,2},{7,3},{8,4},{9,5},{10,6},{11,7},{12,8},{13,9},{1... | collective-permute-start | bytes 786440 | tf_op jit(solution)/shard_map/ppermute | solution.py:26
  100.5 25.3 %collective-permute-start.12 = (bf16[128,1024]{0,1:T(8,128)(2,1)S(1)}, bf16[128,1024]{0,1:T(8,128)(2,1)S(1)}, u32[]{:S(2)}, u32[]{:S(2)}) collective-permute-start(bf16[128,1024]{0,1:T(8,128)(2,1)S(1)} %get-tuple-element.191), channel_id=1, source_target_pairs={{5,0},{6,1},{7,2},{8,3},{9,4},{10,5},{11,6},{12,7},{13,8},{14,9},{... | collective-permute-start | bytes 786440 | tf_op jit(solution)/shard_map/ppermute | solution.py:26
  102.4 29.0 %collective-permute-start.13 = (bf16[128,1024]{0,1:T(8,128)(2,1)S(1)}, bf16[128,1024]{0,1:T(8,128)(2,1)S(1)}, u32[]{:S(2)}, u32[]{:S(2)}) collective-permute-start(bf16[128,1024]{0,1:T(8,128)(2,1)S(1)} %get-tuple-element.190), channel_id=1, source_target_pairs={{6,0},{7,1},{8,2},{9,3},{10,4},{11,5},{12,6},{13,7},{14,8},{15,9},... | collective-permute-start | bytes 786440 | tf_op jit(solution)/shard_map/ppermute | solution.py:26
  107.2 24.2 %collective-permute-start.14 = (bf16[128,1024]{0,1:T(8,128)(2,1)S(1)}, bf16[128,1024]{0,1:T(8,128)(2,1)S(1)}, u32[]{:S(2)}, u32[]{:S(2)}) collective-permute-start(bf16[128,1024]{0,1:T(8,128)(2,1)S(1)} %get-tuple-element.189), channel_id=1, source_target_pairs={{7,0},{8,1},{9,2},{10,3},{11,4},{12,5},{13,6},{14,7},{15,8},{16,9}... | collective-permute-start | bytes 786440 | tf_op jit(solution)/shard_map/ppermute | solution.py:26
  109.1 22.3 %collective-permute-start.15 = (bf16[128,1024]{0,1:T(8,128)(2,1)S(1)}, bf16[128,1024]{0,1:T(8,128)(2,1)S(1)}, u32[]{:S(2)}, u32[]{:S(2)}) collective-permute-start(bf16[128,1024]{0,1:T(8,128)(2,1)S(1)} %get-tuple-element.188), channel_id=1, source_target_pairs={{8,0},{9,1},{10,2},{11,3},{12,4},{13,5},{14,6},{15,7},{16,8},{17,9... | collective-permute-start | bytes 786440 | tf_op jit(solution)/shard_map/ppermute | solution.py:26
  111.7 19.7 %collective-permute-start.8 = (bf16[128,1024]{0,1:T(8,128)(2,1)S(1)}, bf16[128,1024]{0,1:T(8,128)(2,1)S(1)}, u32[]{:S(2)}, u32[]{:S(2)}) collective-permute-start(bf16[128,1024]{0,1:T(8,128)(2,1)S(1)} %get-tuple-element.187), channel_id=1, source_target_pairs={{1,0},{2,1},{3,2},{4,3},{5,4},{6,5},{7,6},{8,7},{9,8},{10,9},{11,1... | collective-permute-start | bytes 786440 | tf_op jit(solution)/shard_map/ppermute | solution.py:26
  125.8 17.3 %collective-permute-start.9 = (bf16[128,1024]{0,1:T(8,128)(2,1)S(1)}, bf16[128,1024]{0,1:T(8,128)(2,1)S(1)}, u32[]{:S(2)}, u32[]{:S(2)}) collective-permute-start(bf16[128,1024]{0,1:T(8,128)(2,1)S(1)} %get-tuple-element.194), channel_id=1, source_target_pairs={{2,0},{3,1},{4,2},{5,3},{6,4},{7,5},{8,6},{9,7},{10,8},{11,9},{12,... | collective-permute-start | bytes 786440 | tf_op jit(solution)/shard_map/ppermute | solution.py:26
  147.1 8.8 %copy-start.2 = (bf16[336,1024]{1,0:T(8,128)(2,1)S(1)}, bf16[336,1024]{1,0:T(8,128)(2,1)}, u32[]{:S(2)}) copy-start(bf16[336,1024]{1,0:T(8,128)(2,1)} %param.9) | copy-start | bytes 2064388
  147.1 57.9 %copy-start.5 = (f32[1024]{0:T(1024)S(1)}, f32[1024]{0:T(1024)}, u32[]{:S(2)}) copy-start(f32[1024]{0:T(1024)} %param.10) | copy-start | bytes 12292
  147.1 57.9 %all-to-all-start = ((bf16[16,128,1024]{2,1,0:T(8,128)(2,1)}), bf16[16,128,1024]{2,1,0:T(8,128)(2,1)}, u32[]{:S(2)}, u32[]{:S(2)}) async-start(bf16[16,128,1024]{2,1,0:T(8,128)(2,1)} %broadcast_in_dim.44), calls=%async_computation | async-start | bytes 8388608 | tf_op jit(solution)/shard_map/all_to_all | solution.py:92
  156.2 55.0 %copy-start.1 = (bf16[336,1024]{0,1:T(8,128)(2,1)}, bf16[336,1024]{0,1:T(8,128)(2,1)S(1)}, u32[]{:S(2)}) copy-start(bf16[336,1024]{0,1:T(8,128)(2,1)S(1)} %copy.49) | copy-start | bytes 2064388
  211.2 112.5 %all-to-all-start.1 = ((f32[336,32,32]{0,2,1:T(8,128)}), f32[336,32,32]{0,2,1:T(8,128)S(1)}, u32[]{:S(2)}, u32[]{:S(2)}) async-start(f32[336,32,32]{0,2,1:T(8,128)} %bitcast.67), calls=%async_computation.1 | async-start | bytes 3145728 | tf_op jit(solution)/shard_map/all_to_all | solution.py:106

commit v6 on v3

--- a/solution.py
+++ b/solution.py
@@ -99,25 +99,33 @@
         signed = jnp.where(kept_mask, jnp.sign(weight_full), 0.0)
 
         logit_part = jnp.sum(local_grad * signed, axis=0)
-        for axis in reversed(FSDP):
-            logit_part = lax.psum(logit_part, axis)
 
         rows, cols = local_grad.shape
-        piece = cols // n_seq
-        payload = jnp.concatenate([local_grad, logit_part[None]], axis=0)
-        pieces = payload.reshape(rows + 1, n_seq, piece)
-        received = lax.all_to_all(pieces, SEQ, 1, 1, tiled=True)
+        n_z = lax.axis_size("z")
+        half = cols // 2
+        piece = half // n_z
+        xh_index = lax.axis_index("xh")
+        keep = lax.dynamic_slice_in_dim(local_grad, xh_index * half, half, 1)
+        send = lax.dynamic_slice_in_dim(local_grad, (1 - xh_index) * half, half, 1)
+        swapped = keep + lax.ppermute(send, "xh", [(0, 1), (1, 0)])
+        for axis in ("c", "xl", "y", "xh"):
+            logit_part = lax.psum(logit_part, axis)
+        logit_half = lax.dynamic_slice_in_dim(logit_part, xh_index * half, half, 0)
+        payload = jnp.concatenate([swapped, logit_half[None]], axis=0)
+        received = lax.all_to_all(payload.reshape(rows + 1, n_z, piece), "z", 1, 1, tiled=True)
         summed = jnp.sum(received, axis=1)
         dense_piece = summed[:rows]
         logit_piece = summed[rows:]
-        seq_index = lax.axis_index(SEQ)
-        kept_piece = lax.dynamic_slice_in_dim(kept_mask, seq_index * piece, piece, 1)
+        z_index = lax.axis_index("z")
+        kept_piece = lax.dynamic_slice_in_dim(
+            kept_mask, xh_index * half + z_index * piece, piece, 1
+        )
         weight_piece = jnp.where(kept_piece, dense_piece, 0.0).astype(jnp.bfloat16)
         logit_hi = logit_piece.astype(jnp.bfloat16)
         logit_lo = (logit_piece - logit_hi.astype(jnp.float32)).astype(jnp.bfloat16)
         out_piece = jnp.concatenate([weight_piece, logit_hi, logit_lo], axis=0)
-        out_piece = lax.all_gather(out_piece, "xh", axis=1, tiled=True)
-        out_full = lax.all_gather(out_piece, "z", axis=1, tiled=True)
+        out_piece = lax.all_gather(out_piece, "z", axis=1, tiled=True)
+        out_full = lax.all_gather(out_piece, "xh", axis=1, tiled=True)
         grad_weight = out_full[:rows]
         logit_sum = out_full[rows].astype(jnp.float32) + out_full[rows + 1].astype(jnp.float32)
         grad_logit = -logit_sum * threshold * (1.0 - threshold)

time: 378 us -> 352 us (0.931)
  waiting for transfers between devices: 163 us -> 126 us
  local copies, waits for them, and re-layouts: 32.1 us -> 37.7 us
    all_to_all x1, waiting for transfers between devices: 71.1 us -> 34.3 us  [local(): lax.all_to_all(payload.reshape(rows + 1, n_z, piece), 'z', 1, 1, tiled=True)]
    all_gather x2, blocking collectives: 38.1 us -> 42.1 us  [the longest x1 32.2 us: local(): out_piece = lax.all_gather(out_piece, 'z', axis=1, tiled=True)]
    ppermute x0 -> x1, starting transfers between devices: none -> 4.04 us  [local(): swapped = keep + lax.ppermute(send, 'xh', [(0, 1), (1, 0)])]
    psum x3 -> x4, blocking collectives: 27.5 us -> 26.2 us  [local(): logit_part = lax.psum(logit_part, axis)]
    unnamed x20 -> x16, local copies, waits for them, and re-layouts: 8.87 us -> 9.97 us
  transfers between devices with their start and end apart: 18 -> 19, of which waited for: 9 -> 9; matrix products, arithmetic and copies ran while one was open for 2% -> 4% of each run, Pallas kernels for 0% -> 0%
where the time goes in v6:
time: 352 us; the launch traced here: 350 us
  waiting for transfers between devices  126 us (36%)
  starting transfers between devices  77.7 us (22%)
  blocking collectives  68.3 us (19%)
  local copies, waits for them, and re-layouts  37.7 us (11%)
  other arithmetic  19.4 us (6%)
  matrix products  19.1 us (5%)
    all_to_all x1, waiting for transfers between devices, local(): lax.all_to_all(spread, FSDP, 0, 0, tiled=True)  49.2 us
    ppermute x16, starting transfers between devices, passed_along(): lax.ppermute(value, axis, [(source, source + steps) for source in range(f...  48.6 us
    ppermute x16, waiting for transfers between devices, passed_along(): lax.ppermute(value, axis, [(source, source + steps) for source in range(f...  42.8 us
    all_to_all x1, waiting for transfers between devices, local(): lax.all_to_all(payload.reshape(rows + 1, n_z, piece), 'z', 1, 1, tiled=True)  34.3 us
    all_gather x1, blocking collectives, local(): out_piece = lax.all_gather(out_piece, 'z', axis=1, tiled=True)  32.2 us
    psum x4, blocking collectives, local(): logit_part = lax.psum(logit_part, axis)  26.2 us
    all_to_all x1, starting transfers between devices, local(): lax.all_to_all(payload.reshape(rows + 1, n_z, piece), 'z', 1, 1, tiled=True)  16.4 us
    unnamed x16, local copies, waits for them, and re-layouts  9.97 us
  transfers between devices with their start and end apart: 19, of which 9 were waited for; matrix products, arithmetic and copies ran while one was open for 4% of the time, Pallas kernels for 0%

profile of v6, /device:TPU:6, one launch (start us, length us, event | category | flops | bytes accessed | tf_op | source)
XLA Modules:
  0.0 349.5 jit_solution(9408182143248317847)
XLA Ops:
  1.9 5.1 %collective-permute-start = (bf16[128,1024]{0,1:T(8,128)(2,1)S(1)}, bf16[128,1024]{0,1:T(8,128)(2,1)S(1)}, u32[]{:S(2)}, u32[]{:S(2)}) collective-permute-start(bf16[128,1024]{0,1:T(8,128)(2,1)S(1)} %copy.88), channel_id=1, source_target_pairs={{0,8},{1,9},{2,10},{3,11},{4,12},{5,13},{6,14},{7,15},{8,16},{9,17... | collective-permute-start | bytes 786440 | tf_op jit(solution)/shard_map/ppermute | solution.py:26
  7.0 3.0 collective-permute-start.1
  10.0 5.6 %collective-permute-start.2 = (bf16[128,1024]{0,1:T(8,128)(2,1)S(1)}, bf16[128,1024]{0,1:T(8,128)(2,1)S(1)}, u32[]{:S(2)}, u32[]{:S(2)}) collective-permute-start(bf16[128,1024]{0,1:T(8,128)(2,1)S(1)} %copy.88), channel_id=1, source_target_pairs={{0,6},{1,7},{2,8},{3,9},{4,10},{5,11},{6,12},{7,13},{8,14},{9,15},... | collective-permute-start | bytes 786440 | tf_op jit(solution)/shard_map/ppermute | solution.py:26
  15.6 2.3 collective-permute-start.3
  17.9 3.7 %collective-permute-start.4 = (bf16[128,1024]{0,1:T(8,128)(2,1)S(1)}, bf16[128,1024]{0,1:T(8,128)(2,1)S(1)}, u32[]{:S(2)}, u32[]{:S(2)}) collective-permute-start(bf16[128,1024]{0,1:T(8,128)(2,1)S(1)} %copy.88), channel_id=1, source_target_pairs={{0,4},{1,5},{2,6},{3,7},{4,8},{5,9},{6,10},{7,11},{8,12},{9,13},{1... | collective-permute-start | bytes 786440 | tf_op jit(solution)/shard_map/ppermute | solution.py:26
  23.4 1.8 collective-permute-done
  25.2 1.9 collective-permute-start.5
  27.9 3.2 collective-permute-start.6
  31.8 10.8 %collective-permute-done.2 = bf16[128,1024]{0,1:T(8,128)(2,1)S(1)} collective-permute-done((bf16[128,1024]{0,1:T(8,128)(2,1)S(1)}, bf16[128,1024]{0,1:T(8,128)(2,1)S(1)}, u32[]{:S(2)}, u32[]{:S(2)}) %collective-permute-start.2) | collective-permute-done | bytes 262176 | tf_op jit(solution)/shard_map/ppermute | solution.py:26
  42.6 1.9 collective-permute-start.7
  48.3 1.9 collective-permute-done.7
  51.7 2.4 broadcast_in_dim.44
  54.2 37.9 %while.14 = (s32[]{:T(128)}, f32[1152,1024]{0,1:T(8,128)}, bf16[128,2048]{1,0:T(8,128)(2,1)}, bf16[1152,1024]{0,1:T(8,128)(2,1)}, bf16[128,2048]{1,0:T(8,128)(2,...) while((s32[]{:T(128)}, f32[1152,1024]{0,1:T(8,128)}, ...), condition=%wide.region_3.4_spmd.clone, body=%wide.region_0.3_spmd.clone.sunk | while | flops 459033344 | bytes 7793005 | solution.py:76
  57.9 1.6 fusion.48
  60.3 2.2 fusion.49
  69.8 2.2 fusion.49
  76.9 1.6 fusion.48
  79.3 2.2 fusion.49
  88.8 2.2 fusion.49
  92.1 2.6 convert.10
  95.1 4.8 %collective-permute-start.10 = (bf16[128,1024]{0,1:T(8,128)(2,1)S(1)}, bf16[128,1024]{0,1:T(8,128)(2,1)S(1)}, u32[]{:S(2)}, u32[]{:S(2)}) collective-permute-start(bf16[128,1024]{0,1:T(8,128)(2,1)S(1)} %get-tuple-element.211), channel_id=1, source_target_pairs={{3,0},{4,1},{5,2},{6,3},{7,4},{8,5},{9,6},{10,7},{11,8},{12,9},{13... | collective-permute-start | bytes 786440 | tf_op jit(solution)/shard_map/ppermute | solution.py:26
  99.9 2.7 collective-permute-start.11
  102.7 1.9 collective-permute-start.12
  104.6 4.7 %collective-permute-start.13 = (bf16[128,1024]{0,1:T(8,128)(2,1)S(1)}, bf16[128,1024]{0,1:T(8,128)(2,1)S(1)}, u32[]{:S(2)}, u32[]{:S(2)}) collective-permute-start(bf16[128,1024]{0,1:T(8,128)(2,1)S(1)} %get-tuple-element.208), channel_id=1, source_target_pairs={{6,0},{7,1},{8,2},{9,3},{10,4},{11,5},{12,6},{13,7},{14,8},{15,9},... | collective-permute-start | bytes 786440 | tf_op jit(solution)/shard_map/ppermute | solution.py:26
  109.3 1.9 collective-permute-start.14
  111.3 1.9 collective-permute-start.15
  113.9 1.9 collective-permute-start.8
  115.8 12.1 %collective-permute-done.12 = bf16[128,1024]{0,1:T(8,128)(2,1)S(1)} collective-permute-done((bf16[128,1024]{0,1:T(8,128)(2,1)S(1)}, bf16[128,1024]{0,1:T(8,128)(2,1)S(1)}, u32[]{:S(2)}, u32[]{:S(2)}) %collective-permute-start.12) | collective-permute-done | bytes 262176 | tf_op jit(solution)/shard_map/ppermute | solution.py:26
  128.0 1.9 collective-permute-start.9
  129.9 3.7 %collective-permute-done.13 = bf16[128,1024]{0,1:T(8,128)(2,1)S(1)} collective-permute-done((bf16[128,1024]{0,1:T(8,128)(2,1)S(1)}, bf16[128,1024]{0,1:T(8,128)(2,1)S(1)}, u32[]{:S(2)}, u32[]{:S(2)}) %collective-permute-start.13) | collective-permute-done | bytes 262176 | tf_op jit(solution)/shard_map/ppermute | solution.py:26
  133.6 11.7 %collective-permute-done.9 = bf16[128,1024]{0,1:T(8,128)(2,1)S(1)} collective-permute-done((bf16[128,1024]{0,1:T(8,128)(2,1)S(1)}, bf16[128,1024]{0,1:T(8,128)(2,1)S(1)}, u32[]{:S(2)}, u32[]{:S(2)}) %collective-permute-start.9) | collective-permute-done | bytes 262176 | tf_op jit(solution)/shard_map/ppermute | solution.py:26
  146.8 2.5 broadcast_in_dim.45
  149.3 8.6 %all-to-all-start = ((bf16[16,128,1024]{2,1,0:T(8,128)(2,1)}), bf16[16,128,1024]{2,1,0:T(8,128)(2,1)}, u32[]{:S(2)}, u32[]{:S(2)}) async-start(bf16[16,128,1024]{2,1,0:T(8,128)(2,1)} %broadcast_in_dim.45), calls=%async_computation | async-start | bytes 8388608 | tf_op jit(solution)/shard_map/all_to_all | solution.py:92
  157.9 49.2 %all-to-all-done = bf16[16,128,1024]{2,1,0:T(8,128)(2,1)} async-done(((bf16[16,128,1024]{2,1,0:T(8,128)(2,1)}), bf16[16,128,1024]{2,1,0:T(8,128)(2,1)}, u32[]{:S(2)}, u32[]{:S(2)}) %all-to-all-start) | async-done | bytes 4194336 | tf_op jit(solution)/shard_map/all_to_all | solution.py:92
  207.1 3.8 %fusion.26 = f32[1024,336]{0,1:T(8,128)S(1)} fusion(bf16[336,2048]{1,0:T(8,128)(2,1)S(1)} %copy-done, bf16[2048,1024]{1,0:T(8,128)(2,1)} %bitcast), kind=kOutput, calls=%fused_computation.54 | convolution fusion | flops 1409286144 | bytes 6946816 | tf_op jit(solution)/shard_map/dot_general | solution.py:95
  211.8 4.0 %collective-permute-start.16 = (f32[336,512]{1,0:T(8,128)}, f32[336,512]{1,0:T(8,128)}, u32[]{:S(2)}, u32[]{:S(2)}) collective-permute-start(f32[336,512]{1,0:T(8,128)} %dynamic-slice_bitcast_fusion), channel_id=1, source_target_pairs={{0,16},{16,0},{1,17},{17,1},{2,18},{18,2},{3,19},{19,3},{4,20},{20... | collective-permute-start | bytes 2064392 | tf_op jit(solution)/shard_map/ppermute | solution.py:110
  217.3 1.6 copy.101
  218.9 2.2 fusion.21
  221.1 2.5 psum.28
  223.6 8.1 %psum.29 = f32[1024]{0:T(1024)S(1)} all-reduce(f32[1024]{0:T(1024)S(1)} %psum.28), channel_id=1, replica_groups=mesh['z'=16,'xh'=2,'y'=4,'xl'=2,'c'=2] {'xl'}, use_global_device_ids=true, to_apply=%region_6.7 | all-reduce | flops 1024 | bytes 8192 | tf_op jit(solution)/shard_map/psum | solution.py:112
  231.7 9.2 %psum.30 = f32[1024]{0:T(1024)S(1)} all-reduce(f32[1024]{0:T(1024)S(1)} %psum.29), channel_id=1, replica_groups=mesh['z'=16,'xh'=2,'y'=4,'xl'=2,'c'=2] {'y'}, use_global_device_ids=true, to_apply=%region_7.8 | all-reduce | flops 1024 | bytes 8192 | tf_op jit(solution)/shard_map/psum | solution.py:112
  240.9 6.4 %psum.31 = f32[1024]{0:T(1024)S(1)} all-reduce(f32[1024]{0:T(1024)S(1)} %psum.30), channel_id=1, replica_groups=mesh['z'=16,'xh'=2,'y'=4,'xl'=2,'c'=2] {'xh'}, use_global_device_ids=true, to_apply=%region_8.9 | all-reduce | flops 1024 | bytes 8192 | tf_op jit(solution)/shard_map/psum | solution.py:112
  248.3 2.1 bitcast_add_fusion
  251.8 2.0 pad_maximum_fusion
  253.7 16.4 %all-to-all-start.1 = ((f32[337,16,32]{0,2,1:T(8,128)}), f32[337,16,32]{0,2,1:T(8,128)S(1)}, u32[]{:S(2)}, u32[]{:S(2)}) async-start(f32[337,16,32]{0,2,1:T(8,128)} %pad_maximum_fusion), calls=%async_computation.1 | async-start | bytes 1572864 | tf_op jit(solution)/shard_map/all_to_all | solution.py:115
  270.5 34.3 %all-to-all-done.1 = f32[337,16,32]{0,2,1:T(8,128)S(1)} async-done(((f32[337,16,32]{0,2,1:T(8,128)}), f32[337,16,32]{0,2,1:T(8,128)S(1)}, u32[]{:S(2)}, u32[]{:S(2)}) %all-to-all-start.1) | async-done | bytes 690208 | tf_op jit(solution)/shard_map/all_to_all | solution.py:115
  305.3 32.2 %all_gather.6 = bf16[338,512]{0,1:T(8,128)(2,1)S(1)} all-gather(bf16[338,32]{0,1:T(8,128)(2,1)S(1)} %pad_maximum_fusion.1), channel_id=1, replica_groups=mesh['z'=16,'xh'=2,'y'=4,'xl'=2,'c'=2] {'z'}, dimensions={1}, use_global_device_ids=true | all-gather | bytes 367744 | tf_op jit(solution)/shard_map/all_gather | solution.py:127
  337.5 9.9 %all_gather.7 = bf16[338,1024]{0,1:T(8,128)(2,1)S(1)} all-gather(bf16[338,512]{0,1:T(8,128)(2,1)S(1)} %all_gather.6), channel_id=1, replica_groups=mesh['z'=16,'xh'=2,'y'=4,'xl'=2,'c'=2] {'xh'}, dimensions={1}, use_global_device_ids=true | all-gather | bytes 1038336 | tf_op jit(solution)/shard_map/all_gather | solution.py:128
  (74 shorter events, 45.7 us)
Async XLA Ops:
  0.6 206.5 %copy-start = (bf16[336,2048]{1,0:T(8,128)(2,1)S(1)}, bf16[336,2048]{1,0:T(8,128)(2,1)}, u32[]{:S(2)}) copy-start(bf16[336,2048]{1,0:T(8,128)(2,1)} %param.8) | copy-start | bytes 4128772
  1.9 23.3 %collective-permute-start = (bf16[128,1024]{0,1:T(8,128)(2,1)S(1)}, bf16[128,1024]{0,1:T(8,128)(2,1)S(1)}, u32[]{:S(2)}, u32[]{:S(2)}) collective-permute-start(bf16[128,1024]{0,1:T(8,128)(2,1)S(1)} %copy.88), channel_id=1, source_target_pairs={{0,8},{1,9},{2,10},{3,11},{4,12},{5,13},{6,14},{7,15},{8,16},{9,17... | collective-permute-start | bytes 786440 | tf_op jit(solution)/shard_map/ppermute | solution.py:26
  7.0 20.9 %collective-permute-start.1 = (bf16[128,1024]{0,1:T(8,128)(2,1)S(1)}, bf16[128,1024]{0,1:T(8,128)(2,1)S(1)}, u32[]{:S(2)}, u32[]{:S(2)}) collective-permute-start(bf16[128,1024]{0,1:T(8,128)(2,1)S(1)} %copy.88), channel_id=1, source_target_pairs={{0,7},{1,8},{2,9},{3,10},{4,11},{5,12},{6,13},{7,14},{8,15},{9,16}... | collective-permute-start | bytes 786440 | tf_op jit(solution)/shard_map/ppermute | solution.py:26
  10.0 32.6 %collective-permute-start.2 = (bf16[128,1024]{0,1:T(8,128)(2,1)S(1)}, bf16[128,1024]{0,1:T(8,128)(2,1)S(1)}, u32[]{:S(2)}, u32[]{:S(2)}) collective-permute-start(bf16[128,1024]{0,1:T(8,128)(2,1)S(1)} %copy.88), channel_id=1, source_target_pairs={{0,6},{1,7},{2,8},{3,9},{4,10},{5,11},{6,12},{7,13},{8,14},{9,15},... | collective-permute-start | bytes 786440 | tf_op jit(solution)/shard_map/ppermute | solution.py:26
  15.6 29.7 %collective-permute-start.3 = (bf16[128,1024]{0,1:T(8,128)(2,1)S(1)}, bf16[128,1024]{0,1:T(8,128)(2,1)S(1)}, u32[]{:S(2)}, u32[]{:S(2)}) collective-permute-start(bf16[128,1024]{0,1:T(8,128)(2,1)S(1)} %copy.88), channel_id=1, source_target_pairs={{0,5},{1,6},{2,7},{3,8},{4,9},{5,10},{6,11},{7,12},{8,13},{9,14},{... | collective-permute-start | bytes 786440 | tf_op jit(solution)/shard_map/ppermute | solution.py:26
  17.9 28.1 %collective-permute-start.4 = (bf16[128,1024]{0,1:T(8,128)(2,1)S(1)}, bf16[128,1024]{0,1:T(8,128)(2,1)S(1)}, u32[]{:S(2)}, u32[]{:S(2)}) collective-permute-start(bf16[128,1024]{0,1:T(8,128)(2,1)S(1)} %copy.88), channel_id=1, source_target_pairs={{0,4},{1,5},{2,6},{3,7},{4,8},{5,9},{6,10},{7,11},{8,12},{9,13},{1... | collective-permute-start | bytes 786440 | tf_op jit(solution)/shard_map/ppermute | solution.py:26
  25.2 21.6 %collective-permute-start.5 = (bf16[128,1024]{0,1:T(8,128)(2,1)S(1)}, bf16[128,1024]{0,1:T(8,128)(2,1)S(1)}, u32[]{:S(2)}, u32[]{:S(2)}) collective-permute-start(bf16[128,1024]{0,1:T(8,128)(2,1)S(1)} %copy.88), channel_id=1, source_target_pairs={{0,3},{1,4},{2,5},{3,6},{4,7},{5,8},{6,9},{7,10},{8,11},{9,12},{10... | collective-permute-start | bytes 786440 | tf_op jit(solution)/shard_map/ppermute | solution.py:26
  27.9 19.7 %collective-permute-start.6 = (bf16[128,1024]{0,1:T(8,128)(2,1)S(1)}, bf16[128,1024]{0,1:T(8,128)(2,1)S(1)}, u32[]{:S(2)}, u32[]{:S(2)}) collective-permute-start(bf16[128,1024]{0,1:T(8,128)(2,1)S(1)} %copy.88), channel_id=1, source_target_pairs={{0,2},{1,3},{2,4},{3,5},{4,6},{5,7},{6,8},{7,9},{8,10},{9,11},{10,... | collective-permute-start | bytes 786440 | tf_op jit(solution)/shard_map/ppermute | solution.py:26
  42.6 7.7 %collective-permute-start.7 = (bf16[128,1024]{0,1:T(8,128)(2,1)S(1)}, bf16[128,1024]{0,1:T(8,128)(2,1)S(1)}, u32[]{:S(2)}, u32[]{:S(2)}) collective-permute-start(bf16[128,1024]{0,1:T(8,128)(2,1)S(1)} %copy.88), channel_id=1, source_target_pairs={{0,1},{1,2},{2,3},{3,4},{4,5},{5,6},{6,7},{7,8},{8,9},{9,10},{10,1... | collective-permute-start | bytes 786440 | tf_op jit(solution)/shard_map/ppermute | solution.py:26
  95.1 16.2 %collective-permute-start.10 = (bf16[128,1024]{0,1:T(8,128)(2,1)S(1)}, bf16[128,1024]{0,1:T(8,128)(2,1)S(1)}, u32[]{:S(2)}, u32[]{:S(2)}) collective-permute-start(bf16[128,1024]{0,1:T(8,128)(2,1)S(1)} %get-tuple-element.211), channel_id=1, source_target_pairs={{3,0},{4,1},{5,2},{6,3},{7,4},{8,5},{9,6},{10,7},{11,8},{12,9},{13... | collective-permute-start | bytes 786440 | tf_op jit(solution)/shard_map/ppermute | solution.py:26
  99.9 14.0 %collective-permute-start.11 = (bf16[128,1024]{0,1:T(8,128)(2,1)S(1)}, bf16[128,1024]{0,1:T(8,128)(2,1)S(1)}, u32[]{:S(2)}, u32[]{:S(2)}) collective-permute-start(bf16[128,1024]{0,1:T(8,128)(2,1)S(1)} %get-tuple-element.210), channel_id=1, source_target_pairs={{4,0},{5,1},{6,2},{7,3},{8,4},{9,5},{10,6},{11,7},{12,8},{13,9},{1... | collective-permute-start | bytes 786440 | tf_op jit(solution)/shard_map/ppermute | solution.py:26
  102.7 25.3 %collective-permute-start.12 = (bf16[128,1024]{0,1:T(8,128)(2,1)S(1)}, bf16[128,1024]{0,1:T(8,128)(2,1)S(1)}, u32[]{:S(2)}, u32[]{:S(2)}) collective-permute-start(bf16[128,1024]{0,1:T(8,128)(2,1)S(1)} %get-tuple-element.209), channel_id=1, source_target_pairs={{5,0},{6,1},{7,2},{8,3},{9,4},{10,5},{11,6},{12,7},{13,8},{14,9},{... | collective-permute-start | bytes 786440 | tf_op jit(solution)/shard_map/ppermute | solution.py:26
  104.6 29.0 %collective-permute-start.13 = (bf16[128,1024]{0,1:T(8,128)(2,1)S(1)}, bf16[128,1024]{0,1:T(8,128)(2,1)S(1)}, u32[]{:S(2)}, u32[]{:S(2)}) collective-permute-start(bf16[128,1024]{0,1:T(8,128)(2,1)S(1)} %get-tuple-element.208), channel_id=1, source_target_pairs={{6,0},{7,1},{8,2},{9,3},{10,4},{11,5},{12,6},{13,7},{14,8},{15,9},... | collective-permute-start | bytes 786440 | tf_op jit(solution)/shard_map/ppermute | solution.py:26
  109.3 24.3 %collective-permute-start.14 = (bf16[128,1024]{0,1:T(8,128)(2,1)S(1)}, bf16[128,1024]{0,1:T(8,128)(2,1)S(1)}, u32[]{:S(2)}, u32[]{:S(2)}) collective-permute-start(bf16[128,1024]{0,1:T(8,128)(2,1)S(1)} %get-tuple-element.207), channel_id=1, source_target_pairs={{7,0},{8,1},{9,2},{10,3},{11,4},{12,5},{13,6},{14,7},{15,8},{16,9}... | collective-permute-start | bytes 786440 | tf_op jit(solution)/shard_map/ppermute | solution.py:26
  111.3 22.3 %collective-permute-start.15 = (bf16[128,1024]{0,1:T(8,128)(2,1)S(1)}, bf16[128,1024]{0,1:T(8,128)(2,1)S(1)}, u32[]{:S(2)}, u32[]{:S(2)}) collective-permute-start(bf16[128,1024]{0,1:T(8,128)(2,1)S(1)} %get-tuple-element.206), channel_id=1, source_target_pairs={{8,0},{9,1},{10,2},{11,3},{12,4},{13,5},{14,6},{15,7},{16,8},{17,9... | collective-permute-start | bytes 786440 | tf_op jit(solution)/shard_map/ppermute | solution.py:26
  113.9 19.7 %collective-permute-start.8 = (bf16[128,1024]{0,1:T(8,128)(2,1)S(1)}, bf16[128,1024]{0,1:T(8,128)(2,1)S(1)}, u32[]{:S(2)}, u32[]{:S(2)}) collective-permute-start(bf16[128,1024]{0,1:T(8,128)(2,1)S(1)} %get-tuple-element.205), channel_id=1, source_target_pairs={{1,0},{2,1},{3,2},{4,3},{5,4},{6,5},{7,6},{8,7},{9,8},{10,9},{11,1... | collective-permute-start | bytes 786440 | tf_op jit(solution)/shard_map/ppermute | solution.py:26
  128.0 17.3 %collective-permute-start.9 = (bf16[128,1024]{0,1:T(8,128)(2,1)S(1)}, bf16[128,1024]{0,1:T(8,128)(2,1)S(1)}, u32[]{:S(2)}, u32[]{:S(2)}) collective-permute-start(bf16[128,1024]{0,1:T(8,128)(2,1)S(1)} %get-tuple-element.212), channel_id=1, source_target_pairs={{2,0},{3,1},{4,2},{5,3},{6,4},{7,5},{8,6},{9,7},{10,8},{11,9},{12,... | collective-permute-start | bytes 786440 | tf_op jit(solution)/shard_map/ppermute | solution.py:26
  149.3 57.8 %all-to-all-start = ((bf16[16,128,1024]{2,1,0:T(8,128)(2,1)}), bf16[16,128,1024]{2,1,0:T(8,128)(2,1)}, u32[]{:S(2)}, u32[]{:S(2)}) async-start(bf16[16,128,1024]{2,1,0:T(8,128)(2,1)} %broadcast_in_dim.45), calls=%async_computation | async-start | bytes 8388608 | tf_op jit(solution)/shard_map/all_to_all | solution.py:92
  211.8 7.1 %copy-start.1 = (f32[1024]{0:T(1024)S(1)}, f32[1024]{0:T(1024)}, u32[]{:S(2)}) copy-start(f32[1024]{0:T(1024)} %param.10) | copy-start | bytes 12292
  211.8 36.5 %collective-permute-start.16 = (f32[336,512]{1,0:T(8,128)}, f32[336,512]{1,0:T(8,128)}, u32[]{:S(2)}, u32[]{:S(2)}) collective-permute-start(f32[336,512]{1,0:T(8,128)} %dynamic-slice_bitcast_fusion), channel_id=1, source_target_pairs={{0,16},{16,0},{1,17},{17,1},{2,18},{18,2},{3,19},{19,3},{4,20},{20... | collective-permute-start | bytes 2064392 | tf_op jit(solution)/shard_map/ppermute | solution.py:110
  253.7 51.1 %all-to-all-start.1 = ((f32[337,16,32]{0,2,1:T(8,128)}), f32[337,16,32]{0,2,1:T(8,128)S(1)}, u32[]{:S(2)}, u32[]{:S(2)}) async-start(f32[337,16,32]{0,2,1:T(8,128)} %pad_maximum_fusion), calls=%async_computation.1 | async-start | bytes 1572864 | tf_op jit(solution)/shard_map/all_to_all | solution.py:115

commit v7 on v6

--- a/solution.py
+++ b/solution.py
@@ -48,14 +48,15 @@
         q_span = kv_pair * head_ratio * HEAD
         k_span = kv_pair * HEAD
 
-        def group_step(group_index, running):
-            q_cols = lax.dynamic_slice_in_dim(queries, group_index * q_span, q_span, 1).reshape(
+        value_parts = []
+        for group_index in range(group_count):
+            q_cols = queries[:, group_index * q_span : (group_index + 1) * q_span].reshape(
                 tok_rows, kv_pair, head_ratio, HEAD
             )
-            d_cols = lax.dynamic_slice_in_dim(out_grad, group_index * q_span, q_span, 1).reshape(
+            d_cols = out_grad[:, group_index * q_span : (group_index + 1) * q_span].reshape(
                 tok_rows, kv_pair, head_ratio, HEAD
             )
-            k_cols = lax.dynamic_slice_in_dim(key_rows, group_index * k_span, k_span, 1).reshape(
+            k_cols = key_rows[:, group_index * k_span : (group_index + 1) * k_span].reshape(
                 span_keys, kv_pair, HEAD
             )
             scores = (
@@ -69,13 +70,9 @@
             value_part = jnp.einsum(
                 "grqk,qgrd->kgd", probabilities, d_cols, preferred_element_type=jnp.float32
             )
-            return lax.dynamic_update_slice_in_dim(
-                running, value_part.reshape(span_keys, k_span), group_index * k_span, 1
-            )
+            value_parts.append(value_part.reshape(span_keys, k_span))
 
-        partial_grad = lax.fori_loop(
-            0, group_count, group_step, jnp.zeros((span_keys, value_weight.shape[1]), jnp.float32)
-        )
+        partial_grad = jnp.concatenate(value_parts, axis=1)
 
         def block_at(distance):
             return partial_grad[

time: 352 us -> 332 us (0.943)
  waiting for transfers between devices: 126 us -> 111 us
  local copies, waits for them, and re-layouts: 37.7 us -> 24.1 us
  starting transfers between devices: 77.7 us -> 86.8 us
  other arithmetic: 19.4 us -> 12 us
  matrix products: 19.1 us -> 24.7 us
    ppermute x16, waiting for transfers between devices: 42.8 us -> 27.3 us  [passed_along(): lax.ppermute(value, axis, [(source, source + steps) for source in range(f...]
    dynamic_slice x16 -> x0, local copies, waits for them, and re-layouts: 11.9 us -> none  [the longest x4 4.46 us: group_step(): lax.dynamic_slice_in_dim(key_rows, group_index * k_span, k_span, 1)]
    ppermute x16, starting transfers between devices: 48.6 us -> 58.7 us  [passed_along(): lax.ppermute(value, axis, [(source, source + steps) for source in range(f...]
    slice x0 -> x7, local copies, waits for them, and re-layouts: none -> 6.49 us  [the longest x5 4.13 us: local(): out_grad[:, group_index * q_span:(group_index + 1) * q_span]]
    and x4 -> x1, other arithmetic: 6.09 us -> 1.48 us  [local(): visible = (offset >= 0) & (offset < WINDOW) & (key_pos >= 0)[None, :]]
    dynamic_update_slice x4 -> x0, local copies, waits for them, and re-layouts: 4.4 us -> none  [group_step(): lax.dynamic_update_slice_in_dim(running, value_part.reshape(span_keys, k_...]
    dot_general x4, matrix products: 8.88 us -> 12.4 us  [local(): jnp.einsum('grqk,qgrd->kgd', probabilities, d_cols, preferred_element_typ...]
    unnamed x16 -> x40, local copies, waits for them, and re-layouts: 9.97 us -> 9.36 us
  transfers between devices with their start and end apart: 19 -> 19, of which waited for: 9 -> 9; matrix products, arithmetic and copies ran while one was open for 4% -> 6% of each run, Pallas kernels for 0% -> 0%
where the time goes in v7:
time: 332 us; the launch traced here: 328 us
  waiting for transfers between devices  111 us (33%)
  starting transfers between devices  86.8 us (26%)
  blocking collectives  68.3 us (21%)
  matrix products  24.7 us (7%)
  local copies, waits for them, and re-layouts  24.1 us (7%)
  other arithmetic  12 us (4%)
    ppermute x16, starting transfers between devices, passed_along(): lax.ppermute(value, axis, [(source, source + steps) for source in range(f...  58.7 us
    all_to_all x1, waiting for transfers between devices, local(): lax.all_to_all(spread, FSDP, 0, 0, tiled=True)  49.2 us
    all_to_all x1, waiting for transfers between devices, local(): lax.all_to_all(payload.reshape(rows + 1, n_z, piece), 'z', 1, 1, tiled=True)  34.1 us
    all_gather x1, blocking collectives, local(): out_piece = lax.all_gather(out_piece, 'z', axis=1, tiled=True)  31.6 us
    ppermute x16, waiting for transfers between devices, passed_along(): lax.ppermute(value, axis, [(source, source + steps) for source in range(f...  27.3 us
    psum x4, blocking collectives, local(): logit_part = lax.psum(logit_part, axis)  26.8 us
    all_to_all x1, starting transfers between devices, local(): lax.all_to_all(payload.reshape(rows + 1, n_z, piece), 'z', 1, 1, tiled=True)  16.6 us
    dot_general x4, matrix products, local(): jnp.einsum('grqk,qgrd->kgd', probabilities, d_cols, preferred_element_typ...  12.4 us
  transfers between devices with their start and end apart: 19, of which 9 were waited for; matrix products, arithmetic and copies ran while one was open for 6% of the time, Pallas kernels for 0%

profile of v7, /device:TPU:6, one launch (start us, length us, event | category | flops | bytes accessed | tf_op | source)
XLA Modules:
  0.0 327.6 jit_solution(11724854656255010785)
XLA Ops:
  1.9 5.1 %collective-permute-start = (bf16[128,1024]{0,1:T(8,128)(2,1)S(1)}, bf16[128,1024]{0,1:T(8,128)(2,1)}, u32[]{:S(2)}, u32[]{:S(2)}) collective-permute-start(bf16[128,1024]{0,1:T(8,128)(2,1)S(1)} %copy.151), channel_id=1, source_target_pairs={{0,8},{1,9},{2,10},{3,11},{4,12},{5,13},{6,14},{7,15},{8,16},{9,17... | collective-permute-start | bytes 786440 | tf_op jit(solution)/shard_map/ppermute | solution.py:26
  7.0 3.0 collective-permute-start.1
  10.0 5.6 %collective-permute-start.2 = (bf16[128,1024]{0,1:T(8,128)(2,1)S(1)}, bf16[128,1024]{0,1:T(8,128)(2,1)S(1)}, u32[]{:S(2)}, u32[]{:S(2)}) collective-permute-start(bf16[128,1024]{0,1:T(8,128)(2,1)S(1)} %copy.151), channel_id=1, source_target_pairs={{0,6},{1,7},{2,8},{3,9},{4,10},{5,11},{6,12},{7,13},{8,14},{9,15},... | collective-permute-start | bytes 786440 | tf_op jit(solution)/shard_map/ppermute | solution.py:26
  15.6 2.3 collective-permute-start.3
  17.9 3.7 %collective-permute-start.4 = (bf16[128,1024]{0,1:T(8,128)(2,1)S(1)}, bf16[128,1024]{0,1:T(8,128)(2,1)S(1)}, u32[]{:S(2)}, u32[]{:S(2)}) collective-permute-start(bf16[128,1024]{0,1:T(8,128)(2,1)S(1)} %copy.151), channel_id=1, source_target_pairs={{0,4},{1,5},{2,6},{3,7},{4,8},{5,9},{6,10},{7,11},{8,12},{9,13},{1... | collective-permute-start | bytes 786440 | tf_op jit(solution)/shard_map/ppermute | solution.py:26
  31.5 2.5 collective-permute-start.5
  35.1 4.4 %collective-permute-start.6 = (bf16[128,1024]{0,1:T(8,128)(2,1)S(1)}, bf16[128,1024]{0,1:T(8,128)(2,1)S(1)}, u32[]{:S(2)}, u32[]{:S(2)}) collective-permute-start(bf16[128,1024]{0,1:T(8,128)(2,1)S(1)} %copy.151), channel_id=1, source_target_pairs={{0,2},{1,3},{2,4},{3,5},{4,6},{5,7},{6,8},{7,9},{8,10},{9,11},{10,... | collective-permute-start | bytes 786440 | tf_op jit(solution)/shard_map/ppermute | solution.py:26
  40.4 1.9 collective-permute-start.7
  42.8 3.3 %collective-permute-done.6 = bf16[128,1024]{0,1:T(8,128)(2,1)S(1)} collective-permute-done((bf16[128,1024]{0,1:T(8,128)(2,1)S(1)}, bf16[128,1024]{0,1:T(8,128)(2,1)S(1)}, u32[]{:S(2)}, u32[]{:S(2)}) %collective-permute-start.6) | collective-permute-done | bytes 262176 | tf_op jit(solution)/shard_map/ppermute | solution.py:26
  46.2 2.7 collective-permute-done.7
  50.3 1.6 fusion.80
  51.9 2.4 fusion.24
  54.4 2.6 fusion.79
  57.0 3.5 %fusion.25 = f32[2,1152,128,1]{1,2,3,0:T(8,128)} fusion(bf16[128,2,2,128]{0,3,2,1:T(8,128)(2,1)} %bitcast.165, f32[2,2,128]{2,1,0:T(2,128)} %fusion.79, bf16[1152,2,128,1]{0,2,3,1:T(8,128)(2,1)} %bitcast.154, bf16[128,2,2,128]{0,3,2,1:T(8,128)(2,1)S(1)} %bitcast.164, pred[128,1152]{0,1:T(8,128)(4,1)S(1)} %copy-done.5), kind=kOutput, calls=%fused_computation.36 | convolution fusion | flops 304940672 | bytes 2181120 | tf_op jit(solution)/shard_map/grqk,qgrd->kgd/dot_general | solution.py:70
  60.5 2.6 fusion.78
  63.1 3.5 %fusion.26 = f32[2,1152,128,1]{1,2,3,0:T(8,128)} fusion(bf16[128,2,2,128]{0,3,2,1:T(8,128)(2,1)} %bitcast.162, f32[2,2,128]{2,1,0:T(2,128)} %fusion.78, bf16[1152,2,128,1]{0,2,3,1:T(8,128)(2,1)} %bitcast.152, bf16[128,2,2,128]{0,3,2,1:T(8,128)(2,1)S(1)} %bitcast.161, pred[128,1152]{0,1:T(8,128)(4,1)S(1)} %copy-done.5), kind=kOutput, calls=%fused_computation.37 | convolution fusion | flops 304940672 | bytes 2181120 | tf_op jit(solution)/shard_map/grqk,qgrd->kgd/dot_general | solution.py:70
  66.7 1.6 fusion.77
  68.3 3.0 fusion.27
  71.3 2.2 fusion.71
  73.9 6.2 %collective-permute-start.10 = (bf16[128,1024]{0,1:T(8,128)(2,1)S(1)}, bf16[128,1024]{0,1:T(8,128)(2,1)S(1)}, u32[]{:S(2)}, u32[]{:S(2)}) collective-permute-start(bf16[128,1024]{0,1:T(8,128)(2,1)S(1)} %get-tuple-element.14), channel_id=1, source_target_pairs={{3,0},{4,1},{5,2},{6,3},{7,4},{8,5},{9,6},{10,7},{11,8},{12,9},{13... | collective-permute-start | bytes 786440 | tf_op jit(solution)/shard_map/ppermute | solution.py:26
  80.1 4.0 %collective-permute-start.11 = (bf16[128,1024]{0,1:T(8,128)(2,1)S(1)}, bf16[128,1024]{0,1:T(8,128)(2,1)S(1)}, u32[]{:S(2)}, u32[]{:S(2)}) collective-permute-start(bf16[128,1024]{0,1:T(8,128)(2,1)S(1)} %get-tuple-element.13), channel_id=1, source_target_pairs={{4,0},{5,1},{6,2},{7,3},{8,4},{9,5},{10,6},{11,7},{12,8},{13,9},{1... | collective-permute-start | bytes 786440 | tf_op jit(solution)/shard_map/ppermute | solution.py:26
  84.2 1.9 collective-permute-start.12
  86.1 2.9 collective-permute-start.13
  89.0 1.9 collective-permute-start.14
  90.9 1.9 collective-permute-start.15
  92.9 2.8 collective-permute-done.11
  95.7 9.2 %collective-permute-start.8 = (bf16[128,1024]{0,1:T(8,128)(2,1)S(1)}, bf16[128,1024]{0,1:T(8,128)(2,1)S(1)}, u32[]{:S(2)}, u32[]{:S(2)}) collective-permute-start(bf16[128,1024]{0,1:T(8,128)(2,1)S(1)} %get-tuple-element.8), channel_id=1, source_target_pairs={{1,0},{2,1},{3,2},{4,3},{5,4},{6,5},{7,6},{8,7},{9,8},{10,9},{11,1... | collective-permute-start | bytes 786440 | tf_op jit(solution)/shard_map/ppermute | solution.py:26
  104.9 4.0 %collective-permute-done.12 = bf16[128,1024]{0,1:T(8,128)(2,1)S(1)} collective-permute-done((bf16[128,1024]{0,1:T(8,128)(2,1)S(1)}, bf16[128,1024]{0,1:T(8,128)(2,1)S(1)}, u32[]{:S(2)}, u32[]{:S(2)}) %collective-permute-start.12) | collective-permute-done | bytes 262176 | tf_op jit(solution)/shard_map/ppermute | solution.py:26
  108.9 2.1 collective-permute-start.9
  111.3 3.3 %collective-permute-done.13 = bf16[128,1024]{0,1:T(8,128)(2,1)S(1)} collective-permute-done((bf16[128,1024]{0,1:T(8,128)(2,1)S(1)}, bf16[128,1024]{0,1:T(8,128)(2,1)S(1)}, u32[]{:S(2)}, u32[]{:S(2)}) %collective-permute-start.13) | collective-permute-done | bytes 262176 | tf_op jit(solution)/shard_map/ppermute | solution.py:26
  114.7 10.9 %collective-permute-done.9 = bf16[128,1024]{0,1:T(8,128)(2,1)S(1)} collective-permute-done((bf16[128,1024]{0,1:T(8,128)(2,1)S(1)}, bf16[128,1024]{0,1:T(8,128)(2,1)S(1)}, u32[]{:S(2)}, u32[]{:S(2)}) %collective-permute-start.9) | collective-permute-done | bytes 262176 | tf_op jit(solution)/shard_map/ppermute | solution.py:26
  126.1 2.5 broadcast_in_dim.43
  128.6 8.9 %all-to-all-start = ((bf16[16,128,1024]{2,1,0:T(8,128)(2,1)}), bf16[16,128,1024]{2,1,0:T(8,128)(2,1)}, u32[]{:S(2)}, u32[]{:S(2)}) async-start(bf16[16,128,1024]{2,1,0:T(8,128)(2,1)} %broadcast_in_dim.43), calls=%async_computation | async-start | bytes 8388608 | tf_op jit(solution)/shard_map/all_to_all | solution.py:89
  137.4 49.2 %all-to-all-done = bf16[16,128,1024]{2,1,0:T(8,128)(2,1)} async-done(((bf16[16,128,1024]{2,1,0:T(8,128)(2,1)}), bf16[16,128,1024]{2,1,0:T(8,128)(2,1)}, u32[]{:S(2)}, u32[]{:S(2)}) %all-to-all-start) | async-done | bytes 4194336 | tf_op jit(solution)/shard_map/all_to_all | solution.py:89
  186.6 3.8 %fusion.81 = f32[1024,336]{0,1:T(8,128)S(1)} fusion(bf16[336,2048]{1,0:T(8,128)(2,1)S(1)} %copy-done, bf16[2048,1024]{1,0:T(8,128)(2,1)} %bitcast.36), kind=kOutput, calls=%fused_computation.107 | convolution fusion | flops 1409286144 | bytes 6946816 | tf_op jit(solution)/shard_map/dot_general | solution.py:92
  191.3 2.7 collective-permute-start.16
  195.4 1.6 copy.182
  197.0 2.2 fusion.23
  199.3 2.5 psum.28
  201.7 8.3 %psum.29 = f32[1024]{0:T(1024)S(1)} all-reduce(f32[1024]{0:T(1024)S(1)} %psum.28), channel_id=1, replica_groups=mesh['z'=16,'xh'=2,'y'=4,'xl'=2,'c'=2] {'xl'}, use_global_device_ids=true, to_apply=%region_10.11 | all-reduce | flops 1024 | bytes 8192 | tf_op jit(solution)/shard_map/psum | solution.py:109
  210.1 9.2 %psum.30 = f32[1024]{0:T(1024)S(1)} all-reduce(f32[1024]{0:T(1024)S(1)} %psum.29), channel_id=1, replica_groups=mesh['z'=16,'xh'=2,'y'=4,'xl'=2,'c'=2] {'y'}, use_global_device_ids=true, to_apply=%region_11.12 | all-reduce | flops 1024 | bytes 8192 | tf_op jit(solution)/shard_map/psum | solution.py:109
  219.3 6.7 %psum.31 = f32[1024]{0:T(1024)S(1)} all-reduce(f32[1024]{0:T(1024)S(1)} %psum.30), channel_id=1, replica_groups=mesh['z'=16,'xh'=2,'y'=4,'xl'=2,'c'=2] {'xh'}, use_global_device_ids=true, to_apply=%region_12.13 | all-reduce | flops 1024 | bytes 8192 | tf_op jit(solution)/shard_map/psum | solution.py:109
  227.0 2.1 bitcast_add_fusion
  230.5 2.0 pad_maximum_fusion.1
  232.4 16.6 %all-to-all-start.1 = ((f32[337,16,32]{0,2,1:T(8,128)}), f32[337,16,32]{0,2,1:T(8,128)S(1)}, u32[]{:S(2)}, u32[]{:S(2)}) async-start(f32[337,16,32]{0,2,1:T(8,128)} %pad_maximum_fusion.1), calls=%async_computation.1 | async-start | bytes 1572864 | tf_op jit(solution)/shard_map/all_to_all | solution.py:112
  249.3 34.1 %all-to-all-done.1 = f32[337,16,32]{0,2,1:T(8,128)S(1)} async-done(((f32[337,16,32]{0,2,1:T(8,128)}), f32[337,16,32]{0,2,1:T(8,128)S(1)}, u32[]{:S(2)}, u32[]{:S(2)}) %all-to-all-start.1) | async-done | bytes 690208 | tf_op jit(solution)/shard_map/all_to_all | solution.py:112
  284.0 31.6 %all_gather.6 = bf16[338,512]{0,1:T(8,128)(2,1)S(1)} all-gather(bf16[338,32]{0,1:T(8,128)(2,1)S(1)} %pad_maximum_fusion.2), channel_id=1, replica_groups=mesh['z'=16,'xh'=2,'y'=4,'xl'=2,'c'=2] {'z'}, dimensions={1}, use_global_device_ids=true | all-gather | bytes 367744 | tf_op jit(solution)/shard_map/all_gather | solution.py:124
  315.6 9.9 %all_gather.7 = bf16[338,1024]{0,1:T(8,128)(2,1)S(1)} all-gather(bf16[338,512]{0,1:T(8,128)(2,1)S(1)} %all_gather.6), channel_id=1, replica_groups=mesh['z'=16,'xh'=2,'y'=4,'xl'=2,'c'=2] {'xh'}, dimensions={1}, use_global_device_ids=true | all-gather | bytes 1038336 | tf_op jit(solution)/shard_map/all_gather | solution.py:125
  (81 shorter events, 23.8 us)
Async XLA Ops:
  0.6 186.0 %copy-start = (bf16[336,2048]{1,0:T(8,128)(2,1)S(1)}, bf16[336,2048]{1,0:T(8,128)(2,1)}, u32[]{:S(2)}) copy-start(bf16[336,2048]{1,0:T(8,128)(2,1)} %param.6) | copy-start | bytes 4128772
  1.9 29.6 %collective-permute-start = (bf16[128,1024]{0,1:T(8,128)(2,1)S(1)}, bf16[128,1024]{0,1:T(8,128)(2,1)}, u32[]{:S(2)}, u32[]{:S(2)}) collective-permute-start(bf16[128,1024]{0,1:T(8,128)(2,1)S(1)} %copy.151), channel_id=1, source_target_pairs={{0,8},{1,9},{2,10},{3,11},{4,12},{5,13},{6,14},{7,15},{8,16},{9,17... | collective-permute-start | bytes 786440 | tf_op jit(solution)/shard_map/ppermute | solution.py:26
  7.0 28.1 %collective-permute-start.1 = (bf16[128,1024]{0,1:T(8,128)(2,1)S(1)}, bf16[128,1024]{0,1:T(8,128)(2,1)}, u32[]{:S(2)}, u32[]{:S(2)}) collective-permute-start(bf16[128,1024]{0,1:T(8,128)(2,1)S(1)} %copy.151), channel_id=1, source_target_pairs={{0,7},{1,8},{2,9},{3,10},{4,11},{5,12},{6,13},{7,14},{8,15},{9,16}... | collective-permute-start | bytes 786440 | tf_op jit(solution)/shard_map/ppermute | solution.py:26
  10.0 30.5 %collective-permute-start.2 = (bf16[128,1024]{0,1:T(8,128)(2,1)S(1)}, bf16[128,1024]{0,1:T(8,128)(2,1)S(1)}, u32[]{:S(2)}, u32[]{:S(2)}) collective-permute-start(bf16[128,1024]{0,1:T(8,128)(2,1)S(1)} %copy.151), channel_id=1, source_target_pairs={{0,6},{1,7},{2,8},{3,9},{4,10},{5,11},{6,12},{7,13},{8,14},{9,15},... | collective-permute-start | bytes 786440 | tf_op jit(solution)/shard_map/ppermute | solution.py:26
  15.6 26.9 %collective-permute-start.3 = (bf16[128,1024]{0,1:T(8,128)(2,1)S(1)}, bf16[128,1024]{0,1:T(8,128)(2,1)S(1)}, u32[]{:S(2)}, u32[]{:S(2)}) collective-permute-start(bf16[128,1024]{0,1:T(8,128)(2,1)S(1)} %copy.151), channel_id=1, source_target_pairs={{0,5},{1,6},{2,7},{3,8},{4,9},{5,10},{6,11},{7,12},{8,13},{9,14},{... | collective-permute-start | bytes 786440 | tf_op jit(solution)/shard_map/ppermute | solution.py:26
  17.9 24.6 %collective-permute-start.4 = (bf16[128,1024]{0,1:T(8,128)(2,1)S(1)}, bf16[128,1024]{0,1:T(8,128)(2,1)S(1)}, u32[]{:S(2)}, u32[]{:S(2)}) collective-permute-start(bf16[128,1024]{0,1:T(8,128)(2,1)S(1)} %copy.151), channel_id=1, source_target_pairs={{0,4},{1,5},{2,6},{3,7},{4,8},{5,9},{6,10},{7,11},{8,12},{9,13},{1... | collective-permute-start | bytes 786440 | tf_op jit(solution)/shard_map/ppermute | solution.py:26
  31.5 11.3 %collective-permute-start.5 = (bf16[128,1024]{0,1:T(8,128)(2,1)S(1)}, bf16[128,1024]{0,1:T(8,128)(2,1)S(1)}, u32[]{:S(2)}, u32[]{:S(2)}) collective-permute-start(bf16[128,1024]{0,1:T(8,128)(2,1)S(1)} %copy.151), channel_id=1, source_target_pairs={{0,3},{1,4},{2,5},{3,6},{4,7},{5,8},{6,9},{7,10},{8,11},{9,12},{10... | collective-permute-start | bytes 786440 | tf_op jit(solution)/shard_map/ppermute | solution.py:26
  35.1 11.1 %collective-permute-start.6 = (bf16[128,1024]{0,1:T(8,128)(2,1)S(1)}, bf16[128,1024]{0,1:T(8,128)(2,1)S(1)}, u32[]{:S(2)}, u32[]{:S(2)}) collective-permute-start(bf16[128,1024]{0,1:T(8,128)(2,1)S(1)} %copy.151), channel_id=1, source_target_pairs={{0,2},{1,3},{2,4},{3,5},{4,6},{5,7},{6,8},{7,9},{8,10},{9,11},{10,... | collective-permute-start | bytes 786440 | tf_op jit(solution)/shard_map/ppermute | solution.py:26
  40.4 8.5 %collective-permute-start.7 = (bf16[128,1024]{0,1:T(8,128)(2,1)S(1)}, bf16[128,1024]{0,1:T(8,128)(2,1)S(1)}, u32[]{:S(2)}, u32[]{:S(2)}) collective-permute-start(bf16[128,1024]{0,1:T(8,128)(2,1)S(1)} %copy.151), channel_id=1, source_target_pairs={{0,1},{1,2},{2,3},{3,4},{4,5},{5,6},{6,7},{7,8},{8,9},{9,10},{10,1... | collective-permute-start | bytes 786440 | tf_op jit(solution)/shard_map/ppermute | solution.py:26
  49.1 1.2 copy-start.5
  49.1 1.2 copy-start.10
  50.3 1.6 copy-start.4
  51.9 2.5 copy-start.9
  57.0 3.5 %copy-start.8 = (bf16[128,512]{0,1:T(8,128)(2,1)S(1)}, bf16[128,512]{0,1:T(8,128)(2,1)}, u32[]{:S(2)}) copy-start(bf16[128,512]{0,1:T(8,128)(2,1)} %copy.214) | copy-start | bytes 393220
  63.1 3.5 %copy-start.6 = (bf16[128,512]{0,1:T(8,128)(2,1)S(1)}, bf16[128,512]{0,1:T(8,128)(2,1)}, u32[]{:S(2)}) copy-start(bf16[128,512]{0,1:T(8,128)(2,1)} %copy.215) | copy-start | bytes 393220
  66.6 1.6 copy-start.7
  73.5 37.5 %copy-start.1 = (f32[2,1152,128,1]{1,2,3,0:T(8,128)S(1)}, f32[2,1152,128,1]{1,2,3,0:T(8,128)}, u32[]{:S(2)}) copy-start(f32[2,1152,128,1]{1,2,3,0:T(8,128)} %fusion.25) | copy-start | bytes 3538948
  73.5 37.5 %copy-start.2 = (f32[2,1152,128,1]{1,2,3,0:T(8,128)S(1)}, f32[2,1152,128,1]{1,2,3,0:T(8,128)}, u32[]{:S(2)}) copy-start(f32[2,1152,128,1]{1,2,3,0:T(8,128)} %fusion.26) | copy-start | bytes 3538948
  73.5 37.5 %copy-start.3 = (f32[2,1152,128,1]{1,2,3,0:T(8,128)S(1)}, f32[2,1152,128,1]{1,2,3,0:T(8,128)}, u32[]{:S(2)}) copy-start(f32[2,1152,128,1]{1,2,3,0:T(8,128)} %fusion.27) | copy-start | bytes 3538948
  73.9 17.0 %collective-permute-start.10 = (bf16[128,1024]{0,1:T(8,128)(2,1)S(1)}, bf16[128,1024]{0,1:T(8,128)(2,1)S(1)}, u32[]{:S(2)}, u32[]{:S(2)}) collective-permute-start(bf16[128,1024]{0,1:T(8,128)(2,1)S(1)} %get-tuple-element.14), channel_id=1, source_target_pairs={{3,0},{4,1},{5,2},{6,3},{7,4},{8,5},{9,6},{10,7},{11,8},{12,9},{13... | collective-permute-start | bytes 786440 | tf_op jit(solution)/shard_map/ppermute | solution.py:26
  80.1 15.5 %collective-permute-start.11 = (bf16[128,1024]{0,1:T(8,128)(2,1)S(1)}, bf16[128,1024]{0,1:T(8,128)(2,1)S(1)}, u32[]{:S(2)}, u32[]{:S(2)}) collective-permute-start(bf16[128,1024]{0,1:T(8,128)(2,1)S(1)} %get-tuple-element.13), channel_id=1, source_target_pairs={{4,0},{5,1},{6,2},{7,3},{8,4},{9,5},{10,6},{11,7},{12,8},{13,9},{1... | collective-permute-start | bytes 786440 | tf_op jit(solution)/shard_map/ppermute | solution.py:26
  84.2 24.7 %collective-permute-start.12 = (bf16[128,1024]{0,1:T(8,128)(2,1)S(1)}, bf16[128,1024]{0,1:T(8,128)(2,1)S(1)}, u32[]{:S(2)}, u32[]{:S(2)}) collective-permute-start(bf16[128,1024]{0,1:T(8,128)(2,1)S(1)} %get-tuple-element.12), channel_id=1, source_target_pairs={{5,0},{6,1},{7,2},{8,3},{9,4},{10,5},{11,6},{12,7},{13,8},{14,9},{... | collective-permute-start | bytes 786440 | tf_op jit(solution)/shard_map/ppermute | solution.py:26
  86.1 28.5 %collective-permute-start.13 = (bf16[128,1024]{0,1:T(8,128)(2,1)S(1)}, bf16[128,1024]{0,1:T(8,128)(2,1)S(1)}, u32[]{:S(2)}, u32[]{:S(2)}) collective-permute-start(bf16[128,1024]{0,1:T(8,128)(2,1)S(1)} %get-tuple-element.11), channel_id=1, source_target_pairs={{6,0},{7,1},{8,2},{9,3},{10,4},{11,5},{12,6},{13,7},{14,8},{15,9},... | collective-permute-start | bytes 786440 | tf_op jit(solution)/shard_map/ppermute | solution.py:26
  89.0 25.7 %collective-permute-start.14 = (bf16[128,1024]{0,1:T(8,128)(2,1)S(1)}, bf16[128,1024]{0,1:T(8,128)(2,1)S(1)}, u32[]{:S(2)}, u32[]{:S(2)}) collective-permute-start(bf16[128,1024]{0,1:T(8,128)(2,1)S(1)} %get-tuple-element.10), channel_id=1, source_target_pairs={{7,0},{8,1},{9,2},{10,3},{11,4},{12,5},{13,6},{14,7},{15,8},{16,9}... | collective-permute-start | bytes 786440 | tf_op jit(solution)/shard_map/ppermute | solution.py:26
  90.9 23.7 %collective-permute-start.15 = (bf16[128,1024]{0,1:T(8,128)(2,1)S(1)}, bf16[128,1024]{0,1:T(8,128)(2,1)S(1)}, u32[]{:S(2)}, u32[]{:S(2)}) collective-permute-start(bf16[128,1024]{0,1:T(8,128)(2,1)S(1)} %get-tuple-element.9), channel_id=1, source_target_pairs={{8,0},{9,1},{10,2},{11,3},{12,4},{13,5},{14,6},{15,7},{16,8},{17,9... | collective-permute-start | bytes 786440 | tf_op jit(solution)/shard_map/ppermute | solution.py:26
  95.7 19.0 %collective-permute-start.8 = (bf16[128,1024]{0,1:T(8,128)(2,1)S(1)}, bf16[128,1024]{0,1:T(8,128)(2,1)S(1)}, u32[]{:S(2)}, u32[]{:S(2)}) collective-permute-start(bf16[128,1024]{0,1:T(8,128)(2,1)S(1)} %get-tuple-element.8), channel_id=1, source_target_pairs={{1,0},{2,1},{3,2},{4,3},{5,4},{6,5},{7,6},{8,7},{9,8},{10,9},{11,1... | collective-permute-start | bytes 786440 | tf_op jit(solution)/shard_map/ppermute | solution.py:26
  108.9 16.7 %collective-permute-start.9 = (bf16[128,1024]{0,1:T(8,128)(2,1)S(1)}, bf16[128,1024]{0,1:T(8,128)(2,1)S(1)}, u32[]{:S(2)}, u32[]{:S(2)}) collective-permute-start(bf16[128,1024]{0,1:T(8,128)(2,1)S(1)} %get-tuple-element.15), channel_id=1, source_target_pairs={{2,0},{3,1},{4,2},{5,3},{6,4},{7,5},{8,6},{9,7},{10,8},{11,9},{12,... | collective-permute-start | bytes 786440 | tf_op jit(solution)/shard_map/ppermute | solution.py:26
  128.6 58.0 %all-to-all-start = ((bf16[16,128,1024]{2,1,0:T(8,128)(2,1)}), bf16[16,128,1024]{2,1,0:T(8,128)(2,1)}, u32[]{:S(2)}, u32[]{:S(2)}) async-start(bf16[16,128,1024]{2,1,0:T(8,128)(2,1)} %broadcast_in_dim.43), calls=%async_computation | async-start | bytes 8388608 | tf_op jit(solution)/shard_map/all_to_all | solution.py:89
  191.3 5.8 %copy-start.11 = (f32[1024]{0:T(1024)S(1)}, f32[1024]{0:T(1024)}, u32[]{:S(2)}) copy-start(f32[1024]{0:T(1024)} %param.8) | copy-start | bytes 12292
  191.3 35.7 %collective-permute-start.16 = (f32[336,512]{1,0:T(8,128)}, f32[336,512]{1,0:T(8,128)}, u32[]{:S(2)}, u32[]{:S(2)}) collective-permute-start(f32[336,512]{1,0:T(8,128)} %dynamic-slice_bitcast_fusion), channel_id=1, source_target_pairs={{0,16},{16,0},{1,17},{17,1},{2,18},{18,2},{3,19},{19,3},{4,20},{20... | collective-permute-start | bytes 2064392 | tf_op jit(solution)/shard_map/ppermute | solution.py:107
  232.4 51.0 %all-to-all-start.1 = ((f32[337,16,32]{0,2,1:T(8,128)}), f32[337,16,32]{0,2,1:T(8,128)S(1)}, u32[]{:S(2)}, u32[]{:S(2)}) async-start(f32[337,16,32]{0,2,1:T(8,128)} %pad_maximum_fusion.1), calls=%async_computation.1 | async-start | bytes 1572864 | tf_op jit(solution)/shard_map/all_to_all | solution.py:112

commit v8 on v7

--- a/solution.py
+++ b/solution.py
@@ -24,6 +24,18 @@
 def passed_along(value, axis, count, steps):
     first, last = (max(0, -steps), min(count, count - steps))
     return lax.ppermute(value, axis, [(source, source + steps) for source in range(first, last)])
+
+
+def doubling_gather(value, axis, count, index):
+    step = 1
+    while step < count:
+        other = lax.ppermute(value, axis, [(i, i ^ step) for i in range(count)])
+        low = (index & step) == 0
+        value = jnp.where(
+            low, jnp.concatenate([value, other], axis=1), jnp.concatenate([other, value], axis=1)
+        )
+        step *= 2
+    return value
 
 
 def make_local(sizes):
@@ -121,8 +133,8 @@
         logit_hi = logit_piece.astype(jnp.bfloat16)
         logit_lo = (logit_piece - logit_hi.astype(jnp.float32)).astype(jnp.bfloat16)
         out_piece = jnp.concatenate([weight_piece, logit_hi, logit_lo], axis=0)
-        out_piece = lax.all_gather(out_piece, "z", axis=1, tiled=True)
-        out_full = lax.all_gather(out_piece, "xh", axis=1, tiled=True)
+        out_full = doubling_gather(out_piece, "z", n_z, z_index)
+        out_full = doubling_gather(out_full, "xh", 2, xh_index)
         grad_weight = out_full[:rows]
         logit_sum = out_full[rows].astype(jnp.float32) + out_full[rows + 1].astype(jnp.float32)
         grad_logit = -logit_sum * threshold * (1.0 - threshold)

time: 332 us -> 350 us (1.054)
  blocking collectives: 68.3 us -> 26.8 us
  waiting for transfers between devices: 111 us -> 143 us
  starting transfers between devices: 86.8 us -> 113 us
    all_gather x2 -> x0, blocking collectives: 41.6 us -> none  [the longest x1 31.6 us: local(): out_piece = lax.all_gather(out_piece, 'z', axis=1, tiled=True)]
    ppermute x0 -> x5, waiting for transfers between devices: none -> 32.9 us  [doubling_gather(): other = lax.ppermute(value, axis, [(i, i ^ step) for i in range(count)])]
    ppermute x0 -> x5, starting transfers between devices: none -> 25.7 us  [doubling_gather(): other = lax.ppermute(value, axis, [(i, i ^ step) for i in range(count)])]
  transfers between devices with their start and end apart: 19 -> 24, of which waited for: 9 -> 14; matrix products, arithmetic and copies ran while one was open for 6% -> 6% of each run, Pallas kernels for 0% -> 0%
where the time goes in v8:
time: 350 us; the launch traced here: 345 us
  waiting for transfers between devices  143 us (41%)
  starting transfers between devices  113 us (32%)
  blocking collectives  26.8 us (8%)
  matrix products  24.7 us (7%)
  local copies, waits for them, and re-layouts  24.1 us (7%)
  other arithmetic  12.6 us (4%)
    ppermute x16, starting transfers between devices, passed_along(): lax.ppermute(value, axis, [(source, source + steps) for source in range(f...  58.7 us
    all_to_all x1, waiting for transfers between devices, local(): lax.all_to_all(spread, FSDP, 0, 0, tiled=True)  49.2 us
    all_to_all x1, waiting for transfers between devices, local(): lax.all_to_all(payload.reshape(rows + 1, n_z, piece), 'z', 1, 1, tiled=True)  34.1 us
    ppermute x5, waiting for transfers between devices, doubling_gather(): other = lax.ppermute(value, axis, [(i, i ^ step) for i in range(count)])  32.9 us
    ppermute x16, waiting for transfers between devices, passed_along(): lax.ppermute(value, axis, [(source, source + steps) for source in range(f...  27.3 us
    psum x4, blocking collectives, local(): logit_part = lax.psum(logit_part, axis)  26.8 us
    ppermute x5, starting transfers between devices, doubling_gather(): other = lax.ppermute(value, axis, [(i, i ^ step) for i in range(count)])  25.7 us
    all_to_all x1, starting transfers between devices, local(): lax.all_to_all(payload.reshape(rows + 1, n_z, piece), 'z', 1, 1, tiled=True)  16.6 us
  transfers between devices with their start and end apart: 24, of which 14 were waited for; matrix products, arithmetic and copies ran while one was open for 6% of the time, Pallas kernels for 0%

profile of v8, /device:TPU:6, one launch (start us, length us, event | category | flops | bytes accessed | tf_op | source)
XLA Modules:
  0.0 345.4 jit_solution(15782870251890263004)
XLA Ops:
  1.9 5.1 %collective-permute-start = (bf16[128,1024]{0,1:T(8,128)(2,1)S(1)}, bf16[128,1024]{0,1:T(8,128)(2,1)}, u32[]{:S(2)}, u32[]{:S(2)}) collective-permute-start(bf16[128,1024]{0,1:T(8,128)(2,1)S(1)} %copy.151), channel_id=1, source_target_pairs={{0,8},{1,9},{2,10},{3,11},{4,12},{5,13},{6,14},{7,15},{8,16},{9,17... | collective-permute-start | bytes 786440 | tf_op jit(solution)/shard_map/ppermute | solution.py:26
  7.0 3.0 collective-permute-start.1
  10.0 5.6 %collective-permute-start.2 = (bf16[128,1024]{0,1:T(8,128)(2,1)S(1)}, bf16[128,1024]{0,1:T(8,128)(2,1)S(1)}, u32[]{:S(2)}, u32[]{:S(2)}) collective-permute-start(bf16[128,1024]{0,1:T(8,128)(2,1)S(1)} %copy.151), channel_id=1, source_target_pairs={{0,6},{1,7},{2,8},{3,9},{4,10},{5,11},{6,12},{7,13},{8,14},{9,15},... | collective-permute-start | bytes 786440 | tf_op jit(solution)/shard_map/ppermute | solution.py:26
  15.6 2.3 collective-permute-start.3
  17.9 3.7 %collective-permute-start.4 = (bf16[128,1024]{0,1:T(8,128)(2,1)S(1)}, bf16[128,1024]{0,1:T(8,128)(2,1)S(1)}, u32[]{:S(2)}, u32[]{:S(2)}) collective-permute-start(bf16[128,1024]{0,1:T(8,128)(2,1)S(1)} %copy.151), channel_id=1, source_target_pairs={{0,4},{1,5},{2,6},{3,7},{4,8},{5,9},{6,10},{7,11},{8,12},{9,13},{1... | collective-permute-start | bytes 786440 | tf_op jit(solution)/shard_map/ppermute | solution.py:26
  31.5 2.5 collective-permute-start.5
  35.1 4.4 %collective-permute-start.6 = (bf16[128,1024]{0,1:T(8,128)(2,1)S(1)}, bf16[128,1024]{0,1:T(8,128)(2,1)S(1)}, u32[]{:S(2)}, u32[]{:S(2)}) collective-permute-start(bf16[128,1024]{0,1:T(8,128)(2,1)S(1)} %copy.151), channel_id=1, source_target_pairs={{0,2},{1,3},{2,4},{3,5},{4,6},{5,7},{6,8},{7,9},{8,10},{9,11},{10,... | collective-permute-start | bytes 786440 | tf_op jit(solution)/shard_map/ppermute | solution.py:26
  42.8 3.3 collective-permute-done.6
  46.2 2.7 collective-permute-done.7
  51.9 2.4 fusion.24
  54.4 2.6 fusion.79
  57.0 3.5 %fusion.25 = f32[2,1152,128,1]{1,2,3,0:T(8,128)} fusion(bf16[128,2,2,128]{0,3,2,1:T(8,128)(2,1)} %bitcast.165, f32[2,2,128]{2,1,0:T(2,128)} %fusion.79, bf16[1152,2,128,1]{0,2,3,1:T(8,128)(2,1)} %bitcast.154, bf16[128,2,2,128]{0,3,2,1:T(8,128)(2,1)S(1)} %bitcast.164, pred[128,1152]{0,1:T(8,128)(4,1)S(1)} %copy-done.5), kind=kOutput, calls=%fused_computation.36 | convolution fusion | flops 304940672 | bytes 2181120 | tf_op jit(solution)/shard_map/grqk,qgrd->kgd/dot_general | solution.py:82
  60.5 2.6 fusion.78
  63.1 3.5 %fusion.26 = f32[2,1152,128,1]{1,2,3,0:T(8,128)} fusion(bf16[128,2,2,128]{0,3,2,1:T(8,128)(2,1)} %bitcast.162, f32[2,2,128]{2,1,0:T(2,128)} %fusion.78, bf16[1152,2,128,1]{0,2,3,1:T(8,128)(2,1)} %bitcast.152, bf16[128,2,2,128]{0,3,2,1:T(8,128)(2,1)S(1)} %bitcast.161, pred[128,1152]{0,1:T(8,128)(4,1)S(1)} %copy-done.5), kind=kOutput, calls=%fused_computation.37 | convolution fusion | flops 304940672 | bytes 2181120 | tf_op jit(solution)/shard_map/grqk,qgrd->kgd/dot_general | solution.py:82
  68.3 3.0 fusion.27
  71.3 2.2 fusion.71
  73.9 6.2 %collective-permute-start.10 = (bf16[128,1024]{0,1:T(8,128)(2,1)S(1)}, bf16[128,1024]{0,1:T(8,128)(2,1)S(1)}, u32[]{:S(2)}, u32[]{:S(2)}) collective-permute-start(bf16[128,1024]{0,1:T(8,128)(2,1)S(1)} %get-tuple-element.14), channel_id=1, source_target_pairs={{3,0},{4,1},{5,2},{6,3},{7,4},{8,5},{9,6},{10,7},{11,8},{12,9},{13... | collective-permute-start | bytes 786440 | tf_op jit(solution)/shard_map/ppermute | solution.py:26
  80.1 4.0 %collective-permute-start.11 = (bf16[128,1024]{0,1:T(8,128)(2,1)S(1)}, bf16[128,1024]{0,1:T(8,128)(2,1)S(1)}, u32[]{:S(2)}, u32[]{:S(2)}) collective-permute-start(bf16[128,1024]{0,1:T(8,128)(2,1)S(1)} %get-tuple-element.13), channel_id=1, source_target_pairs={{4,0},{5,1},{6,2},{7,3},{8,4},{9,5},{10,6},{11,7},{12,8},{13,9},{1... | collective-permute-start | bytes 786440 | tf_op jit(solution)/shard_map/ppermute | solution.py:26
  86.1 2.9 collective-permute-start.13
  92.9 2.8 collective-permute-done.11
  95.7 9.2 %collective-permute-start.8 = (bf16[128,1024]{0,1:T(8,128)(2,1)S(1)}, bf16[128,1024]{0,1:T(8,128)(2,1)S(1)}, u32[]{:S(2)}, u32[]{:S(2)}) collective-permute-start(bf16[128,1024]{0,1:T(8,128)(2,1)S(1)} %get-tuple-element.8), channel_id=1, source_target_pairs={{1,0},{2,1},{3,2},{4,3},{5,4},{6,5},{7,6},{8,7},{9,8},{10,9},{11,1... | collective-permute-start | bytes 786440 | tf_op jit(solution)/shard_map/ppermute | solution.py:26
  104.9 4.0 %collective-permute-done.12 = bf16[128,1024]{0,1:T(8,128)(2,1)S(1)} collective-permute-done((bf16[128,1024]{0,1:T(8,128)(2,1)S(1)}, bf16[128,1024]{0,1:T(8,128)(2,1)S(1)}, u32[]{:S(2)}, u32[]{:S(2)}) %collective-permute-start.12) | collective-permute-done | bytes 262176 | tf_op jit(solution)/shard_map/ppermute | solution.py:26
  108.9 2.1 collective-permute-start.9
  111.3 3.3 collective-permute-done.13
  114.7 10.9 %collective-permute-done.9 = bf16[128,1024]{0,1:T(8,128)(2,1)S(1)} collective-permute-done((bf16[128,1024]{0,1:T(8,128)(2,1)S(1)}, bf16[128,1024]{0,1:T(8,128)(2,1)S(1)}, u32[]{:S(2)}, u32[]{:S(2)}) %collective-permute-start.9) | collective-permute-done | bytes 262176 | tf_op jit(solution)/shard_map/ppermute | solution.py:26
  126.1 2.5 broadcast_in_dim.43
  128.6 8.9 %all-to-all-start = ((bf16[16,128,1024]{2,1,0:T(8,128)(2,1)}), bf16[16,128,1024]{2,1,0:T(8,128)(2,1)}, u32[]{:S(2)}, u32[]{:S(2)}) async-start(bf16[16,128,1024]{2,1,0:T(8,128)(2,1)} %broadcast_in_dim.43), calls=%async_computation | async-start | bytes 8388608 | tf_op jit(solution)/shard_map/all_to_all | solution.py:101
  137.4 49.2 %all-to-all-done = bf16[16,128,1024]{2,1,0:T(8,128)(2,1)} async-done(((bf16[16,128,1024]{2,1,0:T(8,128)(2,1)}), bf16[16,128,1024]{2,1,0:T(8,128)(2,1)}, u32[]{:S(2)}, u32[]{:S(2)}) %all-to-all-start) | async-done | bytes 4194336 | tf_op jit(solution)/shard_map/all_to_all | solution.py:101
  186.6 3.8 %fusion.81 = f32[1024,336]{0,1:T(8,128)S(1)} fusion(bf16[336,2048]{1,0:T(8,128)(2,1)S(1)} %copy-done, bf16[2048,1024]{1,0:T(8,128)(2,1)} %bitcast.36), kind=kOutput, calls=%fused_computation.112 | convolution fusion | flops 1409286144 | bytes 6946816 | tf_op jit(solution)/shard_map/dot_general | solution.py:104
  191.3 2.7 collective-permute-start.16
  197.0 2.2 fusion.23
  199.3 2.5 psum.28
  201.7 8.3 %psum.29 = f32[1024]{0:T(1024)S(1)} all-reduce(f32[1024]{0:T(1024)S(1)} %psum.28), channel_id=1, replica_groups=mesh['z'=16,'xh'=2,'y'=4,'xl'=2,'c'=2] {'xl'}, use_global_device_ids=true, to_apply=%region_10.11 | all-reduce | flops 1024 | bytes 8192 | tf_op jit(solution)/shard_map/psum | solution.py:121
  210.1 9.2 %psum.30 = f32[1024]{0:T(1024)S(1)} all-reduce(f32[1024]{0:T(1024)S(1)} %psum.29), channel_id=1, replica_groups=mesh['z'=16,'xh'=2,'y'=4,'xl'=2,'c'=2] {'y'}, use_global_device_ids=true, to_apply=%region_11.12 | all-reduce | flops 1024 | bytes 8192 | tf_op jit(solution)/shard_map/psum | solution.py:121
  219.3 6.7 %psum.31 = f32[1024]{0:T(1024)S(1)} all-reduce(f32[1024]{0:T(1024)S(1)} %psum.30), channel_id=1, replica_groups=mesh['z'=16,'xh'=2,'y'=4,'xl'=2,'c'=2] {'xh'}, use_global_device_ids=true, to_apply=%region_12.13 | all-reduce | flops 1024 | bytes 8192 | tf_op jit(solution)/shard_map/psum | solution.py:121
  227.0 2.1 bitcast_add_fusion
  230.5 2.0 pad_maximum_fusion.1
  232.4 16.6 %all-to-all-start.1 = ((f32[337,16,32]{0,2,1:T(8,128)}), f32[337,16,32]{0,2,1:T(8,128)S(1)}, u32[]{:S(2)}, u32[]{:S(2)}) async-start(f32[337,16,32]{0,2,1:T(8,128)} %pad_maximum_fusion.1), calls=%async_computation.1 | async-start | bytes 1572864 | tf_op jit(solution)/shard_map/all_to_all | solution.py:124
  249.3 34.1 %all-to-all-done.1 = f32[337,16,32]{0,2,1:T(8,128)S(1)} async-done(((f32[337,16,32]{0,2,1:T(8,128)}), f32[337,16,32]{0,2,1:T(8,128)S(1)}, u32[]{:S(2)}, u32[]{:S(2)}) %all-to-all-start.1) | async-done | bytes 690208 | tf_op jit(solution)/shard_map/all_to_all | solution.py:124
  284.0 3.7 %collective-permute-start.17 = (bf16[338,32]{0,1:T(8,128)(2,1)S(1)}, bf16[338,32]{0,1:T(8,128)(2,1)S(1)}, u32[]{:S(2)}, u32[]{:S(2)}) collective-permute-start(bf16[338,32]{0,1:T(8,128)(2,1)S(1)} %pad_maximum_fusion.2), channel_id=1, source_target_pairs={{0,32},{32,0},{64,96},{96,64},{128,160},{160,128},{192,224},{224,1... | collective-permute-start | bytes 64904 | tf_op jit(solution)/shard_map/ppermute | solution.py:32
  287.6 2.0 collective-permute-done.17
  289.8 5.4 %collective-permute-start.18 = (bf16[338,64]{0,1:T(8,128)(2,1)S(1)}, bf16[338,64]{0,1:T(8,128)(2,1)S(1)}, u32[]{:S(2)}, u32[]{:S(2)}) collective-permute-start(bf16[338,64]{0,1:T(8,128)(2,1)S(1)} %maximum_select_fusion.4), channel_id=1, source_target_pairs={{0,64},{32,96},{64,0},{96,32},{128,192},{160,224},{192,128},{224,1... | collective-permute-start | bytes 129800 | tf_op jit(solution)/shard_map/ppermute | solution.py:32
  295.2 2.0 collective-permute-done.18
  297.3 5.6 %collective-permute-start.19 = (bf16[338,128]{0,1:T(8,128)(2,1)S(1)}, bf16[338,128]{0,1:T(8,128)(2,1)S(1)}, u32[]{:S(2)}, u32[]{:S(2)}) collective-permute-start(bf16[338,128]{0,1:T(8,128)(2,1)S(1)} %maximum_select_fusion.3), channel_id=1, source_target_pairs={{0,128},{32,160},{64,192},{96,224},{128,0},{160,32},{192,64},{224,... | collective-permute-start | bytes 259592 | tf_op jit(solution)/shard_map/ppermute | solution.py:32
  302.9 4.8 %collective-permute-done.19 = bf16[338,128]{0,1:T(8,128)(2,1)S(1)} collective-permute-done((bf16[338,128]{0,1:T(8,128)(2,1)S(1)}, bf16[338,128]{0,1:T(8,128)(2,1)S(1)}, u32[]{:S(2)}, u32[]{:S(2)}) %collective-permute-start.19) | collective-permute-done | bytes 86560 | tf_op jit(solution)/shard_map/ppermute | solution.py:32
  307.7 9.1 %collective-permute-start.20 = (bf16[338,256]{0,1:T(8,128)(2,1)S(1)}, bf16[338,256]{0,1:T(8,128)(2,1)S(1)}, u32[]{:S(2)}, u32[]{:S(2)}) collective-permute-start(bf16[338,256]{0,1:T(8,128)(2,1)S(1)} %maximum_select_fusion.2), channel_id=1, source_target_pairs={{0,256},{32,288},{64,320},{96,352},{128,384},{160,416},{192,448},{... | collective-permute-start | bytes 519176 | tf_op jit(solution)/shard_map/ppermute | solution.py:32
  316.9 14.7 %collective-permute-done.20 = bf16[338,256]{0,1:T(8,128)(2,1)S(1)} collective-permute-done((bf16[338,256]{0,1:T(8,128)(2,1)S(1)}, bf16[338,256]{0,1:T(8,128)(2,1)S(1)}, u32[]{:S(2)}, u32[]{:S(2)}) %collective-permute-start.20) | collective-permute-done | bytes 173088 | tf_op jit(solution)/shard_map/ppermute | solution.py:32
  333.7 9.2 %collective-permute-done.21 = bf16[338,512]{0,1:T(8,128)(2,1)S(1)} collective-permute-done((bf16[338,512]{0,1:T(8,128)(2,1)S(1)}, bf16[338,512]{0,1:T(8,128)(2,1)S(1)}, u32[]{:S(2)}, u32[]{:S(2)}) %collective-permute-start.21) | collective-permute-done | bytes 346144 | tf_op jit(solution)/shard_map/ppermute | solution.py:32
  (94 shorter events, 38.8 us)
Async XLA Ops:
  0.6 186.0 %copy-start = (bf16[336,2048]{1,0:T(8,128)(2,1)S(1)}, bf16[336,2048]{1,0:T(8,128)(2,1)}, u32[]{:S(2)}) copy-start(bf16[336,2048]{1,0:T(8,128)(2,1)} %param.6) | copy-start | bytes 4128772
  1.9 29.6 %collective-permute-start = (bf16[128,1024]{0,1:T(8,128)(2,1)S(1)}, bf16[128,1024]{0,1:T(8,128)(2,1)}, u32[]{:S(2)}, u32[]{:S(2)}) collective-permute-start(bf16[128,1024]{0,1:T(8,128)(2,1)S(1)} %copy.151), channel_id=1, source_target_pairs={{0,8},{1,9},{2,10},{3,11},{4,12},{5,13},{6,14},{7,15},{8,16},{9,17... | collective-permute-start | bytes 786440 | tf_op jit(solution)/shard_map/ppermute | solution.py:26
  7.0 28.1 %collective-permute-start.1 = (bf16[128,1024]{0,1:T(8,128)(2,1)S(1)}, bf16[128,1024]{0,1:T(8,128)(2,1)}, u32[]{:S(2)}, u32[]{:S(2)}) collective-permute-start(bf16[128,1024]{0,1:T(8,128)(2,1)S(1)} %copy.151), channel_id=1, source_target_pairs={{0,7},{1,8},{2,9},{3,10},{4,11},{5,12},{6,13},{7,14},{8,15},{9,16}... | collective-permute-start | bytes 786440 | tf_op jit(solution)/shard_map/ppermute | solution.py:26
  10.0 30.5 %collective-permute-start.2 = (bf16[128,1024]{0,1:T(8,128)(2,1)S(1)}, bf16[128,1024]{0,1:T(8,128)(2,1)S(1)}, u32[]{:S(2)}, u32[]{:S(2)}) collective-permute-start(bf16[128,1024]{0,1:T(8,128)(2,1)S(1)} %copy.151), channel_id=1, source_target_pairs={{0,6},{1,7},{2,8},{3,9},{4,10},{5,11},{6,12},{7,13},{8,14},{9,15},... | collective-permute-start | bytes 786440 | tf_op jit(solution)/shard_map/ppermute | solution.py:26
  15.6 26.9 %collective-permute-start.3 = (bf16[128,1024]{0,1:T(8,128)(2,1)S(1)}, bf16[128,1024]{0,1:T(8,128)(2,1)S(1)}, u32[]{:S(2)}, u32[]{:S(2)}) collective-permute-start(bf16[128,1024]{0,1:T(8,128)(2,1)S(1)} %copy.151), channel_id=1, source_target_pairs={{0,5},{1,6},{2,7},{3,8},{4,9},{5,10},{6,11},{7,12},{8,13},{9,14},{... | collective-permute-start | bytes 786440 | tf_op jit(solution)/shard_map/ppermute | solution.py:26
  17.9 24.6 %collective-permute-start.4 = (bf16[128,1024]{0,1:T(8,128)(2,1)S(1)}, bf16[128,1024]{0,1:T(8,128)(2,1)S(1)}, u32[]{:S(2)}, u32[]{:S(2)}) collective-permute-start(bf16[128,1024]{0,1:T(8,128)(2,1)S(1)} %copy.151), channel_id=1, source_target_pairs={{0,4},{1,5},{2,6},{3,7},{4,8},{5,9},{6,10},{7,11},{8,12},{9,13},{1... | collective-permute-start | bytes 786440 | tf_op jit(solution)/shard_map/ppermute | solution.py:26
  31.5 11.3 %collective-permute-start.5 = (bf16[128,1024]{0,1:T(8,128)(2,1)S(1)}, bf16[128,1024]{0,1:T(8,128)(2,1)S(1)}, u32[]{:S(2)}, u32[]{:S(2)}) collective-permute-start(bf16[128,1024]{0,1:T(8,128)(2,1)S(1)} %copy.151), channel_id=1, source_target_pairs={{0,3},{1,4},{2,5},{3,6},{4,7},{5,8},{6,9},{7,10},{8,11},{9,12},{10... | collective-permute-start | bytes 786440 | tf_op jit(solution)/shard_map/ppermute | solution.py:26
  35.1 11.1 %collective-permute-start.6 = (bf16[128,1024]{0,1:T(8,128)(2,1)S(1)}, bf16[128,1024]{0,1:T(8,128)(2,1)S(1)}, u32[]{:S(2)}, u32[]{:S(2)}) collective-permute-start(bf16[128,1024]{0,1:T(8,128)(2,1)S(1)} %copy.151), channel_id=1, source_target_pairs={{0,2},{1,3},{2,4},{3,5},{4,6},{5,7},{6,8},{7,9},{8,10},{9,11},{10,... | collective-permute-start | bytes 786440 | tf_op jit(solution)/shard_map/ppermute | solution.py:26
  40.4 8.5 %collective-permute-start.7 = (bf16[128,1024]{0,1:T(8,128)(2,1)S(1)}, bf16[128,1024]{0,1:T(8,128)(2,1)S(1)}, u32[]{:S(2)}, u32[]{:S(2)}) collective-permute-start(bf16[128,1024]{0,1:T(8,128)(2,1)S(1)} %copy.151), channel_id=1, source_target_pairs={{0,1},{1,2},{2,3},{3,4},{4,5},{5,6},{6,7},{7,8},{8,9},{9,10},{10,1... | collective-permute-start | bytes 786440 | tf_op jit(solution)/shard_map/ppermute | solution.py:26
  49.1 1.2 copy-start.5
  49.1 1.2 copy-start.10
  50.3 1.6 copy-start.4
  51.9 2.5 copy-start.9
  57.0 3.5 %copy-start.8 = (bf16[128,512]{0,1:T(8,128)(2,1)S(1)}, bf16[128,512]{0,1:T(8,128)(2,1)}, u32[]{:S(2)}) copy-start(bf16[128,512]{0,1:T(8,128)(2,1)} %copy.214) | copy-start | bytes 393220
  63.1 3.5 %copy-start.6 = (bf16[128,512]{0,1:T(8,128)(2,1)S(1)}, bf16[128,512]{0,1:T(8,128)(2,1)}, u32[]{:S(2)}) copy-start(bf16[128,512]{0,1:T(8,128)(2,1)} %copy.215) | copy-start | bytes 393220
  66.6 1.6 copy-start.7
  73.5 37.5 %copy-start.1 = (f32[2,1152,128,1]{1,2,3,0:T(8,128)S(1)}, f32[2,1152,128,1]{1,2,3,0:T(8,128)}, u32[]{:S(2)}) copy-start(f32[2,1152,128,1]{1,2,3,0:T(8,128)} %fusion.25) | copy-start | bytes 3538948
  73.5 37.5 %copy-start.2 = (f32[2,1152,128,1]{1,2,3,0:T(8,128)S(1)}, f32[2,1152,128,1]{1,2,3,0:T(8,128)}, u32[]{:S(2)}) copy-start(f32[2,1152,128,1]{1,2,3,0:T(8,128)} %fusion.26) | copy-start | bytes 3538948
  73.5 37.5 %copy-start.3 = (f32[2,1152,128,1]{1,2,3,0:T(8,128)S(1)}, f32[2,1152,128,1]{1,2,3,0:T(8,128)}, u32[]{:S(2)}) copy-start(f32[2,1152,128,1]{1,2,3,0:T(8,128)} %fusion.27) | copy-start | bytes 3538948
  73.9 17.0 %collective-permute-start.10 = (bf16[128,1024]{0,1:T(8,128)(2,1)S(1)}, bf16[128,1024]{0,1:T(8,128)(2,1)S(1)}, u32[]{:S(2)}, u32[]{:S(2)}) collective-permute-start(bf16[128,1024]{0,1:T(8,128)(2,1)S(1)} %get-tuple-element.14), channel_id=1, source_target_pairs={{3,0},{4,1},{5,2},{6,3},{7,4},{8,5},{9,6},{10,7},{11,8},{12,9},{13... | collective-permute-start | bytes 786440 | tf_op jit(solution)/shard_map/ppermute | solution.py:26
  80.1 15.5 %collective-permute-start.11 = (bf16[128,1024]{0,1:T(8,128)(2,1)S(1)}, bf16[128,1024]{0,1:T(8,128)(2,1)S(1)}, u32[]{:S(2)}, u32[]{:S(2)}) collective-permute-start(bf16[128,1024]{0,1:T(8,128)(2,1)S(1)} %get-tuple-element.13), channel_id=1, source_target_pairs={{4,0},{5,1},{6,2},{7,3},{8,4},{9,5},{10,6},{11,7},{12,8},{13,9},{1... | collective-permute-start | bytes 786440 | tf_op jit(solution)/shard_map/ppermute | solution.py:26
  84.2 24.7 %collective-permute-start.12 = (bf16[128,1024]{0,1:T(8,128)(2,1)S(1)}, bf16[128,1024]{0,1:T(8,128)(2,1)S(1)}, u32[]{:S(2)}, u32[]{:S(2)}) collective-permute-start(bf16[128,1024]{0,1:T(8,128)(2,1)S(1)} %get-tuple-element.12), channel_id=1, source_target_pairs={{5,0},{6,1},{7,2},{8,3},{9,4},{10,5},{11,6},{12,7},{13,8},{14,9},{... | collective-permute-start | bytes 786440 | tf_op jit(solution)/shard_map/ppermute | solution.py:26
  86.1 28.5 %collective-permute-start.13 = (bf16[128,1024]{0,1:T(8,128)(2,1)S(1)}, bf16[128,1024]{0,1:T(8,128)(2,1)S(1)}, u32[]{:S(2)}, u32[]{:S(2)}) collective-permute-start(bf16[128,1024]{0,1:T(8,128)(2,1)S(1)} %get-tuple-element.11), channel_id=1, source_target_pairs={{6,0},{7,1},{8,2},{9,3},{10,4},{11,5},{12,6},{13,7},{14,8},{15,9},... | collective-permute-start | bytes 786440 | tf_op jit(solution)/shard_map/ppermute | solution.py:26
  89.0 25.7 %collective-permute-start.14 = (bf16[128,1024]{0,1:T(8,128)(2,1)S(1)}, bf16[128,1024]{0,1:T(8,128)(2,1)S(1)}, u32[]{:S(2)}, u32[]{:S(2)}) collective-permute-start(bf16[128,1024]{0,1:T(8,128)(2,1)S(1)} %get-tuple-element.10), channel_id=1, source_target_pairs={{7,0},{8,1},{9,2},{10,3},{11,4},{12,5},{13,6},{14,7},{15,8},{16,9}... | collective-permute-start | bytes 786440 | tf_op jit(solution)/shard_map/ppermute | solution.py:26
  90.9 23.7 %collective-permute-start.15 = (bf16[128,1024]{0,1:T(8,128)(2,1)S(1)}, bf16[128,1024]{0,1:T(8,128)(2,1)S(1)}, u32[]{:S(2)}, u32[]{:S(2)}) collective-permute-start(bf16[128,1024]{0,1:T(8,128)(2,1)S(1)} %get-tuple-element.9), channel_id=1, source_target_pairs={{8,0},{9,1},{10,2},{11,3},{12,4},{13,5},{14,6},{15,7},{16,8},{17,9... | collective-permute-start | bytes 786440 | tf_op jit(solution)/shard_map/ppermute | solution.py:26
  95.7 19.0 %collective-permute-start.8 = (bf16[128,1024]{0,1:T(8,128)(2,1)S(1)}, bf16[128,1024]{0,1:T(8,128)(2,1)S(1)}, u32[]{:S(2)}, u32[]{:S(2)}) collective-permute-start(bf16[128,1024]{0,1:T(8,128)(2,1)S(1)} %get-tuple-element.8), channel_id=1, source_target_pairs={{1,0},{2,1},{3,2},{4,3},{5,4},{6,5},{7,6},{8,7},{9,8},{10,9},{11,1... | collective-permute-start | bytes 786440 | tf_op jit(solution)/shard_map/ppermute | solution.py:26
  108.9 16.7 %collective-permute-start.9 = (bf16[128,1024]{0,1:T(8,128)(2,1)S(1)}, bf16[128,1024]{0,1:T(8,128)(2,1)S(1)}, u32[]{:S(2)}, u32[]{:S(2)}) collective-permute-start(bf16[128,1024]{0,1:T(8,128)(2,1)S(1)} %get-tuple-element.15), channel_id=1, source_target_pairs={{2,0},{3,1},{4,2},{5,3},{6,4},{7,5},{8,6},{9,7},{10,8},{11,9},{12,... | collective-permute-start | bytes 786440 | tf_op jit(solution)/shard_map/ppermute | solution.py:26
  128.6 58.0 %all-to-all-start = ((bf16[16,128,1024]{2,1,0:T(8,128)(2,1)}), bf16[16,128,1024]{2,1,0:T(8,128)(2,1)}, u32[]{:S(2)}, u32[]{:S(2)}) async-start(bf16[16,128,1024]{2,1,0:T(8,128)(2,1)} %broadcast_in_dim.43), calls=%async_computation | async-start | bytes 8388608 | tf_op jit(solution)/shard_map/all_to_all | solution.py:101
  191.3 5.8 %copy-start.11 = (f32[1024]{0:T(1024)S(1)}, f32[1024]{0:T(1024)}, u32[]{:S(2)}) copy-start(f32[1024]{0:T(1024)} %param.8) | copy-start | bytes 12292
  191.3 35.7 %collective-permute-start.16 = (f32[336,512]{1,0:T(8,128)}, f32[336,512]{1,0:T(8,128)}, u32[]{:S(2)}, u32[]{:S(2)}) collective-permute-start(f32[336,512]{1,0:T(8,128)} %dynamic-slice_bitcast_fusion), channel_id=1, source_target_pairs={{0,16},{16,0},{1,17},{17,1},{2,18},{18,2},{3,19},{19,3},{4,20},{20... | collective-permute-start | bytes 2064392 | tf_op jit(solution)/shard_map/ppermute | solution.py:119
  232.4 51.0 %all-to-all-start.1 = ((f32[337,16,32]{0,2,1:T(8,128)}), f32[337,16,32]{0,2,1:T(8,128)S(1)}, u32[]{:S(2)}, u32[]{:S(2)}) async-start(f32[337,16,32]{0,2,1:T(8,128)} %pad_maximum_fusion.1), calls=%async_computation.1 | async-start | bytes 1572864 | tf_op jit(solution)/shard_map/all_to_all | solution.py:124
  284.0 5.7 %collective-permute-start.17 = (bf16[338,32]{0,1:T(8,128)(2,1)S(1)}, bf16[338,32]{0,1:T(8,128)(2,1)S(1)}, u32[]{:S(2)}, u32[]{:S(2)}) collective-permute-start(bf16[338,32]{0,1:T(8,128)(2,1)S(1)} %pad_maximum_fusion.2), channel_id=1, source_target_pairs={{0,32},{32,0},{64,96},{96,64},{128,160},{160,128},{192,224},{224,1... | collective-permute-start | bytes 64904 | tf_op jit(solution)/shard_map/ppermute | solution.py:32
  289.8 7.5 %collective-permute-start.18 = (bf16[338,64]{0,1:T(8,128)(2,1)S(1)}, bf16[338,64]{0,1:T(8,128)(2,1)S(1)}, u32[]{:S(2)}, u32[]{:S(2)}) collective-permute-start(bf16[338,64]{0,1:T(8,128)(2,1)S(1)} %maximum_select_fusion.4), channel_id=1, source_target_pairs={{0,64},{32,96},{64,0},{96,32},{128,192},{160,224},{192,128},{224,1... | collective-permute-start | bytes 129800 | tf_op jit(solution)/shard_map/ppermute | solution.py:32
  297.3 10.4 %collective-permute-start.19 = (bf16[338,128]{0,1:T(8,128)(2,1)S(1)}, bf16[338,128]{0,1:T(8,128)(2,1)S(1)}, u32[]{:S(2)}, u32[]{:S(2)}) collective-permute-start(bf16[338,128]{0,1:T(8,128)(2,1)S(1)} %maximum_select_fusion.3), channel_id=1, source_target_pairs={{0,128},{32,160},{64,192},{96,224},{128,0},{160,32},{192,64},{224,... | collective-permute-start | bytes 259592 | tf_op jit(solution)/shard_map/ppermute | solution.py:32
  307.7 23.9 %collective-permute-start.20 = (bf16[338,256]{0,1:T(8,128)(2,1)S(1)}, bf16[338,256]{0,1:T(8,128)(2,1)S(1)}, u32[]{:S(2)}, u32[]{:S(2)}) collective-permute-start(bf16[338,256]{0,1:T(8,128)(2,1)S(1)} %maximum_select_fusion.2), channel_id=1, source_target_pairs={{0,256},{32,288},{64,320},{96,352},{128,384},{160,416},{192,448},{... | collective-permute-start | bytes 519176 | tf_op jit(solution)/shard_map/ppermute | solution.py:32
  331.8 11.2 %collective-permute-start.21 = (bf16[338,512]{0,1:T(8,128)(2,1)S(1)}, bf16[338,512]{0,1:T(8,128)(2,1)S(1)}, u32[]{:S(2)}, u32[]{:S(2)}) collective-permute-start(bf16[338,512]{0,1:T(8,128)(2,1)S(1)} %maximum_select_fusion.1), channel_id=1, source_target_pairs={{0,16},{16,0},{1,17},{17,1},{2,18},{18,2},{3,19},{19,3},{4,20},{20... | collective-permute-start | bytes 1038344 | tf_op jit(solution)/shard_map/ppermute | solution.py:32

commit v9 on v7

--- a/solution.py
+++ b/solution.py
@@ -105,11 +105,12 @@
         keep = lax.dynamic_slice_in_dim(local_grad, xh_index * half, half, 1)
         send = lax.dynamic_slice_in_dim(local_grad, (1 - xh_index) * half, half, 1)
         swapped = keep + lax.ppermute(send, "xh", [(0, 1), (1, 0)])
-        for axis in ("c", "xl", "y", "xh"):
+        for axis in ("c", "xl", "y"):
             logit_part = lax.psum(logit_part, axis)
-        logit_half = lax.dynamic_slice_in_dim(logit_part, xh_index * half, half, 0)
-        payload = jnp.concatenate([swapped, logit_half[None]], axis=0)
-        received = lax.all_to_all(payload.reshape(rows + 1, n_z, piece), "z", 1, 1, tiled=True)
+        logit_keep = lax.dynamic_slice_in_dim(logit_part, xh_index * half, half, 0)
+        logit_other = lax.dynamic_slice_in_dim(logit_part, (1 - xh_index) * half, half, 0)
+        payload = jnp.concatenate([swapped, logit_keep[None], logit_other[None]], axis=0)
+        received = lax.all_to_all(payload.reshape(rows + 2, n_z, piece), "z", 1, 1, tiled=True)
         summed = jnp.sum(received, axis=1)
         dense_piece = summed[:rows]
         logit_piece = summed[rows:]
@@ -120,11 +121,16 @@
         weight_piece = jnp.where(kept_piece, dense_piece, 0.0).astype(jnp.bfloat16)
         logit_hi = logit_piece.astype(jnp.bfloat16)
         logit_lo = (logit_piece - logit_hi.astype(jnp.float32)).astype(jnp.bfloat16)
-        out_piece = jnp.concatenate([weight_piece, logit_hi, logit_lo], axis=0)
+        out_piece = jnp.concatenate(
+            [weight_piece, logit_hi[:1], logit_lo[:1], logit_hi[1:], logit_lo[1:]], axis=0
+        )
         out_piece = lax.all_gather(out_piece, "z", axis=1, tiled=True)
         out_full = lax.all_gather(out_piece, "xh", axis=1, tiled=True)
         grad_weight = out_full[:rows]
-        logit_sum = out_full[rows].astype(jnp.float32) + out_full[rows + 1].astype(jnp.float32)
+        logit_wide = out_full[rows:].astype(jnp.float32)
+        logit_own = logit_wide[0] + logit_wide[1]
+        logit_oth = logit_wide[2] + logit_wide[3]
+        logit_sum = logit_own + jnp.concatenate([logit_oth[half:], logit_oth[:half]], axis=0)
         grad_logit = -logit_sum * threshold * (1.0 - threshold)
         return (grad_weight, grad_logit)
 

time: 332 us -> 329 us (level)
  blocking collectives: 68.3 us -> 62.9 us
    psum x4 -> x3, blocking collectives: 26.8 us -> 20 us  [local(): logit_part = lax.psum(logit_part, axis)]
    unnamed x40 -> x39, local copies, waits for them, and re-layouts: 9.36 us -> 9.28 us
where the time goes in v9:
time: 329 us; the launch traced here: 325 us
  waiting for transfers between devices  112 us (34%)
  starting transfers between devices  86.8 us (26%)
  blocking collectives  62.9 us (19%)
  local copies, waits for them, and re-layouts  25.1 us (8%)
  matrix products  24.7 us (8%)
  other arithmetic  12.5 us (4%)
    ppermute x16, starting transfers between devices, passed_along(): lax.ppermute(value, axis, [(source, source + steps) for source in range(f...  58.7 us
    all_to_all x1, waiting for transfers between devices, local(): lax.all_to_all(spread, FSDP, 0, 0, tiled=True)  49.2 us
    all_to_all x1, waiting for transfers between devices, local(): lax.all_to_all(payload.reshape(rows + 2, n_z, piece), 'z', 1, 1, tiled=True)  35.3 us
    all_gather x1, blocking collectives, local(): out_piece = lax.all_gather(out_piece, 'z', axis=1, tiled=True)  32.9 us
    ppermute x16, waiting for transfers between devices, passed_along(): lax.ppermute(value, axis, [(source, source + steps) for source in range(f...  27.3 us
    psum x3, blocking collectives, local(): logit_part = lax.psum(logit_part, axis)  20 us
    all_to_all x1, starting transfers between devices, local(): lax.all_to_all(payload.reshape(rows + 2, n_z, piece), 'z', 1, 1, tiled=True)  16.6 us
    dot_general x4, matrix products, local(): jnp.einsum('grqk,qgrd->kgd', probabilities, d_cols, preferred_element_typ...  12.4 us
  transfers between devices with their start and end apart: 19, of which 9 were waited for; matrix products, arithmetic and copies ran while one was open for 6% of the time, Pallas kernels for 0%

profile of v9, /device:TPU:6, one launch (start us, length us, event | category | flops | bytes accessed | tf_op | source)
XLA Modules:
  0.0 324.9 jit_solution(9496219497840086701)
XLA Ops:
  1.9 5.1 %collective-permute-start = (bf16[128,1024]{0,1:T(8,128)(2,1)S(1)}, bf16[128,1024]{0,1:T(8,128)(2,1)}, u32[]{:S(2)}, u32[]{:S(2)}) collective-permute-start(bf16[128,1024]{0,1:T(8,128)(2,1)S(1)} %copy.154), channel_id=1, source_target_pairs={{0,8},{1,9},{2,10},{3,11},{4,12},{5,13},{6,14},{7,15},{8,16},{9,17... | collective-permute-start | bytes 786440 | tf_op jit(solution)/shard_map/ppermute | solution.py:26
  7.0 3.0 collective-permute-start.1
  10.0 5.6 %collective-permute-start.2 = (bf16[128,1024]{0,1:T(8,128)(2,1)S(1)}, bf16[128,1024]{0,1:T(8,128)(2,1)S(1)}, u32[]{:S(2)}, u32[]{:S(2)}) collective-permute-start(bf16[128,1024]{0,1:T(8,128)(2,1)S(1)} %copy.154), channel_id=1, source_target_pairs={{0,6},{1,7},{2,8},{3,9},{4,10},{5,11},{6,12},{7,13},{8,14},{9,15},... | collective-permute-start | bytes 786440 | tf_op jit(solution)/shard_map/ppermute | solution.py:26
  15.6 2.3 collective-permute-start.3
  17.9 3.7 %collective-permute-start.4 = (bf16[128,1024]{0,1:T(8,128)(2,1)S(1)}, bf16[128,1024]{0,1:T(8,128)(2,1)S(1)}, u32[]{:S(2)}, u32[]{:S(2)}) collective-permute-start(bf16[128,1024]{0,1:T(8,128)(2,1)S(1)} %copy.154), channel_id=1, source_target_pairs={{0,4},{1,5},{2,6},{3,7},{4,8},{5,9},{6,10},{7,11},{8,12},{9,13},{1... | collective-permute-start | bytes 786440 | tf_op jit(solution)/shard_map/ppermute | solution.py:26
  21.7 1.5 fusion.29
  31.5 2.5 collective-permute-start.5
  35.1 4.4 %collective-permute-start.6 = (bf16[128,1024]{0,1:T(8,128)(2,1)S(1)}, bf16[128,1024]{0,1:T(8,128)(2,1)S(1)}, u32[]{:S(2)}, u32[]{:S(2)}) collective-permute-start(bf16[128,1024]{0,1:T(8,128)(2,1)S(1)} %copy.154), channel_id=1, source_target_pairs={{0,2},{1,3},{2,4},{3,5},{4,6},{5,7},{6,8},{7,9},{8,10},{9,11},{10,... | collective-permute-start | bytes 786440 | tf_op jit(solution)/shard_map/ppermute | solution.py:26
  40.4 1.9 collective-permute-start.7
  42.8 3.3 %collective-permute-done.6 = bf16[128,1024]{0,1:T(8,128)(2,1)S(1)} collective-permute-done((bf16[128,1024]{0,1:T(8,128)(2,1)S(1)}, bf16[128,1024]{0,1:T(8,128)(2,1)S(1)}, u32[]{:S(2)}, u32[]{:S(2)}) %collective-permute-start.6) | collective-permute-done | bytes 262176 | tf_op jit(solution)/shard_map/ppermute | solution.py:26
  46.2 2.7 collective-permute-done.7
  50.3 1.6 fusion.86
  51.9 2.4 fusion.24
  54.4 2.6 fusion.85
  57.0 3.5 %fusion.25 = f32[2,1152,128,1]{1,2,3,0:T(8,128)} fusion(bf16[128,2,2,128]{0,3,2,1:T(8,128)(2,1)} %bitcast.165, f32[2,2,128]{2,1,0:T(2,128)} %fusion.85, bf16[1152,2,128,1]{0,2,3,1:T(8,128)(2,1)} %bitcast.154, bf16[128,2,2,128]{0,3,2,1:T(8,128)(2,1)S(1)} %bitcast.164, pred[128,1152]{0,1:T(8,128)(4,1)S(1)} %copy-done.5), kind=kOutput, calls=%fused_computation.36 | convolution fusion | flops 304940672 | bytes 2181120 | tf_op jit(solution)/shard_map/grqk,qgrd->kgd/dot_general | solution.py:70
  60.5 2.6 fusion.84
  63.1 3.5 %fusion.26 = f32[2,1152,128,1]{1,2,3,0:T(8,128)} fusion(bf16[128,2,2,128]{0,3,2,1:T(8,128)(2,1)} %bitcast.162, f32[2,2,128]{2,1,0:T(2,128)} %fusion.84, bf16[1152,2,128,1]{0,2,3,1:T(8,128)(2,1)} %bitcast.152, bf16[128,2,2,128]{0,3,2,1:T(8,128)(2,1)S(1)} %bitcast.161, pred[128,1152]{0,1:T(8,128)(4,1)S(1)} %copy-done.5), kind=kOutput, calls=%fused_computation.37 | convolution fusion | flops 304940672 | bytes 2181120 | tf_op jit(solution)/shard_map/grqk,qgrd->kgd/dot_general | solution.py:70
  66.7 1.6 fusion.83
  68.3 3.0 fusion.27
  71.3 2.2 fusion.75
  73.9 6.2 %collective-permute-start.10 = (bf16[128,1024]{0,1:T(8,128)(2,1)S(1)}, bf16[128,1024]{0,1:T(8,128)(2,1)S(1)}, u32[]{:S(2)}, u32[]{:S(2)}) collective-permute-start(bf16[128,1024]{0,1:T(8,128)(2,1)S(1)} %get-tuple-element.18), channel_id=1, source_target_pairs={{3,0},{4,1},{5,2},{6,3},{7,4},{8,5},{9,6},{10,7},{11,8},{12,9},{13... | collective-permute-start | bytes 786440 | tf_op jit(solution)/shard_map/ppermute | solution.py:26
  80.1 4.0 %collective-permute-start.11 = (bf16[128,1024]{0,1:T(8,128)(2,1)S(1)}, bf16[128,1024]{0,1:T(8,128)(2,1)S(1)}, u32[]{:S(2)}, u32[]{:S(2)}) collective-permute-start(bf16[128,1024]{0,1:T(8,128)(2,1)S(1)} %get-tuple-element.17), channel_id=1, source_target_pairs={{4,0},{5,1},{6,2},{7,3},{8,4},{9,5},{10,6},{11,7},{12,8},{13,9},{1... | collective-permute-start | bytes 786440 | tf_op jit(solution)/shard_map/ppermute | solution.py:26
  84.2 1.9 collective-permute-start.12
  86.1 2.9 collective-permute-start.13
  89.0 1.9 collective-permute-start.14
  90.9 1.9 collective-permute-start.15
  92.9 2.8 collective-permute-done.11
  95.7 9.2 %collective-permute-start.8 = (bf16[128,1024]{0,1:T(8,128)(2,1)S(1)}, bf16[128,1024]{0,1:T(8,128)(2,1)S(1)}, u32[]{:S(2)}, u32[]{:S(2)}) collective-permute-start(bf16[128,1024]{0,1:T(8,128)(2,1)S(1)} %get-tuple-element.12), channel_id=1, source_target_pairs={{1,0},{2,1},{3,2},{4,3},{5,4},{6,5},{7,6},{8,7},{9,8},{10,9},{11,1... | collective-permute-start | bytes 786440 | tf_op jit(solution)/shard_map/ppermute | solution.py:26
  104.9 4.0 %collective-permute-done.12 = bf16[128,1024]{0,1:T(8,128)(2,1)S(1)} collective-permute-done((bf16[128,1024]{0,1:T(8,128)(2,1)S(1)}, bf16[128,1024]{0,1:T(8,128)(2,1)S(1)}, u32[]{:S(2)}, u32[]{:S(2)}) %collective-permute-start.12) | collective-permute-done | bytes 262176 | tf_op jit(solution)/shard_map/ppermute | solution.py:26
  108.9 2.1 collective-permute-start.9
  111.3 3.3 %collective-permute-done.13 = bf16[128,1024]{0,1:T(8,128)(2,1)S(1)} collective-permute-done((bf16[128,1024]{0,1:T(8,128)(2,1)S(1)}, bf16[128,1024]{0,1:T(8,128)(2,1)S(1)}, u32[]{:S(2)}, u32[]{:S(2)}) %collective-permute-start.13) | collective-permute-done | bytes 262176 | tf_op jit(solution)/shard_map/ppermute | solution.py:26
  114.7 10.9 %collective-permute-done.9 = bf16[128,1024]{0,1:T(8,128)(2,1)S(1)} collective-permute-done((bf16[128,1024]{0,1:T(8,128)(2,1)S(1)}, bf16[128,1024]{0,1:T(8,128)(2,1)S(1)}, u32[]{:S(2)}, u32[]{:S(2)}) %collective-permute-start.9) | collective-permute-done | bytes 262176 | tf_op jit(solution)/shard_map/ppermute | solution.py:26
  126.1 2.5 broadcast_in_dim.44
  128.6 8.9 %all-to-all-start = ((bf16[16,128,1024]{2,1,0:T(8,128)(2,1)}), bf16[16,128,1024]{2,1,0:T(8,128)(2,1)}, u32[]{:S(2)}, u32[]{:S(2)}) async-start(bf16[16,128,1024]{2,1,0:T(8,128)(2,1)} %broadcast_in_dim.44), calls=%async_computation | async-start | bytes 8388608 | tf_op jit(solution)/shard_map/all_to_all | solution.py:89
  137.4 49.2 %all-to-all-done = bf16[16,128,1024]{2,1,0:T(8,128)(2,1)} async-done(((bf16[16,128,1024]{2,1,0:T(8,128)(2,1)}), bf16[16,128,1024]{2,1,0:T(8,128)(2,1)}, u32[]{:S(2)}, u32[]{:S(2)}) %all-to-all-start) | async-done | bytes 4194336 | tf_op jit(solution)/shard_map/all_to_all | solution.py:89
  186.6 3.8 %fusion.87 = f32[1024,336]{0,1:T(8,128)S(1)} fusion(bf16[336,2048]{1,0:T(8,128)(2,1)S(1)} %copy-done, bf16[2048,1024]{1,0:T(8,128)(2,1)} %bitcast.36), kind=kOutput, calls=%fused_computation.117 | convolution fusion | flops 1409286144 | bytes 6946816 | tf_op jit(solution)/shard_map/dot_general | solution.py:92
  191.3 2.7 collective-permute-start.16
  195.4 1.6 copy.185
  197.0 2.2 fusion.23
  199.3 2.5 psum.21
  201.7 8.3 %psum.22 = f32[1024]{0:T(1024)S(1)} all-reduce(f32[1024]{0:T(1024)S(1)} %psum.21), channel_id=1, replica_groups=mesh['z'=16,'xh'=2,'y'=4,'xl'=2,'c'=2] {'xl'}, use_global_device_ids=true, to_apply=%region_10.11 | all-reduce | flops 1024 | bytes 8192 | tf_op jit(solution)/shard_map/psum | solution.py:109
  210.1 9.2 %psum.23 = f32[1024]{0:T(1024)S(1)} all-reduce(f32[1024]{0:T(1024)S(1)} %psum.22), channel_id=1, replica_groups=mesh['z'=16,'xh'=2,'y'=4,'xl'=2,'c'=2] {'y'}, use_global_device_ids=true, to_apply=%region_11.12 | all-reduce | flops 1024 | bytes 8192 | tf_op jit(solution)/shard_map/psum | solution.py:109
  221.2 2.1 bitcast_add_fusion
  224.7 2.1 pad_maximum_fusion.1
  226.8 16.6 %all-to-all-start.1 = ((f32[338,16,32]{0,2,1:T(8,128)}), f32[338,16,32]{0,2,1:T(8,128)S(1)}, u32[]{:S(2)}, u32[]{:S(2)}) async-start(f32[338,16,32]{0,2,1:T(8,128)} %pad_maximum_fusion.1), calls=%async_computation.1 | async-start | bytes 1572864 | tf_op jit(solution)/shard_map/all_to_all | solution.py:113
  243.7 35.3 %all-to-all-done.1 = f32[338,16,32]{0,2,1:T(8,128)S(1)} async-done(((f32[338,16,32]{0,2,1:T(8,128)}), f32[338,16,32]{0,2,1:T(8,128)S(1)}, u32[]{:S(2)}, u32[]{:S(2)}) %all-to-all-start.1) | async-done | bytes 692256 | tf_op jit(solution)/shard_map/all_to_all | solution.py:113
  279.3 32.9 %all_gather.6 = bf16[340,512]{0,1:T(8,128)(2,1)S(1)} all-gather(bf16[340,32]{0,1:T(8,128)(2,1)S(1)} %concatenate.28), channel_id=1, replica_groups=mesh['z'=16,'xh'=2,'y'=4,'xl'=2,'c'=2] {'z'}, dimensions={1}, use_global_device_ids=true | all-gather | bytes 369920 | tf_op jit(solution)/shard_map/all_gather | solution.py:127
  312.2 9.9 %all_gather.7 = bf16[340,1024]{0,1:T(8,128)(2,1)S(1)} all-gather(bf16[340,512]{0,1:T(8,128)(2,1)S(1)} %all_gather.6), channel_id=1, replica_groups=mesh['z'=16,'xh'=2,'y'=4,'xl'=2,'c'=2] {'xh'}, dimensions={1}, use_global_device_ids=true | all-gather | bytes 1044480 | tf_op jit(solution)/shard_map/all_gather | solution.py:128
  (80 shorter events, 23.6 us)
Async XLA Ops:
  0.6 186.0 %copy-start = (bf16[336,2048]{1,0:T(8,128)(2,1)S(1)}, bf16[336,2048]{1,0:T(8,128)(2,1)}, u32[]{:S(2)}) copy-start(bf16[336,2048]{1,0:T(8,128)(2,1)} %param.6) | copy-start | bytes 4128772
  1.9 29.6 %collective-permute-start = (bf16[128,1024]{0,1:T(8,128)(2,1)S(1)}, bf16[128,1024]{0,1:T(8,128)(2,1)}, u32[]{:S(2)}, u32[]{:S(2)}) collective-permute-start(bf16[128,1024]{0,1:T(8,128)(2,1)S(1)} %copy.154), channel_id=1, source_target_pairs={{0,8},{1,9},{2,10},{3,11},{4,12},{5,13},{6,14},{7,15},{8,16},{9,17... | collective-permute-start | bytes 786440 | tf_op jit(solution)/shard_map/ppermute | solution.py:26
  7.0 28.1 %collective-permute-start.1 = (bf16[128,1024]{0,1:T(8,128)(2,1)S(1)}, bf16[128,1024]{0,1:T(8,128)(2,1)}, u32[]{:S(2)}, u32[]{:S(2)}) collective-permute-start(bf16[128,1024]{0,1:T(8,128)(2,1)S(1)} %copy.154), channel_id=1, source_target_pairs={{0,7},{1,8},{2,9},{3,10},{4,11},{5,12},{6,13},{7,14},{8,15},{9,16}... | collective-permute-start | bytes 786440 | tf_op jit(solution)/shard_map/ppermute | solution.py:26
  10.0 30.5 %collective-permute-start.2 = (bf16[128,1024]{0,1:T(8,128)(2,1)S(1)}, bf16[128,1024]{0,1:T(8,128)(2,1)S(1)}, u32[]{:S(2)}, u32[]{:S(2)}) collective-permute-start(bf16[128,1024]{0,1:T(8,128)(2,1)S(1)} %copy.154), channel_id=1, source_target_pairs={{0,6},{1,7},{2,8},{3,9},{4,10},{5,11},{6,12},{7,13},{8,14},{9,15},... | collective-permute-start | bytes 786440 | tf_op jit(solution)/shard_map/ppermute | solution.py:26
  15.6 26.9 %collective-permute-start.3 = (bf16[128,1024]{0,1:T(8,128)(2,1)S(1)}, bf16[128,1024]{0,1:T(8,128)(2,1)S(1)}, u32[]{:S(2)}, u32[]{:S(2)}) collective-permute-start(bf16[128,1024]{0,1:T(8,128)(2,1)S(1)} %copy.154), channel_id=1, source_target_pairs={{0,5},{1,6},{2,7},{3,8},{4,9},{5,10},{6,11},{7,12},{8,13},{9,14},{... | collective-permute-start | bytes 786440 | tf_op jit(solution)/shard_map/ppermute | solution.py:26
  17.9 24.6 %collective-permute-start.4 = (bf16[128,1024]{0,1:T(8,128)(2,1)S(1)}, bf16[128,1024]{0,1:T(8,128)(2,1)S(1)}, u32[]{:S(2)}, u32[]{:S(2)}) collective-permute-start(bf16[128,1024]{0,1:T(8,128)(2,1)S(1)} %copy.154), channel_id=1, source_target_pairs={{0,4},{1,5},{2,6},{3,7},{4,8},{5,9},{6,10},{7,11},{8,12},{9,13},{1... | collective-permute-start | bytes 786440 | tf_op jit(solution)/shard_map/ppermute | solution.py:26
  31.5 11.3 %collective-permute-start.5 = (bf16[128,1024]{0,1:T(8,128)(2,1)S(1)}, bf16[128,1024]{0,1:T(8,128)(2,1)S(1)}, u32[]{:S(2)}, u32[]{:S(2)}) collective-permute-start(bf16[128,1024]{0,1:T(8,128)(2,1)S(1)} %copy.154), channel_id=1, source_target_pairs={{0,3},{1,4},{2,5},{3,6},{4,7},{5,8},{6,9},{7,10},{8,11},{9,12},{10... | collective-permute-start | bytes 786440 | tf_op jit(solution)/shard_map/ppermute | solution.py:26
  35.1 11.1 %collective-permute-start.6 = (bf16[128,1024]{0,1:T(8,128)(2,1)S(1)}, bf16[128,1024]{0,1:T(8,128)(2,1)S(1)}, u32[]{:S(2)}, u32[]{:S(2)}) collective-permute-start(bf16[128,1024]{0,1:T(8,128)(2,1)S(1)} %copy.154), channel_id=1, source_target_pairs={{0,2},{1,3},{2,4},{3,5},{4,6},{5,7},{6,8},{7,9},{8,10},{9,11},{10,... | collective-permute-start | bytes 786440 | tf_op jit(solution)/shard_map/ppermute | solution.py:26
  40.4 8.5 %collective-permute-start.7 = (bf16[128,1024]{0,1:T(8,128)(2,1)S(1)}, bf16[128,1024]{0,1:T(8,128)(2,1)S(1)}, u32[]{:S(2)}, u32[]{:S(2)}) collective-permute-start(bf16[128,1024]{0,1:T(8,128)(2,1)S(1)} %copy.154), channel_id=1, source_target_pairs={{0,1},{1,2},{2,3},{3,4},{4,5},{5,6},{6,7},{7,8},{8,9},{9,10},{10,1... | collective-permute-start | bytes 786440 | tf_op jit(solution)/shard_map/ppermute | solution.py:26
  49.1 1.2 copy-start.5
  49.1 1.2 copy-start.10
  50.3 1.6 copy-start.4
  51.9 2.5 copy-start.9
  57.0 3.5 %copy-start.8 = (bf16[128,512]{0,1:T(8,128)(2,1)S(1)}, bf16[128,512]{0,1:T(8,128)(2,1)}, u32[]{:S(2)}) copy-start(bf16[128,512]{0,1:T(8,128)(2,1)} %copy.215) | copy-start | bytes 393220
  63.1 3.5 %copy-start.6 = (bf16[128,512]{0,1:T(8,128)(2,1)S(1)}, bf16[128,512]{0,1:T(8,128)(2,1)}, u32[]{:S(2)}) copy-start(bf16[128,512]{0,1:T(8,128)(2,1)} %copy.216) | copy-start | bytes 393220
  66.6 1.6 copy-start.7
  73.5 37.5 %copy-start.1 = (f32[2,1152,128,1]{1,2,3,0:T(8,128)S(1)}, f32[2,1152,128,1]{1,2,3,0:T(8,128)}, u32[]{:S(2)}) copy-start(f32[2,1152,128,1]{1,2,3,0:T(8,128)} %fusion.25) | copy-start | bytes 3538948
  73.5 37.5 %copy-start.2 = (f32[2,1152,128,1]{1,2,3,0:T(8,128)S(1)}, f32[2,1152,128,1]{1,2,3,0:T(8,128)}, u32[]{:S(2)}) copy-start(f32[2,1152,128,1]{1,2,3,0:T(8,128)} %fusion.26) | copy-start | bytes 3538948
  73.5 37.5 %copy-start.3 = (f32[2,1152,128,1]{1,2,3,0:T(8,128)S(1)}, f32[2,1152,128,1]{1,2,3,0:T(8,128)}, u32[]{:S(2)}) copy-start(f32[2,1152,128,1]{1,2,3,0:T(8,128)} %fusion.27) | copy-start | bytes 3538948
  73.9 17.0 %collective-permute-start.10 = (bf16[128,1024]{0,1:T(8,128)(2,1)S(1)}, bf16[128,1024]{0,1:T(8,128)(2,1)S(1)}, u32[]{:S(2)}, u32[]{:S(2)}) collective-permute-start(bf16[128,1024]{0,1:T(8,128)(2,1)S(1)} %get-tuple-element.18), channel_id=1, source_target_pairs={{3,0},{4,1},{5,2},{6,3},{7,4},{8,5},{9,6},{10,7},{11,8},{12,9},{13... | collective-permute-start | bytes 786440 | tf_op jit(solution)/shard_map/ppermute | solution.py:26
  80.1 15.5 %collective-permute-start.11 = (bf16[128,1024]{0,1:T(8,128)(2,1)S(1)}, bf16[128,1024]{0,1:T(8,128)(2,1)S(1)}, u32[]{:S(2)}, u32[]{:S(2)}) collective-permute-start(bf16[128,1024]{0,1:T(8,128)(2,1)S(1)} %get-tuple-element.17), channel_id=1, source_target_pairs={{4,0},{5,1},{6,2},{7,3},{8,4},{9,5},{10,6},{11,7},{12,8},{13,9},{1... | collective-permute-start | bytes 786440 | tf_op jit(solution)/shard_map/ppermute | solution.py:26
  84.2 24.7 %collective-permute-start.12 = (bf16[128,1024]{0,1:T(8,128)(2,1)S(1)}, bf16[128,1024]{0,1:T(8,128)(2,1)S(1)}, u32[]{:S(2)}, u32[]{:S(2)}) collective-permute-start(bf16[128,1024]{0,1:T(8,128)(2,1)S(1)} %get-tuple-element.16), channel_id=1, source_target_pairs={{5,0},{6,1},{7,2},{8,3},{9,4},{10,5},{11,6},{12,7},{13,8},{14,9},{... | collective-permute-start | bytes 786440 | tf_op jit(solution)/shard_map/ppermute | solution.py:26
  86.1 28.5 %collective-permute-start.13 = (bf16[128,1024]{0,1:T(8,128)(2,1)S(1)}, bf16[128,1024]{0,1:T(8,128)(2,1)S(1)}, u32[]{:S(2)}, u32[]{:S(2)}) collective-permute-start(bf16[128,1024]{0,1:T(8,128)(2,1)S(1)} %get-tuple-element.15), channel_id=1, source_target_pairs={{6,0},{7,1},{8,2},{9,3},{10,4},{11,5},{12,6},{13,7},{14,8},{15,9},... | collective-permute-start | bytes 786440 | tf_op jit(solution)/shard_map/ppermute | solution.py:26
  89.0 25.7 %collective-permute-start.14 = (bf16[128,1024]{0,1:T(8,128)(2,1)S(1)}, bf16[128,1024]{0,1:T(8,128)(2,1)S(1)}, u32[]{:S(2)}, u32[]{:S(2)}) collective-permute-start(bf16[128,1024]{0,1:T(8,128)(2,1)S(1)} %get-tuple-element.14), channel_id=1, source_target_pairs={{7,0},{8,1},{9,2},{10,3},{11,4},{12,5},{13,6},{14,7},{15,8},{16,9}... | collective-permute-start | bytes 786440 | tf_op jit(solution)/shard_map/ppermute | solution.py:26
  90.9 23.7 %collective-permute-start.15 = (bf16[128,1024]{0,1:T(8,128)(2,1)S(1)}, bf16[128,1024]{0,1:T(8,128)(2,1)S(1)}, u32[]{:S(2)}, u32[]{:S(2)}) collective-permute-start(bf16[128,1024]{0,1:T(8,128)(2,1)S(1)} %get-tuple-element.13), channel_id=1, source_target_pairs={{8,0},{9,1},{10,2},{11,3},{12,4},{13,5},{14,6},{15,7},{16,8},{17,9... | collective-permute-start | bytes 786440 | tf_op jit(solution)/shard_map/ppermute | solution.py:26
  95.7 19.0 %collective-permute-start.8 = (bf16[128,1024]{0,1:T(8,128)(2,1)S(1)}, bf16[128,1024]{0,1:T(8,128)(2,1)S(1)}, u32[]{:S(2)}, u32[]{:S(2)}) collective-permute-start(bf16[128,1024]{0,1:T(8,128)(2,1)S(1)} %get-tuple-element.12), channel_id=1, source_target_pairs={{1,0},{2,1},{3,2},{4,3},{5,4},{6,5},{7,6},{8,7},{9,8},{10,9},{11,1... | collective-permute-start | bytes 786440 | tf_op jit(solution)/shard_map/ppermute | solution.py:26
  108.9 16.7 %collective-permute-start.9 = (bf16[128,1024]{0,1:T(8,128)(2,1)S(1)}, bf16[128,1024]{0,1:T(8,128)(2,1)S(1)}, u32[]{:S(2)}, u32[]{:S(2)}) collective-permute-start(bf16[128,1024]{0,1:T(8,128)(2,1)S(1)} %get-tuple-element.19), channel_id=1, source_target_pairs={{2,0},{3,1},{4,2},{5,3},{6,4},{7,5},{8,6},{9,7},{10,8},{11,9},{12,... | collective-permute-start | bytes 786440 | tf_op jit(solution)/shard_map/ppermute | solution.py:26
  128.6 58.0 %all-to-all-start = ((bf16[16,128,1024]{2,1,0:T(8,128)(2,1)}), bf16[16,128,1024]{2,1,0:T(8,128)(2,1)}, u32[]{:S(2)}, u32[]{:S(2)}) async-start(bf16[16,128,1024]{2,1,0:T(8,128)(2,1)} %broadcast_in_dim.44), calls=%async_computation | async-start | bytes 8388608 | tf_op jit(solution)/shard_map/all_to_all | solution.py:89
  191.3 5.8 %copy-start.11 = (f32[1024]{0:T(1024)S(1)}, f32[1024]{0:T(1024)}, u32[]{:S(2)}) copy-start(f32[1024]{0:T(1024)} %param.8) | copy-start | bytes 12292
  191.3 29.9 %collective-permute-start.16 = (f32[336,512]{1,0:T(8,128)}, f32[336,512]{1,0:T(8,128)}, u32[]{:S(2)}, u32[]{:S(2)}) collective-permute-start(f32[336,512]{1,0:T(8,128)} %dynamic-slice_bitcast_fusion), channel_id=1, source_target_pairs={{0,16},{16,0},{1,17},{17,1},{2,18},{18,2},{3,19},{19,3},{4,20},{20... | collective-permute-start | bytes 2064392 | tf_op jit(solution)/shard_map/ppermute | solution.py:107
  226.8 52.2 %all-to-all-start.1 = ((f32[338,16,32]{0,2,1:T(8,128)}), f32[338,16,32]{0,2,1:T(8,128)S(1)}, u32[]{:S(2)}, u32[]{:S(2)}) async-start(f32[338,16,32]{0,2,1:T(8,128)} %pad_maximum_fusion.1), calls=%async_computation.1 | async-start | bytes 1572864 | tf_op jit(solution)/shard_map/all_to_all | solution.py:113
